TPU v7x, 128 devices: a whole 4x4x4 slice. The times are simulated.
128 devices in a mesh: ctx: 16 (over y, x), exp: 8 (over z, core).
Axes of the slice: x: 4, y: 4, z: 4, core: 2. Of those that a mesh axis runs over, the one named last changes fastest.
Arguments:
- queries: bfloat16 [8192, 8192], P('ctx', 'exp'), may hold values from -6 to 6
- keys: bfloat16 [8192, 8192], P('ctx', 'exp'), may hold values from -6 to 6
- values: bfloat16 [8192, 8192], P('ctx', 'exp'), may hold values from -6 to 6
- log_decay: float32 [8192, 64], P('ctx', 'exp'), may hold values from -2 to 0, as said below
- residual: bfloat16 [8192, 3072], P(('ctx', 'exp')), may hold values from -6 to 6
- out_proj: bfloat16 [8192, 3072], P('exp'), may hold values from -0.0625 to 0.0625
- expert_ids: int32 [8192, 2], P(('ctx', 'exp')), may hold values from 0 to 15, all different within a row; in each aligned block of 64 rows (0 to 63, 64 to 127, ...) at most 10 rows name the same one
- route_weights: float32 [8192, 2], P(('ctx', 'exp')), may hold values from 0.1 to 0.9
- w_gate: bfloat16 [16, 3072, 6144], P('exp', None, 'ctx'), may hold values from -0.109375 to 0.109375
- w_up: bfloat16 [16, 3072, 6144], P('exp', None, 'ctx'), may hold values from -0.109375 to 0.109375
- w_down: bfloat16 [16, 6144, 3072], P('exp', 'ctx'), may hold values from -0.078125 to 0.078125
Outputs:
- mixed: bfloat16 [8192, 3072], P(('ctx', 'exp'))
Inputs may be any that keep to these rules, and one draw needn't show every extreme that they name: `expert_ids`: each token names two different experts. In each aligned block of 64 tokens no expert is named more than 10 times, and in some blocks one expert is named exactly 10 times. `log_decay`: every entry is negative.
All inputs are finite; a program needn't handle non-finite values.
Results may differ from a plain program's by a relative error of at most 0.019.
Values may be sent and summed in bfloat16 or wider, within the bound.
No kernel may reach another device: no remote copies, remote signals or barrier semaphores. Data moves between devices by JAX's collectives and lax.ppermute only.
A program may use at most 128 MiB of HBM per device.

v0:
```python
import jax
import jax.numpy as jnp
from jax import lax
from jax.sharding import PartitionSpec as P

EPS = 1e-06


def prefix(shard, axis, combine, identity):
    length, here = (lax.axis_size(axis), lax.axis_index(axis))
    everything = jax.tree.map(
        lambda part, kind: lax.all_gather(part.astype(kind), axis),
        shard,
        (jnp.bfloat16, jnp.bfloat16),
    )
    start = jax.tree.map(
        lambda part, zero: jnp.broadcast_to(jnp.asarray(zero, part.dtype), part.shape),
        shard,
        identity,
    )

    def hop(k, before):
        reached = k < here
        new = combine(
            before, jax.tree.map(lambda part, own: part[k].astype(own.dtype), everything, shard)
        )
        return jax.tree.map(lambda a, b: jnp.where(reached, a, b), new, before)

    return lax.fori_loop(0, length, hop, start)


def chain_combine(earlier, later):
    return (earlier[0] + later[0], jnp.exp(later[0])[:, None, None] * earlier[1] + later[1])


def slot_table(chosen_specialist_index, capacity, local_experts, experts):
    flat = chosen_specialist_index.reshape(-1)
    onehot = (flat[:, None] == jnp.arange(experts, dtype=jnp.int32)[None, :]).astype(jnp.int32)
    preceding_sum = jnp.cumsum(onehot, axis=0) - onehot
    position = jnp.sum(preceding_sum * onehot, axis=1)
    slots = (
        flat // local_experts * (capacity * local_experts)
        + position * local_experts
        + flat % local_experts
    )
    return slots.reshape(chosen_specialist_index.shape)


def dispatch_table(slots, total_slots):
    assignment_tally = slots[None, :, :] == jnp.arange(total_slots, dtype=jnp.int32)[:, None, None]
    return jnp.any(assignment_tally, axis=2).astype(jnp.bfloat16)


def on_device(
    queries,
    keys,
    values,
    log_decay,
    residual,
    out_proj,
    expert_ids,
    route_weights,
    w_gate,
    w_up,
    w_down,
):
    tok = queries.shape[0]
    heads_here = log_decay.shape[1]
    head_dim = queries.shape[1] // heads_here
    q_heads = queries.reshape(tok, heads_here, head_dim)
    k_heads = keys.reshape(tok, heads_here, head_dim)
    v_heads = values.reshape(tok, heads_here, head_dim)
    cum = jnp.cumsum(log_decay, axis=0)
    scores = jnp.einsum("thd,shd->hts", q_heads, k_heads, preferred_element_type=jnp.float32)
    place = jnp.arange(tok, dtype=jnp.int32)
    causal = (place[:, None] >= place[None, :])[None]
    diff = cum.T[:, :, None] - cum.T[:, None, :]
    weights = jnp.where(causal, scores * jnp.exp(jnp.where(causal, diff, 0.0)), 0.0).astype(
        jnp.bfloat16
    )
    intra = jnp.einsum("hts,shd->thd", weights, v_heads, preferred_element_type=jnp.float32)
    last = cum[-1]
    scaled_keys = (k_heads.astype(jnp.float32) * jnp.exp(last[None, :] - cum)[:, :, None]).astype(
        jnp.bfloat16
    )
    summary = jnp.einsum("thd,the->hde", scaled_keys, v_heads, preferred_element_type=jnp.float32)
    _, carried = prefix(
        (last, summary), "ctx", chain_combine, (jnp.zeros_like(last), jnp.zeros_like(summary))
    )
    inter = jnp.exp(cum)[:, :, None] * jnp.einsum(
        "thd,hde->the", q_heads.astype(jnp.float32), carried, precision=lax.Precision.HIGHEST
    )
    attn = intra + inter
    normed = (
        (attn * lax.rsqrt(jnp.mean(attn * attn, axis=-1, keepdims=True) + EPS))
        .astype(jnp.bfloat16)
        .reshape(tok, heads_here * head_dim)
    )
    n_exp = lax.axis_size("exp")
    proj = lax.psum_scatter(
        jnp.dot(normed, out_proj, preferred_element_type=jnp.float32).astype(jnp.bfloat16),
        "exp",
        scatter_dimension=0,
        tiled=True,
    ).astype(jnp.float32)
    feature_vector = residual.astype(jnp.float32) + proj
    moe_in = (
        feature_vector
        * lax.rsqrt(jnp.mean(feature_vector * feature_vector, axis=-1, keepdims=True) + EPS)
    ).astype(jnp.bfloat16)
    local_experts = w_gate.shape[0]
    experts = local_experts * n_exp
    mtok = residual.shape[0]
    width = residual.shape[1]
    capacity = max(2, (5 * mtok + 2 * experts - 1) // (2 * experts))
    total_slots = experts * capacity
    local_slot_table = slot_table(expert_ids, capacity, local_experts, experts)
    packed = jnp.dot(
        dispatch_table(local_slot_table, total_slots), moe_in, preferred_element_type=jnp.float32
    ).astype(jnp.bfloat16)
    packed = packed.reshape(n_exp, capacity, local_experts, width)
    arrived = lax.all_to_all(packed, "exp", split_axis=0, concat_axis=1, tiled=True).reshape(
        n_exp * capacity, local_experts, width
    )
    piece = lax.all_gather(arrived, "ctx", axis=0, tiled=True)
    gate = jnp.einsum("red,edf->ref", piece, w_gate, preferred_element_type=jnp.float32)
    upper = jnp.einsum("red,edf->ref", piece, w_up, preferred_element_type=jnp.float32)
    acts = (jax.nn.silu(gate) * upper).astype(jnp.bfloat16)
    summed = lax.psum_scatter(
        jnp.einsum("ref,efd->red", acts, w_down, preferred_element_type=jnp.float32).astype(
            jnp.bfloat16
        ),
        "ctx",
        scatter_dimension=0,
        tiled=True,
    )
    outgoing = summed.reshape(n_exp, capacity, local_experts, width)
    returned = lax.all_to_all(outgoing, "exp", split_axis=0, concat_axis=0, tiled=True).reshape(
        total_slots, width
    )
    picker = (
        local_slot_table.reshape(-1)[:, None] == jnp.arange(total_slots, dtype=jnp.int32)[None, :]
    ).astype(jnp.bfloat16)
    fetched = jnp.dot(picker, returned, preferred_element_type=jnp.float32).reshape(mtok, 2, width)
    moe = route_weights[:, 0:1] * fetched[:, 0] + route_weights[:, 1:2] * fetched[:, 1]
    return (feature_vector + moe).astype(jnp.bfloat16)


def solution(mesh):
    placed = (
        P("ctx", "exp"),
        P("ctx", "exp"),
        P("ctx", "exp"),
        P("ctx", "exp"),
        P(("ctx", "exp"), None),
        P("exp", None),
        P(("ctx", "exp"), None),
        P(("ctx", "exp"), None),
        P("exp", None, "ctx"),
        P("exp", None, "ctx"),
        P("exp", "ctx", None),
    )
    return jax.shard_map(
        on_device, mesh=mesh, in_specs=placed, out_specs=P(("ctx", "exp"), None), check_vma=False
    )
```

profile of v0, /device:TPU:1, one launch (start us, length us, event | category | flops | bytes accessed | tf_op | source)
XLA Modules:
  0.0 437.0 jit_solution(16674942714231050304)
XLA Ops:
  6.5 2.3 reduce-window.6
  9.4 1.5 copy.128
  10.9 2.4 convolution_convert_fusion.3
  13.6 17.2 %all-gather.1 = bf16[16,1,8]{2,1,0:T(2,128)(2,1)S(1)} all-gather(bf16[1,1,8]{2,1,0:T(2,128)(2,1)S(1)} %bitcast.139), channel_id=1, replica_groups=mesh['ctx'=16,'exp'=8] {'ctx'}, dimensions={0}, use_global_device_ids=true | all-gather | bytes 272 | tf_op jit(solution)/shard_map/all_gather | solution.py:12
  30.9 6.2 %fusion.2 = f32[8,512,128]{1,2,0:T(8,128)} fusion(f32[8,512]{1,0:T(8,128)S(1)} %add_bitcast_fusion.1, pred[512,512]{1,0:T(8,128)(4,1)S(1)} %iota_compare_fusion, bf16[512,8,128]{0,2,1:T(8,128)(2,1)S(1)} %bitcast.135, bf16[512,1024]{1,0:T(8,128)(2,1)} %param.15, bf16[512,1024]{1,0:T(8,128)(2,1)S(1)} %copy-done), kind=kOutput, calls=%fused_computation.7 | convolution fusion | flops 1084227584 | bytes 5521408 | tf_op jit(solution)/shard_map/hts,shd->thd/dot_general | solution.py:81
  37.1 30.6 %all-gather.7.cloned.1.call-done = bf16[128,128,128]{2,1,0:T(8,128)(2,1)} async-done(((bf16[8,128,128]{2,1,0:T(8,128)(2,1)}), bf16[128,128,128]{2,1,0:T(8,128)(2,1)}) %all-gather.7.cloned.1.call-update) | async-done | bytes 4194320 | tf_op jit(solution)/shard_map/all_gather | solution.py:12
  67.8 18.1 %while.14 = (s32[]{:T(128)}, f32[8,128,128]{2,1,0:T(8,128)S(1)}, s32[]{:T(128)}, bf16[16,8]{1,0:T(8,128)(2,1)S(1)}, bf16[16,8,128,128]{3,2,1,0:T(8,128)(2,1)}, /*index=5*/s32[]{:T(128)}, s32[]{:T(128)}) while((s32[]{:T(128)}, f32[8,128,128]{2,1,0:T(8,128)S(1)}, s32[]{:T(128)}, bf16[16,8]{1,0:T(8,128)(2,1)S(1)}, ...), condition=%wide.region_3.4_spmd.clone, body=%wide.region_2.3_spmd.clone.sunk | while | flops 655372 | bytes 1310905 | solution.py:29
  67.8 1.1 fusion.64
  68.9 1.1 fusion.64
  85.9 2.9 multiply_reduce_fusion
  89.1 7.7 %convolution_convert_fusion.1 = bf16[512,3072]{1,0:T(8,128)(2,1)} fusion(bf16[512,1024]{0,1:T(8,128)(2,1)S(1)} %bitcast.133, bf16[1024,3072]{1,0:T(8,128)(2,1)} %param.18), kind=kOutput, calls=%fused_computation.6 | convolution fusion | flops 3222798336 | bytes 10485760 | tf_op jit(solution)/shard_map/dot_general | solution.py:101
  97.9 32.0 %reduce-scatter.3.cloned.1.call-done = bf16[64,3072]{1,0:T(8,128)(2,1)} async-done(((bf16[512,3072]{1,0:T(8,128)(2,1)}), bf16[64,3072]{1,0:T(8,128)(2,1)}) %reduce-scatter.3.cloned.1.call-update) | async-done | bytes 393232 | tf_op jit(solution)/shard_map/reduce_scatter | solution.py:100
  129.9 1.2 multiply_reduce_fusion.1
  131.1 1.5 convolution_convert_fusion.2
  133.0 20.6 %all_to_all.14 = bf16[8,10,2,3072]{3,2,1,0:T(2,128)(2,1)S(1)} all-to-all(bf16[8,10,2,3072]{3,2,1,0:T(2,128)(2,1)S(1)} %reshape.217), channel_id=1, replica_groups=mesh['ctx'=16,'exp'=8] {'exp'}, dimensions={0} | all-to-all | bytes 1966080 | tf_op jit(solution)/shard_map/all_to_all | solution.py:122
  153.6 1.2 copy.124
  155.0 104.9 %all-gather.5.cloned.1.call-done = bf16[1280,2,3072]{2,0,1:T(8,128)(2,1)} async-done(((bf16[80,2,3072]{2,0,1:T(8,128)(2,1)}), bf16[1280,2,3072]{2,0,1:T(8,128)(2,1)}) %all-gather.5.cloned.1.call-update) | async-done | bytes 15728656 | tf_op jit(solution)/shard_map/all_gather | solution.py:125
  259.9 14.3 %fusion.38 = f32[2,1280,384]{2,1,0:T(8,128)} fusion(bf16[1280,2,3072]{2,0,1:T(8,128)(2,1)} %all-gather.5.cloned.1.call-done, bf16[2,3072,384]{2,1,0:T(8,128)(2,1)} %param.22), kind=kOutput, calls=%fused_computation.75 | convolution fusion | flops 6039797760 | bytes 24379392 | tf_op jit(solution)/shard_map/red,edf->ref/dot_general | solution.py:127
  274.3 25.0 %fusion.1 = bf16[1280,2,3072]{2,0,1:T(8,128)(2,1)} fusion(bf16[2,384,3072]{2,1,0:T(8,128)(2,1)} %param.23, f32[2,1280,384]{2,1,0:T(8,128)} %fusion.38, bf16[1280,2,3072]{2,0,1:T(8,128)(2,1)} %all-gather.5.cloned.1.call-done, bf16[2,3072,384]{2,1,0:T(8,128)(2,1)} %param.21), kind=kOutput, calls=%fused_computation.4 | convolution fusion | flops 12093358080 | bytes 44826624 | tf_op jit(solution)/shard_map/ref,efd->red/dot_general | solution.py:130
  299.3 105.0 %reduce-scatter.5.cloned.1.call-done = bf16[80,2,3072]{2,0,1:T(8,128)(2,1)} async-done(((bf16[1280,2,3072]{2,0,1:T(8,128)(2,1)}), bf16[80,2,3072]{2,0,1:T(8,128)(2,1)}) %reduce-scatter.5.cloned.1.call-update) | async-done | bytes 983056 | tf_op jit(solution)/shard_map/reduce_scatter | solution.py:129
  404.3 3.2 copy.125
  407.5 5.9 %all-to-all-start.1 = ((bf16[8,10,2,3072]{3,2,1,0:T(2,128)(2,1)}), bf16[8,10,2,3072]{3,2,1,0:T(2,128)(2,1)S(1)}, u32[]{:S(2)}, u32[]{:S(2)}) async-start(bf16[8,10,2,3072]{3,2,1,0:T(2,128)(2,1)} %bitcast.17), calls=%async_computation.3 | async-start | bytes 1966080 | tf_op jit(solution)/shard_map/all_to_all | solution.py:138
  413.5 14.3 %all-to-all-done.1 = bf16[8,10,2,3072]{3,2,1,0:T(2,128)(2,1)S(1)} async-done(((bf16[8,10,2,3072]{3,2,1,0:T(2,128)(2,1)}), bf16[8,10,2,3072]{3,2,1,0:T(2,128)(2,1)S(1)}, u32[]{:S(2)}, u32[]{:S(2)}) %all-to-all-start.1) | async-done | bytes 983072 | tf_op jit(solution)/shard_map/all_to_all | solution.py:138
  428.5 2.0 fusion.25
  (76 shorter events, 19.2 us)
Async XLA Ops:
  6.5 24.3 %copy-start = (bf16[512,1024]{1,0:T(8,128)(2,1)S(1)}, bf16[512,1024]{1,0:T(8,128)(2,1)}, u32[]{:S(2)}) copy-start(bf16[512,1024]{1,0:T(8,128)(2,1)} %param.13) | copy-start | bytes 3145732
  6.5 61.2 %all-gather.7.cloned.1.call-start = ((), (), s32[]{:S(2)}) async-start(), calls=%async_computation.7 | async-start | bytes 4456448 | tf_op jit(solution)/shard_map/all_gather | solution.py:12
  13.3 116.6 %reduce-scatter.3.cloned.1.call-start = ((), (), s32[]{:S(2)}) async-start(), calls=%async_computation.4 | async-start | bytes 3538944 | tf_op jit(solution)/shard_map/reduce_scatter | solution.py:100
  89.1 7.8 %copy-start.3 = (s32[64,2]{0,1:T(2,128)S(1)}, s32[64,2]{0,1:T(2,128)}, u32[]{:S(2)}) copy-start(s32[64,2]{0,1:T(2,128)} %param.19) | copy-start | bytes 1540
  89.1 40.8 %copy-start.2 = (bf16[64,3072]{1,0:T(8,128)(2,1)S(1)}, bf16[64,3072]{1,0:T(8,128)(2,1)}, u32[]{:S(2)}) copy-start(bf16[64,3072]{1,0:T(8,128)(2,1)} %param.17) | copy-start | bytes 1179652
  96.8 163.1 %all-gather.5.cloned.1.call-start = ((), (), s32[]{:S(2)}) async-start(), calls=%async_computation.5 | async-start | bytes 16711680 | tf_op jit(solution)/shard_map/all_gather | solution.py:125
  154.8 249.5 %reduce-scatter.5.cloned.1.call-start = ((), (), s32[]{:S(2)}) async-start(), calls=%async_computation.6 | async-start | bytes 16711680 | tf_op jit(solution)/shard_map/reduce_scatter | solution.py:129
  299.3 114.2 %copy-start.4 = (f32[64,2]{0,1:T(2,128)S(1)}, f32[64,2]{0,1:T(2,128)}, u32[]{:S(2)}) copy-start(f32[64,2]{0,1:T(2,128)} %param.20) | copy-start | bytes 1540
  407.5 23.0 %copy-start.1 = (bf16[512,1024]{1,0:T(8,128)(2,1)S(1)}, bf16[512,1024]{1,0:T(8,128)(2,1)}, u32[]{:S(2)}) copy-start(bf16[512,1024]{1,0:T(8,128)(2,1)} %param.13) | copy-start | bytes 3145732
  407.5 20.2 %all-to-all-start.1 = ((bf16[8,10,2,3072]{3,2,1,0:T(2,128)(2,1)}), bf16[8,10,2,3072]{3,2,1,0:T(2,128)(2,1)S(1)}, u32[]{:S(2)}, u32[]{:S(2)}) async-start(bf16[8,10,2,3072]{3,2,1,0:T(2,128)(2,1)} %bitcast.17), calls=%async_computation.3 | async-start | bytes 1966080 | tf_op jit(solution)/shard_map/all_to_all | solution.py:138
Sparse Core Ops, SparseCore 0:
  13.4 54.2 all-gather.6
  96.9 32.8 reduce-scatter.2
  154.9 105.0 all-gather.4
  299.5 104.8 reduce-scatter.4
where the time goes:
time: 438 us; the launch traced here: 437 us
  waiting for transfers between devices  287 us (66%)
  matrix products  60.5 us (14%)
  blocking collectives  37.8 us (9%)
  other arithmetic  24.4 us (6%)
  between operations  13.3 us (3%)
  local copies, waits for them, and re-layouts  7.61 us (2%)
  starting transfers between devices  6.25 us (1%)
    reduce_scatter x1, waiting for transfers between devices, on_device(): lax.psum_scatter(jnp.einsum('ref,efd->red', acts, w_down, preferred_eleme...  105 us
    all_gather x1, waiting for transfers between devices, on_device(): piece = lax.all_gather(arrived, 'ctx', axis=0, tiled=True)  105 us
    reduce_scatter x1, waiting for transfers between devices, on_device(): lax.psum_scatter(jnp.dot(normed, out_proj, preferred_element_type=jnp.flo...  32 us
    all_gather x1, waiting for transfers between devices, prefix(): lax.all_gather(part.astype(kind), axis)  30.6 us
    dot_general x1, matrix products, on_device(): jnp.einsum('ref,efd->red', acts, w_down, preferred_element_type=jnp.float32)  25 us
    all_to_all x1, blocking collectives, on_device(): lax.all_to_all(packed, 'exp', split_axis=0, concat_axis=1, tiled=True)  20.6 us
    select_n x16, other arithmetic, hop(): return jax.tree.map(lambda a, b: jnp.where(reached, a, b), new, before)  17.5 us
    all_gather x1, blocking collectives, prefix(): lax.all_gather(part.astype(kind), axis)  17.2 us
  transfers between devices with their start and end apart: 5, of which 5 were waited for; matrix products, arithmetic and copies ran while one was open for 2% of the time, Pallas kernels for 0%

commit v1 on v0

v1 whole, which is shorter than its diff:
```python
import jax
import jax.numpy as jnp
from jax import lax
from jax.sharding import PartitionSpec as P

EPS = 1e-06


def exclusive_scan(rate, state, axis):
    length = lax.axis_size(axis)
    first = [(i, i + 1) for i in range(length - 1)]
    r = lax.ppermute(rate, axis, first)
    s = lax.ppermute(state.astype(jnp.bfloat16), axis, first).astype(jnp.float32)
    shift = 1
    while shift < length - 1:
        pairs = [(i, i + shift) for i in range(length - shift)]
        s_in = lax.ppermute(s.astype(jnp.bfloat16), axis, pairs).astype(jnp.float32)
        decay = jnp.exp(r)
        if 2 * shift < length - 1:
            r_in = lax.ppermute(r, axis, pairs)
            r = r + r_in
        s = decay[:, None, None] * s_in + s
        shift *= 2
    return s


def slot_table(chosen, capacity, local_experts, n_exp, experts):
    flat = chosen.reshape(-1)
    onehot = (flat[:, None] == jnp.arange(experts, dtype=jnp.int32)[None, :]).astype(jnp.int32)
    preceding_sum = jnp.cumsum(onehot, axis=0) - onehot
    position = jnp.sum(preceding_sum * onehot, axis=1)
    slots = (
        flat % local_experts * (n_exp * capacity)
        + flat // local_experts * capacity
        + position
    )
    return slots.reshape(chosen.shape)


def dispatch_table(slots, total_slots):
    tally = slots[None, :, :] == jnp.arange(total_slots, dtype=jnp.int32)[:, None, None]
    return jnp.any(tally, axis=2).astype(jnp.bfloat16)


def on_device(
    queries,
    keys,
    values,
    log_decay,
    residual,
    out_proj,
    expert_ids,
    route_weights,
    w_gate,
    w_up,
    w_down,
):
    tok = queries.shape[0]
    heads_here = log_decay.shape[1]
    head_dim = queries.shape[1] // heads_here
    q_heads = queries.reshape(tok, heads_here, head_dim)
    k_heads = keys.reshape(tok, heads_here, head_dim)
    v_heads = values.reshape(tok, heads_here, head_dim)
    cum = jnp.cumsum(log_decay, axis=0)
    last = cum[-1]
    scaled_keys = (k_heads.astype(jnp.float32) * jnp.exp(last[None, :] - cum)[:, :, None]).astype(
        jnp.bfloat16
    )
    summary = jnp.einsum("thd,the->hde", scaled_keys, v_heads, preferred_element_type=jnp.float32)
    carried = exclusive_scan(last, summary, "ctx")
    scores = jnp.einsum("thd,shd->hts", q_heads, k_heads, preferred_element_type=jnp.float32)
    place = jnp.arange(tok, dtype=jnp.int32)
    causal = (place[:, None] >= place[None, :])[None]
    diff = cum.T[:, :, None] - cum.T[:, None, :]
    weights = jnp.where(causal, scores * jnp.exp(jnp.where(causal, diff, 0.0)), 0.0).astype(
        jnp.bfloat16
    )
    intra = jnp.einsum("hts,shd->thd", weights, v_heads, preferred_element_type=jnp.float32)
    inter = jnp.exp(cum)[:, :, None] * jnp.einsum(
        "thd,hde->the", q_heads.astype(jnp.float32), carried, precision=lax.Precision.HIGHEST
    )
    attn = intra + inter
    normed = (
        (attn * lax.rsqrt(jnp.mean(attn * attn, axis=-1, keepdims=True) + EPS))
        .astype(jnp.bfloat16)
        .reshape(tok, heads_here * head_dim)
    )
    n_exp = lax.axis_size("exp")
    proj = lax.psum_scatter(
        jnp.dot(normed, out_proj, preferred_element_type=jnp.float32).astype(jnp.bfloat16),
        "exp",
        scatter_dimension=0,
        tiled=True,
    ).astype(jnp.float32)
    feature_vector = residual.astype(jnp.float32) + proj
    moe_in = (
        feature_vector
        * lax.rsqrt(jnp.mean(feature_vector * feature_vector, axis=-1, keepdims=True) + EPS)
    ).astype(jnp.bfloat16)
    local_experts = w_gate.shape[0]
    experts = local_experts * n_exp
    mtok = residual.shape[0]
    width = residual.shape[1]
    capacity = max(2, (5 * mtok + 2 * experts - 1) // (2 * experts))
    total_slots = experts * capacity
    table = slot_table(expert_ids, capacity, local_experts, n_exp, experts)
    packed = jnp.dot(
        dispatch_table(table, total_slots), moe_in, preferred_element_type=jnp.float32
    ).astype(jnp.bfloat16)
    packed = packed.reshape(local_experts, n_exp, capacity, width)
    returned = []
    for e in range(local_experts):
        arrived = lax.all_to_all(packed[e], "exp", split_axis=0, concat_axis=0, tiled=True)
        piece = lax.all_gather(arrived.reshape(n_exp * capacity, width), "ctx", axis=0, tiled=True)
        gate = jnp.dot(piece, w_gate[e], preferred_element_type=jnp.float32)
        upper = jnp.dot(piece, w_up[e], preferred_element_type=jnp.float32)
        acts = (jax.nn.silu(gate) * upper).astype(jnp.bfloat16)
        down = jnp.dot(acts, w_down[e], preferred_element_type=jnp.float32).astype(jnp.bfloat16)
        summed = lax.psum_scatter(down, "ctx", scatter_dimension=0, tiled=True)
        back = lax.all_to_all(
            summed.reshape(n_exp, capacity, width), "exp", split_axis=0, concat_axis=0, tiled=True
        )
        returned.append(back.reshape(n_exp * capacity, width))
    returned = jnp.concatenate(returned, axis=0)
    picker = (
        table.reshape(-1)[:, None] == jnp.arange(total_slots, dtype=jnp.int32)[None, :]
    ).astype(jnp.bfloat16)
    fetched = jnp.dot(picker, returned, preferred_element_type=jnp.float32).reshape(mtok, 2, width)
    moe = route_weights[:, 0:1] * fetched[:, 0] + route_weights[:, 1:2] * fetched[:, 1]
    return (feature_vector + moe).astype(jnp.bfloat16)


def solution(mesh):
    placed = (
        P("ctx", "exp"),
        P("ctx", "exp"),
        P("ctx", "exp"),
        P("ctx", "exp"),
        P(("ctx", "exp"), None),
        P("exp", None),
        P(("ctx", "exp"), None),
        P(("ctx", "exp"), None),
        P("exp", None, "ctx"),
        P("exp", None, "ctx"),
        P("exp", "ctx", None),
    )
    return jax.shard_map(
        on_device, mesh=mesh, in_specs=placed, out_specs=P(("ctx", "exp"), None), check_vma=False
    )
```

time: 438 us -> 495 us (1.13)
  starting transfers between devices: 6.25 us -> 56.4 us
  waiting for transfers between devices: 287 us -> 307 us
  other arithmetic: 24.4 us -> 8.1 us
  local copies, waits for them, and re-layouts: 7.61 us -> 13.4 us
    ppermute x0 -> x9, starting transfers between devices: none -> 43.1 us  [the longest x4 29.1 us: exclusive_scan(): s_in = lax.ppermute(s.astype(jnp.bfloat16), axis, pairs).astype(jnp.float32)]
    reduce_scatter x1 -> x2, waiting for transfers between devices: 105 us -> 145 us  [on_device(): summed = lax.psum_scatter(down, 'ctx', scatter_dimension=0, tiled=True)]
    all_gather x2, waiting for transfers between devices: 136 us -> 101 us  [on_device(): lax.all_gather(arrived.reshape(n_exp * capacity, width), 'ctx', axis=0, t...]
    select_n x16 -> x0, other arithmetic: 17.5 us -> none  [hop(): return jax.tree.map(lambda a, b: jnp.where(reached, a, b), new, before)]
    all_gather x1 -> x0, blocking collectives: 17.2 us -> none  [prefix(): lax.all_gather(part.astype(kind), axis)]
    all_to_all x1 -> x2, blocking collectives: 20.6 us -> 34 us  [on_device(): lax.all_to_all(packed[e], 'exp', split_axis=0, concat_axis=0, tiled=True)]
    ppermute x0 -> x9, waiting for transfers between devices: none -> 11.5 us  [the longest x1 4.96 us: exclusive_scan(): lax.ppermute(state.astype(jnp.bfloat16), axis, first).astype(jnp.float32)]
    reshape x3 -> x8, local copies, waits for them, and re-layouts: 1.91 us -> 9 us  [the longest x2 4.24 us: on_device(): summed.reshape(n_exp, capacity, width)]
  transfers between devices with their start and end apart: 5 -> 16, of which waited for: 5 -> 13; matrix products, arithmetic and copies ran while one was open for 2% -> 11% of each run, Pallas kernels for 0% -> 0%
where the time goes in v1:
time: 495 us; the launch traced here: 494 us
  waiting for transfers between devices  307 us (62%)
  matrix products  61.9 us (13%)
  starting transfers between devices  56.4 us (11%)
  blocking collectives  34 us (7%)
  between operations  13.5 us (3%)
  local copies, waits for them, and re-layouts  13.4 us (3%)
  other arithmetic  8.1 us (2%)
    reduce_scatter x2, waiting for transfers between devices, on_device(): summed = lax.psum_scatter(down, 'ctx', scatter_dimension=0, tiled=True)  145 us
    all_gather x2, waiting for transfers between devices, on_device(): lax.all_gather(arrived.reshape(n_exp * capacity, width), 'ctx', axis=0, t...  101 us
    reduce_scatter x1, waiting for transfers between devices, on_device(): lax.psum_scatter(jnp.dot(normed, out_proj, preferred_element_type=jnp.flo...  36.9 us
    all_to_all x2, blocking collectives, on_device(): lax.all_to_all(packed[e], 'exp', split_axis=0, concat_axis=0, tiled=True)  34 us
    ppermute x4, starting transfers between devices, exclusive_scan(): s_in = lax.ppermute(s.astype(jnp.bfloat16), axis, pairs).astype(jnp.float32)  29.1 us
    dot_general x2, matrix products, on_device(): gate = jnp.dot(piece, w_gate[e], preferred_element_type=jnp.float32)  14.8 us
    all_to_all x2, starting transfers between devices, on_device(): lax.all_to_all(summed.reshape(n_exp, capacity, width), 'exp', split_axis=...  12.9 us
    dot_general x2, matrix products, on_device(): jnp.dot(acts, w_down[e], preferred_element_type=jnp.float32)  12.9 us
  transfers between devices with their start and end apart: 16, of which 13 were waited for; matrix products, arithmetic and copies ran while one was open for 11% of the time, Pallas kernels for 0%

profile of v1, /device:TPU:1, one launch (start us, length us, event | category | flops | bytes accessed | tf_op | source)
XLA Modules:
  0.0 493.9 jit_solution(13422686085543914302)
XLA Ops:
  16.5 5.0 %collective-permute-done.4 = bf16[8,128,128]{2,1,0:T(8,128)(2,1)S(1)} collective-permute-done((bf16[8,128,128]{2,1,0:T(8,128)(2,1)S(1)}, bf16[8,128,128]{2,1,0:T(8,128)(2,1)S(1)}, u32[]{:S(2)}, u32[]{:S(2)}) %collective-permute-start.4) | collective-permute-done | bytes 262176 | tf_op jit(solution)/shard_map/ppermute | solution.py:13
  21.5 4.1 collective-permute-start.5
  29.8 4.1 collective-permute-start.1
  34.7 6.0 %collective-permute-start.6 = (bf16[8,128,128]{2,1,0:T(8,128)(2,1)S(1)}, bf16[8,128,128]{2,1,0:T(8,128)(2,1)S(1)}, u32[]{:S(2)}, u32[]{:S(2)}) collective-permute-start(bf16[8,128,128]{2,1,0:T(8,128)(2,1)S(1)} %fusion.44), channel_id=1, source_target_pairs={{0,16},{8,24},{16,32},{24,40},{32,48},{40,56},{48,64},{56,72},{64,... | collective-permute-start | bytes 786440 | tf_op jit(solution)/shard_map/ppermute | solution.py:17
  44.2 10.3 %collective-permute-start.7 = (bf16[8,128,128]{2,1,0:T(8,128)(2,1)S(1)}, bf16[8,128,128]{2,1,0:T(8,128)(2,1)S(1)}, u32[]{:S(2)}, u32[]{:S(2)}) collective-permute-start(bf16[8,128,128]{2,1,0:T(8,128)(2,1)S(1)} %fusion.60), channel_id=1, source_target_pairs={{0,32},{8,40},{16,48},{24,56},{32,64},{40,72},{48,80},{56,88},{64,... | collective-permute-start | bytes 786440 | tf_op jit(solution)/shard_map/ppermute | solution.py:17
  58.8 8.8 %collective-permute-start.8 = (bf16[8,128,128]{2,1,0:T(8,128)(2,1)}, bf16[8,128,128]{2,1,0:T(8,128)(2,1)S(1)}, u32[]{:S(2)}, u32[]{:S(2)}) collective-permute-start(bf16[8,128,128]{2,1,0:T(8,128)(2,1)} %fusion.46), channel_id=1, source_target_pairs={{0,64},{8,72},{16,80},{24,88},{32,96},{40,104},{48,112},{56,120},{... | collective-permute-start | bytes 786440 | tf_op jit(solution)/shard_map/ppermute | solution.py:17
  67.6 6.3 %fusion = f32[8,512,128]{1,2,0:T(8,128)} fusion(f32[8,512]{1,0:T(8,128)S(1)} %add_bitcast_fusion.1, pred[512,512]{1,0:T(8,128)(4,1)} %iota_compare_fusion, bf16[512,8,128]{0,2,1:T(8,128)(2,1)S(1)} %bitcast.95, bf16[512,1024]{1,0:T(8,128)(2,1)} %param.13, bf16[512,1024]{1,0:T(8,128)(2,1)S(1)} %copy-done), kind=kOutput, calls=%fused_computation.4 | convolution fusion | flops 1084227584 | bytes 5521408 | tf_op jit(solution)/shard_map/hts,shd->thd/dot_general | solution.py:78
  79.3 7.6 %convolution_convert_fusion.2 = bf16[512,3072]{1,0:T(8,128)(2,1)} fusion(bf16[512,1024]{0,1:T(8,128)(2,1)S(1)} %bitcast.93, bf16[1024,3072]{1,0:T(8,128)(2,1)} %param.16), kind=kOutput, calls=%fused_computation.3 | convolution fusion | flops 3222798336 | bytes 10485760 | tf_op jit(solution)/shard_map/dot_general | solution.py:90
  88.6 36.9 %reduce-scatter.4.cloned.1.call-done = bf16[64,3072]{1,0:T(8,128)(2,1)} async-done(((bf16[512,3072]{1,0:T(8,128)(2,1)}), bf16[64,3072]{1,0:T(8,128)(2,1)}) %reduce-scatter.4.cloned.1.call-update) | async-done | bytes 393232 | tf_op jit(solution)/shard_map/reduce_scatter | solution.py:89
  128.4 18.4 %all_to_all.20 = bf16[8,10,3072]{2,1,0:T(8,128)(2,1)S(1)} all-to-all(bf16[8,10,3072]{2,1,0:T(8,128)(2,1)S(1)} %squeeze.34), channel_id=1, replica_groups=mesh['ctx'=16,'exp'=8] {'exp'}, dimensions={0} | all-to-all | bytes 983040 | tf_op jit(solution)/shard_map/all_to_all | solution.py:113
  148.1 15.6 %all_to_all.21 = bf16[8,10,3072]{2,1,0:T(8,128)(2,1)S(1)} all-to-all(bf16[8,10,3072]{2,1,0:T(8,128)(2,1)S(1)} %squeeze.38), channel_id=1, replica_groups=mesh['ctx'=16,'exp'=8] {'exp'}, dimensions={0} | all-to-all | bytes 983040 | tf_op jit(solution)/shard_map/all_to_all | solution.py:113
  164.9 50.9 %all-gather.3.cloned.1.call-done = bf16[1280,3072]{1,0:T(8,128)(2,1)} async-done(((bf16[80,3072]{1,0:T(8,128)(2,1)}), bf16[1280,3072]{1,0:T(8,128)(2,1)}) %all-gather.3.cloned.1.call-update) | async-done | bytes 7864336 | tf_op jit(solution)/shard_map/all_gather | solution.py:114
  215.8 7.4 %fusion.12 = f32[1280,384]{1,0:T(8,128)S(1)} fusion(bf16[1280,3072]{1,0:T(8,128)(2,1)} %all-gather.3.cloned.1.call-done, bf16[2,3072,384]{2,1,0:T(8,128)(2,1)} %param.19), kind=kOutput, calls=%fused_computation.18 | convolution fusion | flops 3019898880 | bytes 12189696 | tf_op jit(solution)/shard_map/dot_general | solution.py:115
  223.3 6.2 %fusion.4 = bf16[1280,384]{1,0:T(8,128)(2,1)S(1)} fusion(bf16[1280,3072]{1,0:T(8,128)(2,1)S(1)} %copy-done.7, bf16[2,3072,384]{2,1,0:T(8,128)(2,1)} %param.20, f32[1280,384]{1,0:T(8,128)S(1)} %fusion.12), kind=kOutput, calls=%fused_computation.10 | convolution fusion | flops 3022848000 | bytes 13172736 | tf_op jit(solution)/shard_map/dot_general | solution.py:116
  229.5 6.4 %convolution_convert_fusion.1 = bf16[1280,3072]{1,0:T(8,128)(2,1)} fusion(bf16[1280,384]{1,0:T(8,128)(2,1)S(1)} %fusion.4, bf16[2,384,3072]{2,1,0:T(8,128)(2,1)S(1)} %bitcast.98), kind=kOutput, calls=%fused_computation.1 | convolution fusion | flops 3023831040 | bytes 11206656 | tf_op jit(solution)/shard_map/dot_general | solution.py:118
  236.0 50.0 %all-gather.5.cloned.1.call-done = bf16[1280,3072]{1,0:T(8,128)(2,1)} async-done(((bf16[80,3072]{1,0:T(8,128)(2,1)}), bf16[1280,3072]{1,0:T(8,128)(2,1)}) %all-gather.5.cloned.1.call-update) | async-done | bytes 7864336 | tf_op jit(solution)/shard_map/all_gather | solution.py:114
  286.0 7.4 %fusion.8 = f32[1280,384]{1,0:T(8,128)S(1)} fusion(bf16[1280,3072]{1,0:T(8,128)(2,1)} %all-gather.5.cloned.1.call-done, bf16[2,3072,384]{2,1,0:T(8,128)(2,1)} %param.19), kind=kOutput, calls=%fused_computation.14 | convolution fusion | flops 3019898880 | bytes 12189696 | tf_op jit(solution)/shard_map/dot_general | solution.py:115
  293.5 6.2 %fusion.5 = bf16[1280,384]{1,0:T(8,128)(2,1)S(1)} fusion(bf16[1280,3072]{1,0:T(8,128)(2,1)S(1)} %copy-done.6, bf16[2,3072,384]{2,1,0:T(8,128)(2,1)} %param.20, f32[1280,384]{1,0:T(8,128)S(1)} %fusion.8), kind=kOutput, calls=%fused_computation.11 | convolution fusion | flops 3022848000 | bytes 13172736 | tf_op jit(solution)/shard_map/dot_general | solution.py:116
  299.7 6.5 %convolution_convert_fusion = bf16[1280,3072]{1,0:T(8,128)(2,1)} fusion(bf16[1280,384]{1,0:T(8,128)(2,1)S(1)} %fusion.5, bf16[2,384,3072]{2,1,0:T(8,128)(2,1)S(1)} %bitcast.100), kind=kOutput, calls=%fused_computation | convolution fusion | flops 3023831040 | bytes 11206656 | tf_op jit(solution)/shard_map/dot_general | solution.py:118
  306.2 66.4 %reduce-scatter.6.cloned.1.call-done = bf16[80,3072]{1,0:T(8,128)(2,1)} async-done(((bf16[1280,3072]{1,0:T(8,128)(2,1)}), bf16[80,3072]{1,0:T(8,128)(2,1)}) %reduce-scatter.6.cloned.1.call-update) | async-done | bytes 491536 | tf_op jit(solution)/shard_map/reduce_scatter | solution.py:119
  374.7 6.5 %all-to-all-start.1 = ((bf16[8,10,3072]{2,1,0:T(8,128)(2,1)}), bf16[8,10,3072]{2,1,0:T(8,128)(2,1)S(1)}, u32[]{:S(2)}, u32[]{:S(2)}) async-start(bf16[8,10,3072]{2,1,0:T(8,128)(2,1)} %reshape.203), calls=%async_computation.3 | async-start | bytes 1572864 | tf_op jit(solution)/shard_map/all_to_all | solution.py:120
  381.3 78.9 %reduce-scatter.8.cloned.1.call-done = bf16[80,3072]{1,0:T(8,128)(2,1)} async-done(((bf16[1280,3072]{1,0:T(8,128)(2,1)}), bf16[80,3072]{1,0:T(8,128)(2,1)}) %reduce-scatter.8.cloned.1.call-update) | async-done | bytes 491536 | tf_op jit(solution)/shard_map/reduce_scatter | solution.py:119
  462.3 6.4 %all-to-all-start.3 = ((bf16[8,10,3072]{2,1,0:T(8,128)(2,1)}), bf16[8,10,3072]{2,1,0:T(8,128)(2,1)S(1)}, u32[]{:S(2)}, u32[]{:S(2)}) async-start(bf16[8,10,3072]{2,1,0:T(8,128)(2,1)} %reshape.206), calls=%async_computation.6 | async-start | bytes 1572864 | tf_op jit(solution)/shard_map/all_to_all | solution.py:120
  468.9 11.9 %all-to-all-done.3 = bf16[8,10,3072]{2,1,0:T(8,128)(2,1)S(1)} async-done(((bf16[8,10,3072]{2,1,0:T(8,128)(2,1)}), bf16[8,10,3072]{2,1,0:T(8,128)(2,1)S(1)}, u32[]{:S(2)}, u32[]{:S(2)}) %all-to-all-start.3) | async-done | bytes 491552 | tf_op jit(solution)/shard_map/all_to_all | solution.py:120
  (96 shorter events, 46.3 us)
Async XLA Ops:
  6.5 61.0 %copy-start = (bf16[512,1024]{1,0:T(8,128)(2,1)S(1)}, bf16[512,1024]{1,0:T(8,128)(2,1)}, u32[]{:S(2)}) copy-start(bf16[512,1024]{1,0:T(8,128)(2,1)} %param.11) | copy-start | bytes 3145732
  6.5 118.9 %reduce-scatter.4.cloned.1.call-start = ((), (), s32[]{:S(2)}) async-start(), calls=%async_computation.7 | async-start | bytes 3538944 | tf_op jit(solution)/shard_map/reduce_scatter | solution.py:89
  12.6 8.9 %collective-permute-start.4 = (bf16[8,128,128]{2,1,0:T(8,128)(2,1)S(1)}, bf16[8,128,128]{2,1,0:T(8,128)(2,1)S(1)}, u32[]{:S(2)}, u32[]{:S(2)}) collective-permute-start(bf16[8,128,128]{2,1,0:T(8,128)(2,1)S(1)} %convolution_convert_fusion.4), channel_id=1, source_target_pairs={{0,8},{8,16},{16,24},{24,32},{32,40},{40,48},{48,56},{56,64},{64,7... | collective-permute-start | bytes 786440 | tf_op jit(solution)/shard_map/ppermute | solution.py:13
  21.5 13.0 %collective-permute-start.5 = (bf16[8,128,128]{2,1,0:T(8,128)(2,1)S(1)}, bf16[8,128,128]{2,1,0:T(8,128)(2,1)S(1)}, u32[]{:S(2)}, u32[]{:S(2)}) collective-permute-start(bf16[8,128,128]{2,1,0:T(8,128)(2,1)S(1)} %collective-permute-done.4), channel_id=1, source_target_pairs={{0,8},{8,16},{16,24},{24,32},{32,40},{40,48},{48,56},{56,64},{64,7... | collective-permute-start | bytes 786440 | tf_op jit(solution)/shard_map/ppermute | solution.py:17
  25.6 4.1 collective-permute-start
  29.8 4.8 collective-permute-start.1
  34.7 9.3 %collective-permute-start.6 = (bf16[8,128,128]{2,1,0:T(8,128)(2,1)S(1)}, bf16[8,128,128]{2,1,0:T(8,128)(2,1)S(1)}, u32[]{:S(2)}, u32[]{:S(2)}) collective-permute-start(bf16[8,128,128]{2,1,0:T(8,128)(2,1)S(1)} %fusion.44), channel_id=1, source_target_pairs={{0,16},{8,24},{16,32},{24,40},{32,48},{40,56},{48,64},{56,72},{64,... | collective-permute-start | bytes 786440 | tf_op jit(solution)/shard_map/ppermute | solution.py:17
  44.2 13.6 %collective-permute-start.7 = (bf16[8,128,128]{2,1,0:T(8,128)(2,1)S(1)}, bf16[8,128,128]{2,1,0:T(8,128)(2,1)S(1)}, u32[]{:S(2)}, u32[]{:S(2)}) collective-permute-start(bf16[8,128,128]{2,1,0:T(8,128)(2,1)S(1)} %fusion.60), channel_id=1, source_target_pairs={{0,32},{8,40},{16,48},{24,56},{32,64},{40,72},{48,80},{56,88},{64,... | collective-permute-start | bytes 786440 | tf_op jit(solution)/shard_map/ppermute | solution.py:17
  55.3 2.3 collective-permute-start.2
  58.8 17.1 %collective-permute-start.8 = (bf16[8,128,128]{2,1,0:T(8,128)(2,1)}, bf16[8,128,128]{2,1,0:T(8,128)(2,1)S(1)}, u32[]{:S(2)}, u32[]{:S(2)}) collective-permute-start(bf16[8,128,128]{2,1,0:T(8,128)(2,1)} %fusion.46), channel_id=1, source_target_pairs={{0,64},{8,72},{16,80},{24,88},{32,96},{40,104},{48,112},{56,120},{... | collective-permute-start | bytes 786440 | tf_op jit(solution)/shard_map/ppermute | solution.py:17
  73.8 2.0 collective-permute-start.3
  86.9 38.6 %copy-start.2 = (bf16[64,3072]{1,0:T(8,128)(2,1)S(1)}, bf16[64,3072]{1,0:T(8,128)(2,1)}, u32[]{:S(2)}) copy-start(bf16[64,3072]{1,0:T(8,128)(2,1)} %param.15) | copy-start | bytes 1179652
  86.9 128.9 %all-gather.3.cloned.1.call-start = ((), (), s32[]{:S(2)}) async-start(), calls=%async_computation.8 | async-start | bytes 8355840 | tf_op jit(solution)/shard_map/all_gather | solution.py:114
  147.8 138.2 %all-gather.5.cloned.1.call-start = ((), (), s32[]{:S(2)}) async-start(), calls=%async_computation.10 | async-start | bytes 8355840 | tf_op jit(solution)/shard_map/all_gather | solution.py:114
  164.7 207.9 %reduce-scatter.6.cloned.1.call-start = ((), (), s32[]{:S(2)}) async-start(), calls=%async_computation.9 | async-start | bytes 8355840 | tf_op jit(solution)/shard_map/reduce_scatter | solution.py:119
  215.8 7.5 %copy-start.7 = (bf16[1280,3072]{1,0:T(8,128)(2,1)S(1)}, bf16[1280,3072]{1,0:T(8,128)(2,1)}, u32[]{:S(2)}) copy-start(bf16[1280,3072]{1,0:T(8,128)(2,1)} %all-gather.3.cloned.1.call-done) | copy-start | bytes 23592964
  215.8 13.7 %slice-start = ((s8[4718592]{0:T(1024)(128)(4,1)}), s8[4194304]{0:T(1024)(128)(4,1)S(1)}, s32[]{:S(2)}) async-start(s8[4718592]{0:T(1024)(128)(4,1)} %bitcast.97), calls=%async_computation.12 | async-start | bytes 8388608
  223.2 6.2 %slice-start.1 = ((s8[4718592]{0:T(1024)(128)(4,1)}), s8[524288]{0:T(1024)(128)(4,1)S(1)}, s32[]{:S(2)}) async-start(s8[4718592]{0:T(1024)(128)(4,1)} %bitcast.97), calls=%async_computation.13 | async-start | bytes 1048576
  235.9 224.3 %reduce-scatter.8.cloned.1.call-start = ((), (), s32[]{:S(2)}) async-start(), calls=%async_computation.11 | async-start | bytes 8355840 | tf_op jit(solution)/shard_map/reduce_scatter | solution.py:119
  286.0 7.4 %copy-start.6 = (bf16[1280,3072]{1,0:T(8,128)(2,1)S(1)}, bf16[1280,3072]{1,0:T(8,128)(2,1)}, u32[]{:S(2)}) copy-start(bf16[1280,3072]{1,0:T(8,128)(2,1)} %all-gather.5.cloned.1.call-done) | copy-start | bytes 23592964
  286.0 13.7 %slice-start.2 = ((s8[4718592]{0:T(1024)(128)(4,1)}), s8[4194304]{0:T(1024)(128)(4,1)S(1)}, s32[]{:S(2)}) async-start(s8[4718592]{0:T(1024)(128)(4,1)} %bitcast.99), calls=%async_computation.14 | async-start | bytes 8388608
  374.7 94.0 %copy-start.5 = (f32[64,2]{0,1:T(2,128)S(1)}, f32[64,2]{0,1:T(2,128)}, u32[]{:S(2)}) copy-start(f32[64,2]{0,1:T(2,128)} %param.18) | copy-start | bytes 1540
  374.7 87.6 %all-to-all-start.1 = ((bf16[8,10,3072]{2,1,0:T(8,128)(2,1)}), bf16[8,10,3072]{2,1,0:T(8,128)(2,1)S(1)}, u32[]{:S(2)}, u32[]{:S(2)}) async-start(bf16[8,10,3072]{2,1,0:T(8,128)(2,1)} %reshape.203), calls=%async_computation.3 | async-start | bytes 1572864 | tf_op jit(solution)/shard_map/all_to_all | solution.py:120
  462.3 18.5 %all-to-all-start.3 = ((bf16[8,10,3072]{2,1,0:T(8,128)(2,1)}), bf16[8,10,3072]{2,1,0:T(8,128)(2,1)S(1)}, u32[]{:S(2)}, u32[]{:S(2)}) async-start(bf16[8,10,3072]{2,1,0:T(8,128)(2,1)} %reshape.206), calls=%async_computation.6 | async-start | bytes 1572864 | tf_op jit(solution)/shard_map/all_to_all | solution.py:120
  (4 other events, 13.0 us)
Sparse Core Ops, SparseCore 0:
  87.0 38.3 reduce-scatter.3
  148.0 67.7 all-gather.2
  217.9 68.0 all-gather.4
  289.4 83.1 reduce-scatter.5
  375.9 84.2 reduce-scatter.7

commit v2 on v0

--- a/solution.py
+++ b/solution.py
@@ -6,31 +6,29 @@
 EPS = 1e-06
 
 
-def prefix(shard, axis, combine, identity):
+def carried_state(last, summary, axis):
     length, here = (lax.axis_size(axis), lax.axis_index(axis))
-    everything = jax.tree.map(
-        lambda part, kind: lax.all_gather(part.astype(kind), axis),
-        shard,
-        (jnp.bfloat16, jnp.bfloat16),
+    heads, hd, _ = summary.shape
+    hi = last.astype(jnp.bfloat16)
+    lo = (last - hi.astype(jnp.float32)).astype(jnp.bfloat16)
+    lane = jnp.arange(hd, dtype=jnp.int32)[None, :]
+    rate_row = jnp.where(lane == 0, hi[:, None], jnp.where(lane == 1, lo[:, None], 0.0)).astype(
+        jnp.bfloat16
     )
-    start = jax.tree.map(
-        lambda part, zero: jnp.broadcast_to(jnp.asarray(zero, part.dtype), part.shape),
-        shard,
-        identity,
+    payload = jnp.concatenate(
+        [summary.astype(jnp.bfloat16).reshape(heads, hd * hd), rate_row], axis=1
     )
-
-    def hop(k, before):
-        reached = k < here
-        new = combine(
-            before, jax.tree.map(lambda part, own: part[k].astype(own.dtype), everything, shard)
-        )
-        return jax.tree.map(lambda a, b: jnp.where(reached, a, b), new, before)
-
-    return lax.fori_loop(0, length, hop, start)
-
-
-def chain_combine(earlier, later):
-    return (earlier[0] + later[0], jnp.exp(later[0])[:, None, None] * earlier[1] + later[1])
+    everything = lax.all_gather(payload, axis)
+    states = everything[:, :, : hd * hd].astype(jnp.float32)
+    rates = everything[:, :, hd * hd].astype(jnp.float32) + everything[:, :, hd * hd + 1].astype(
+        jnp.float32
+    )
+    block = jnp.arange(length, dtype=jnp.int32)
+    between = ((block[:, None] < block[None, :]) & (block[None, :] < here)).astype(jnp.float32)
+    exponent = jnp.sum(between[:, :, None] * rates[None, :, :], axis=1)
+    weight = jnp.where((block < here)[:, None], jnp.exp(exponent), 0.0)
+    carried = jnp.sum(weight[:, :, None] * states, axis=0)
+    return carried.reshape(heads, hd, hd)
 
 
 def slot_table(chosen_specialist_index, capacity, local_experts, experts):
@@ -84,9 +82,7 @@
         jnp.bfloat16
     )
     summary = jnp.einsum("thd,the->hde", scaled_keys, v_heads, preferred_element_type=jnp.float32)
-    _, carried = prefix(
-        (last, summary), "ctx", chain_combine, (jnp.zeros_like(last), jnp.zeros_like(summary))
-    )
+    carried = carried_state(last, summary, "ctx")
     inter = jnp.exp(cum)[:, :, None] * jnp.einsum(
         "thd,hde->the", q_heads.astype(jnp.float32), carried, precision=lax.Precision.HIGHEST
     )

time: 438 us -> 421 us (0.961)
  waiting for transfers between devices: 287 us -> 306 us
  blocking collectives: 37.8 us -> 20.6 us
  other arithmetic: 24.4 us -> 11 us
  matrix products: 60.5 us -> 54.8 us
    all_gather x1, waiting for transfers between devices: 30.6 us -> 49.2 us  [carried_state(): everything = lax.all_gather(payload, axis)]
    select_n x16 -> x2, other arithmetic: 17.5 us -> 0.15 us  [the longest x1 0.08 us: carried_state(): jnp.where(lane == 0, hi[:, None], jnp.where(lane == 1, lo[:, None], 0.0))]
    all_gather x1 -> x0, blocking collectives: 17.2 us -> none  [prefix(): lax.all_gather(part.astype(kind), axis)]
where the time goes in v2:
time: 421 us; the launch traced here: 420 us
  waiting for transfers between devices  306 us (73%)
  matrix products  54.8 us (13%)
  blocking collectives  20.6 us (5%)
  between operations  13.4 us (3%)
  other arithmetic  11 us (3%)
  local copies, waits for them, and re-layouts  8.8 us (2%)
  starting transfers between devices  6.23 us (1%)
    reduce_scatter x1, waiting for transfers between devices, on_device(): lax.psum_scatter(jnp.einsum('ref,efd->red', acts, w_down, preferred_eleme...  105 us
    all_gather x1, waiting for transfers between devices, on_device(): piece = lax.all_gather(arrived, 'ctx', axis=0, tiled=True)  105 us
    all_gather x1, waiting for transfers between devices, carried_state(): everything = lax.all_gather(payload, axis)  49.2 us
    reduce_scatter x1, waiting for transfers between devices, on_device(): lax.psum_scatter(jnp.dot(normed, out_proj, preferred_element_type=jnp.flo...  32 us
    dot_general x1, matrix products, on_device(): jnp.einsum('ref,efd->red', acts, w_down, preferred_element_type=jnp.float32)  25 us
    all_to_all x1, blocking collectives, on_device(): lax.all_to_all(packed, 'exp', split_axis=0, concat_axis=1, tiled=True)  20.6 us
    dot_general x1, matrix products, on_device(): jnp.einsum('red,edf->ref', piece, w_up, preferred_element_type=jnp.float32)  14.3 us
    all_to_all x1, waiting for transfers between devices, on_device(): lax.all_to_all(outgoing, 'exp', split_axis=0, concat_axis=0, tiled=True)  14.3 us
  transfers between devices with their start and end apart: 5, of which 5 were waited for; matrix products, arithmetic and copies ran while one was open for 2% of the time, Pallas kernels for 0%

profile of v2, /device:TPU:1, one launch (start us, length us, event | category | flops | bytes accessed | tf_op | source)
XLA Modules:
  0.0 420.3 jit_solution(829509402692624545)
XLA Ops:
  6.5 2.3 reduce-window.6
  9.4 1.5 copy.106
  10.9 2.1 fusion.10
  13.2 0.7 pad_maximum_fusion
  14.2 5.2 %fusion.1 = f32[8,512,128]{1,2,0:T(8,128)S(1)} fusion(f32[8,512]{1,0:T(8,128)S(1)} %add_bitcast_fusion.1, pred[512,512]{1,0:T(8,128)(4,1)S(1)} %iota_compare_fusion, bf16[512,8,128]{0,2,1:T(8,128)(2,1)} %bitcast.136, bf16[512,1024]{1,0:T(8,128)(2,1)} %param.13, bf16[512,1024]{1,0:T(8,128)(2,1)S(1)} %copy-done), kind=kOutput, calls=%fused_computation.5 | convolution fusion | flops 1084227584 | bytes 5521408 | tf_op jit(solution)/shard_map/hts,shd->thd/dot_general | solution.py:79
  19.4 49.2 %all-gather.6.cloned.1.call-done = bf16[128,16512]{1,0:T(8,128)(2,1)} async-done(((bf16[8,16512]{1,0:T(8,128)(2,1)}), bf16[128,16512]{1,0:T(8,128)(2,1)}) %all-gather.6.cloned.1.call-update) | async-done | bytes 4227088 | tf_op jit(solution)/shard_map/all_gather | solution.py:21
  68.6 0.9 fusion.41
  70.0 3.3 multiply_reduce_fusion
  73.3 1.3 multiply_reduce_fusion.1
  75.0 4.9 %convolution_convert_fusion.1 = bf16[512,3072]{1,0:T(8,128)(2,1)} fusion(bf16[512,1024]{0,1:T(8,128)(2,1)S(1)} %bitcast.134, bf16[1024,3072]{1,0:T(8,128)(2,1)S(1)} %bitcast.140), kind=kOutput, calls=%fused_computation.4 | convolution fusion | flops 3222798336 | bytes 10485760 | tf_op jit(solution)/shard_map/dot_general | solution.py:97
  81.1 32.0 %reduce-scatter.3.cloned.1.call-done = bf16[64,3072]{1,0:T(8,128)(2,1)} async-done(((bf16[512,3072]{1,0:T(8,128)(2,1)}), bf16[64,3072]{1,0:T(8,128)(2,1)}) %reduce-scatter.3.cloned.1.call-update) | async-done | bytes 393232 | tf_op jit(solution)/shard_map/reduce_scatter | solution.py:96
  113.0 1.2 multiply_reduce_fusion.2
  114.3 1.5 convolution_convert_fusion.2
  116.1 20.6 %all_to_all.14 = bf16[8,10,2,3072]{3,2,1,0:T(2,128)(2,1)S(1)} all-to-all(bf16[8,10,2,3072]{3,2,1,0:T(2,128)(2,1)S(1)} %reshape.304), channel_id=1, replica_groups=mesh['ctx'=16,'exp'=8] {'exp'}, dimensions={0} | all-to-all | bytes 1966080 | tf_op jit(solution)/shard_map/all_to_all | solution.py:118
  136.7 1.2 copy.101
  138.2 105.0 %all-gather.4.cloned.1.call-done = bf16[1280,2,3072]{2,0,1:T(8,128)(2,1)} async-done(((bf16[80,2,3072]{2,0,1:T(8,128)(2,1)}), bf16[1280,2,3072]{2,0,1:T(8,128)(2,1)}) %all-gather.4.cloned.1.call-update) | async-done | bytes 15728656 | tf_op jit(solution)/shard_map/all_gather | solution.py:121
  243.2 14.3 %fusion.43 = f32[2,1280,384]{2,1,0:T(8,128)} fusion(bf16[1280,2,3072]{2,0,1:T(8,128)(2,1)} %all-gather.4.cloned.1.call-done, bf16[2,3072,384]{2,1,0:T(8,128)(2,1)} %param.20), kind=kOutput, calls=%fused_computation.88 | convolution fusion | flops 6039797760 | bytes 24379392 | tf_op jit(solution)/shard_map/red,edf->ref/dot_general | solution.py:123
  257.5 25.0 %fusion = bf16[1280,2,3072]{2,0,1:T(8,128)(2,1)} fusion(bf16[2,384,3072]{2,1,0:T(8,128)(2,1)} %param.21, f32[2,1280,384]{2,1,0:T(8,128)} %fusion.43, bf16[1280,2,3072]{2,0,1:T(8,128)(2,1)} %all-gather.4.cloned.1.call-done, bf16[2,3072,384]{2,1,0:T(8,128)(2,1)} %param.19), kind=kOutput, calls=%fused_computation.1 | convolution fusion | flops 12093358080 | bytes 44826624 | tf_op jit(solution)/shard_map/ref,efd->red/dot_general | solution.py:126
  282.6 105.0 %reduce-scatter.5.cloned.1.call-done = bf16[80,2,3072]{2,0,1:T(8,128)(2,1)} async-done(((bf16[1280,2,3072]{2,0,1:T(8,128)(2,1)}), bf16[80,2,3072]{2,0,1:T(8,128)(2,1)}) %reduce-scatter.5.cloned.1.call-update) | async-done | bytes 983056 | tf_op jit(solution)/shard_map/reduce_scatter | solution.py:125
  387.6 3.2 copy.102
  390.8 5.9 %all-to-all-start.1 = ((bf16[8,10,2,3072]{3,2,1,0:T(2,128)(2,1)}), bf16[8,10,2,3072]{3,2,1,0:T(2,128)(2,1)S(1)}, u32[]{:S(2)}, u32[]{:S(2)}) async-start(bf16[8,10,2,3072]{3,2,1,0:T(2,128)(2,1)} %bitcast.16), calls=%async_computation.3 | async-start | bytes 1966080 | tf_op jit(solution)/shard_map/all_to_all | solution.py:134
  396.7 14.3 %all-to-all-done.1 = bf16[8,10,2,3072]{3,2,1,0:T(2,128)(2,1)S(1)} async-done(((bf16[8,10,2,3072]{3,2,1,0:T(2,128)(2,1)}), bf16[8,10,2,3072]{3,2,1,0:T(2,128)(2,1)S(1)}, u32[]{:S(2)}, u32[]{:S(2)}) %all-to-all-start.1) | async-done | bytes 983072 | tf_op jit(solution)/shard_map/all_to_all | solution.py:134
  411.4 0.4 fusion.31
  411.8 2.0 fusion.25
  (60 shorter events, 3.9 us)
Async XLA Ops:
  6.5 7.7 %copy-start = (bf16[512,1024]{1,0:T(8,128)(2,1)S(1)}, bf16[512,1024]{1,0:T(8,128)(2,1)}, u32[]{:S(2)}) copy-start(bf16[512,1024]{1,0:T(8,128)(2,1)} %param.11) | copy-start | bytes 3145732
  6.5 62.1 %all-gather.6.cloned.1.call-start = ((), (), s32[]{:S(2)}) async-start(), calls=%async_computation.7 | async-start | bytes 4491264 | tf_op jit(solution)/shard_map/all_gather | solution.py:21
  10.9 3.3 copy-start.3
  14.0 99.0 %reduce-scatter.3.cloned.1.call-start = ((), (), s32[]{:S(2)}) async-start(), calls=%async_computation.4 | async-start | bytes 3538944 | tf_op jit(solution)/shard_map/reduce_scatter | solution.py:96
  70.0 5.0 %slice-start = ((s8[6291456]{0:T(1024)(128)(4,1)}), s8[4194304]{0:T(1024)(128)(4,1)S(1)}, s32[]{:S(2)}) async-start(s8[6291456]{0:T(1024)(128)(4,1)} %bitcast.139), calls=%async_computation.8 | async-start | bytes 8388608
  73.3 1.7 slice-start.1
  75.0 5.0 %copy-start.4 = (s32[64,2]{0,1:T(2,128)S(1)}, s32[64,2]{0,1:T(2,128)}, u32[]{:S(2)}) copy-start(s32[64,2]{0,1:T(2,128)} %param.17) | copy-start | bytes 1540
  75.0 38.0 %copy-start.2 = (bf16[64,3072]{1,0:T(8,128)(2,1)S(1)}, bf16[64,3072]{1,0:T(8,128)(2,1)}, u32[]{:S(2)}) copy-start(bf16[64,3072]{1,0:T(8,128)(2,1)} %param.15) | copy-start | bytes 1179652
  80.0 163.2 %all-gather.4.cloned.1.call-start = ((), (), s32[]{:S(2)}) async-start(), calls=%async_computation.5 | async-start | bytes 16711680 | tf_op jit(solution)/shard_map/all_gather | solution.py:121
  137.9 249.7 %reduce-scatter.5.cloned.1.call-start = ((), (), s32[]{:S(2)}) async-start(), calls=%async_computation.6 | async-start | bytes 16711680 | tf_op jit(solution)/shard_map/reduce_scatter | solution.py:125
  282.5 114.2 %copy-start.5 = (f32[64,2]{0,1:T(2,128)S(1)}, f32[64,2]{0,1:T(2,128)}, u32[]{:S(2)}) copy-start(f32[64,2]{0,1:T(2,128)} %param.18) | copy-start | bytes 1540
  390.8 23.0 %copy-start.1 = (bf16[512,1024]{1,0:T(8,128)(2,1)S(1)}, bf16[512,1024]{1,0:T(8,128)(2,1)}, u32[]{:S(2)}) copy-start(bf16[512,1024]{1,0:T(8,128)(2,1)} %param.11) | copy-start | bytes 3145732
  390.8 20.2 %all-to-all-start.1 = ((bf16[8,10,2,3072]{3,2,1,0:T(2,128)(2,1)}), bf16[8,10,2,3072]{3,2,1,0:T(2,128)(2,1)S(1)}, u32[]{:S(2)}, u32[]{:S(2)}) async-start(bf16[8,10,2,3072]{3,2,1,0:T(2,128)(2,1)} %bitcast.16), calls=%async_computation.3 | async-start | bytes 1966080 | tf_op jit(solution)/shard_map/all_to_all | solution.py:134
Sparse Core Ops, SparseCore 0:
  14.1 54.4 all-gather.5
  80.1 32.8 reduce-scatter.2
  138.0 105.0 all-gather.3
  282.7 104.8 reduce-scatter.4

commit v3 on v2

--- a/solution.py
+++ b/solution.py
@@ -18,7 +18,9 @@
     payload = jnp.concatenate(
         [summary.astype(jnp.bfloat16).reshape(heads, hd * hd), rate_row], axis=1
     )
-    everything = lax.all_gather(payload, axis)
+    everything = lax.all_to_all(
+        jnp.broadcast_to(payload[None], (length,) + payload.shape), axis, 0, 0, tiled=True
+    )
     states = everything[:, :, : hd * hd].astype(jnp.float32)
     rates = everything[:, :, hd * hd].astype(jnp.float32) + everything[:, :, hd * hd + 1].astype(
         jnp.float32

time: 421 us -> 454 us (1.078)
  local copies, waits for them, and re-layouts: 8.8 us -> 22.3 us
  waiting for transfers between devices: 306 us -> 314 us
  starting transfers between devices: 6.23 us -> 13.8 us
    all_to_all x0 -> x1, waiting for transfers between devices: none -> 56.4 us  [carried_state(): lax.all_to_all(jnp.broadcast_to(payload[None], (length,) + payload.shape)...]
    all_gather x1 -> x0, waiting for transfers between devices: 49.2 us -> none  [carried_state(): everything = lax.all_gather(payload, axis)]
    all_to_all x0 -> x1, starting transfers between devices: none -> 7.61 us  [carried_state(): lax.all_to_all(jnp.broadcast_to(payload[None], (length,) + payload.shape)...]
    reshape x0 -> x1, local copies, waits for them, and re-layouts: none -> 5.99 us  [carried_state(): return carried.reshape(heads, hd, hd)]
    unnamed x20 -> x17, local copies, waits for them, and re-layouts: 0.59 us -> 5.85 us
where the time goes in v3:
time: 454 us; the launch traced here: 453 us
  waiting for transfers between devices  314 us (69%)
  matrix products  59.2 us (13%)
  local copies, waits for them, and re-layouts  22.3 us (5%)
  blocking collectives  20.6 us (5%)
  starting transfers between devices  13.8 us (3%)
  between operations  13.3 us (3%)
  other arithmetic  10.2 us (2%)
    all_gather x1, waiting for transfers between devices, on_device(): piece = lax.all_gather(arrived, 'ctx', axis=0, tiled=True)  105 us
    reduce_scatter x1, waiting for transfers between devices, on_device(): lax.psum_scatter(jnp.einsum('ref,efd->red', acts, w_down, preferred_eleme...  105 us
    all_to_all x1, waiting for transfers between devices, carried_state(): lax.all_to_all(jnp.broadcast_to(payload[None], (length,) + payload.shape)...  56.4 us
    reduce_scatter x1, waiting for transfers between devices, on_device(): lax.psum_scatter(jnp.dot(normed, out_proj, preferred_element_type=jnp.flo...  33 us
    dot_general x1, matrix products, on_device(): jnp.einsum('ref,efd->red', acts, w_down, preferred_element_type=jnp.float32)  25 us
    all_to_all x1, blocking collectives, on_device(): lax.all_to_all(packed, 'exp', split_axis=0, concat_axis=1, tiled=True)  20.6 us
    dot_general x1, matrix products, on_device(): jnp.einsum('red,edf->ref', piece, w_up, preferred_element_type=jnp.float32)  14.3 us
    all_to_all x1, waiting for transfers between devices, on_device(): lax.all_to_all(outgoing, 'exp', split_axis=0, concat_axis=0, tiled=True)  14.3 us
  transfers between devices with their start and end apart: 5, of which 5 were waited for; matrix products, arithmetic and copies ran while one was open for 2% of the time, Pallas kernels for 0%

profile of v3, /device:TPU:1, one launch (start us, length us, event | category | flops | bytes accessed | tf_op | source)
XLA Modules:
  0.0 453.4 jit_solution(17112400150863844373)
XLA Ops:
  6.5 2.3 reduce-window.6
  9.4 1.5 copy.139
  10.9 1.7 fusion.10
  12.9 2.3 broadcast_in_dim.102
  15.1 7.6 %all-to-all-start = ((bf16[16,8,16512]{2,1,0:T(8,128)(2,1)}), bf16[16,8,16512]{2,1,0:T(8,128)(2,1)}, u32[]{:S(2)}, u32[]{:S(2)}) async-start(bf16[16,8,16512]{2,1,0:T(8,128)(2,1)} %broadcast_in_dim.102), calls=%async_computation | async-start | bytes 8454144 | tf_op jit(solution)/shard_map/all_to_all | solution.py:21
  23.0 6.3 %fusion.1 = f32[8,512,128]{1,2,0:T(8,128)} fusion(f32[8,512]{1,0:T(8,128)S(1)} %add_bitcast_fusion.1, pred[512,512]{1,0:T(8,128)(4,1)S(1)} %iota_compare_fusion, bf16[512,8,128]{0,2,1:T(8,128)(2,1)S(1)} %bitcast.129, bf16[512,1024]{1,0:T(8,128)(2,1)} %param.13, bf16[512,1024]{1,0:T(8,128)(2,1)S(1)} %copy-done), kind=kOutput, calls=%fused_computation.5 | convolution fusion | flops 1084227584 | bytes 5521408 | tf_op jit(solution)/shard_map/hts,shd->thd/dot_general | solution.py:81
  29.2 56.4 %all-to-all-done = bf16[16,8,16512]{2,1,0:T(8,128)(2,1)} async-done(((bf16[16,8,16512]{2,1,0:T(8,128)(2,1)}), bf16[16,8,16512]{2,1,0:T(8,128)(2,1)}, u32[]{:S(2)}, u32[]{:S(2)}) %all-to-all-start) | async-done | bytes 4227104 | tf_op jit(solution)/shard_map/all_to_all | solution.py:21
  87.1 3.1 multiply_reduce_fusion
  90.2 5.3 %copy.136 = f32[8,16384]{0,1:T(8,128)} copy(f32[8,16384]{1,0:T(8,128)S(1)} %multiply_reduce_fusion) | data formatting | bytes 1048576
  95.5 6.0 %copy.132 = f32[8,128,128]{2,1,0:T(8,128)} copy(f32[8,128,128]{0,2,1:T(8,128)} %bitcast.125) | data formatting | bytes 1048576 | tf_op jit(solution)/shard_map/reshape | solution.py:33
  101.5 2.3 multiply_reduce_fusion.1
  104.1 7.7 %convolution_convert_fusion.1 = bf16[512,3072]{1,0:T(8,128)(2,1)} fusion(bf16[512,1024]{0,1:T(8,128)(2,1)S(1)} %bitcast.127, bf16[1024,3072]{1,0:T(8,128)(2,1)} %param.16), kind=kOutput, calls=%fused_computation.4 | convolution fusion | flops 3222798336 | bytes 10485760 | tf_op jit(solution)/shard_map/dot_general | solution.py:99
  113.1 33.0 %reduce-scatter.3.cloned.1.call-done = bf16[64,3072]{1,0:T(8,128)(2,1)} async-done(((bf16[512,3072]{1,0:T(8,128)(2,1)}), bf16[64,3072]{1,0:T(8,128)(2,1)}) %reduce-scatter.3.cloned.1.call-update) | async-done | bytes 393232 | tf_op jit(solution)/shard_map/reduce_scatter | solution.py:98
  146.2 1.2 multiply_reduce_fusion.2
  147.4 1.5 convolution_convert_fusion.2
  149.3 20.6 %all_to_all.19 = bf16[8,10,2,3072]{3,2,1,0:T(2,128)(2,1)S(1)} all-to-all(bf16[8,10,2,3072]{3,2,1,0:T(2,128)(2,1)S(1)} %reshape.305), channel_id=1, replica_groups=mesh['ctx'=16,'exp'=8] {'exp'}, dimensions={0} | all-to-all | bytes 1966080 | tf_op jit(solution)/shard_map/all_to_all | solution.py:120
  171.1 105.2 %all-gather.2.cloned.1.call-done = bf16[1280,2,3072]{2,0,1:T(8,128)(2,1)} async-done(((bf16[80,2,3072]{2,0,1:T(8,128)(2,1)}), bf16[1280,2,3072]{2,0,1:T(8,128)(2,1)}) %all-gather.2.cloned.1.call-update) | async-done | bytes 15728656 | tf_op jit(solution)/shard_map/all_gather | solution.py:123
  276.3 14.3 %fusion.41 = f32[2,1280,384]{2,1,0:T(8,128)} fusion(bf16[1280,2,3072]{2,0,1:T(8,128)(2,1)} %all-gather.2.cloned.1.call-done, bf16[2,3072,384]{2,1,0:T(8,128)(2,1)} %param.20), kind=kOutput, calls=%fused_computation.86 | convolution fusion | flops 6039797760 | bytes 24379392 | tf_op jit(solution)/shard_map/red,edf->ref/dot_general | solution.py:125
  290.6 25.0 %fusion = bf16[1280,2,3072]{2,0,1:T(8,128)(2,1)} fusion(bf16[2,384,3072]{2,1,0:T(8,128)(2,1)} %param.21, f32[2,1280,384]{2,1,0:T(8,128)} %fusion.41, bf16[1280,2,3072]{2,0,1:T(8,128)(2,1)} %all-gather.2.cloned.1.call-done, bf16[2,3072,384]{2,1,0:T(8,128)(2,1)} %param.19), kind=kOutput, calls=%fused_computation.1 | convolution fusion | flops 12093358080 | bytes 44826624 | tf_op jit(solution)/shard_map/ref,efd->red/dot_general | solution.py:128
  315.7 105.0 %reduce-scatter.5.cloned.1.call-done = bf16[80,2,3072]{2,0,1:T(8,128)(2,1)} async-done(((bf16[1280,2,3072]{2,0,1:T(8,128)(2,1)}), bf16[80,2,3072]{2,0,1:T(8,128)(2,1)}) %reduce-scatter.5.cloned.1.call-update) | async-done | bytes 983056 | tf_op jit(solution)/shard_map/reduce_scatter | solution.py:127
  420.7 3.2 copy.131
  423.9 5.9 %all-to-all-start.2 = ((bf16[8,10,2,3072]{3,2,1,0:T(2,128)(2,1)}), bf16[8,10,2,3072]{3,2,1,0:T(2,128)(2,1)S(1)}, u32[]{:S(2)}, u32[]{:S(2)}) async-start(bf16[8,10,2,3072]{3,2,1,0:T(2,128)(2,1)} %bitcast.16), calls=%async_computation.4 | async-start | bytes 1966080 | tf_op jit(solution)/shard_map/all_to_all | solution.py:136
  429.8 14.3 %all-to-all-done.2 = bf16[8,10,2,3072]{3,2,1,0:T(2,128)(2,1)S(1)} async-done(((bf16[8,10,2,3072]{3,2,1,0:T(2,128)(2,1)}), bf16[8,10,2,3072]{3,2,1,0:T(2,128)(2,1)S(1)}, u32[]{:S(2)}, u32[]{:S(2)}) %all-to-all-start.2) | async-done | bytes 983072 | tf_op jit(solution)/shard_map/all_to_all | solution.py:136
  444.9 2.0 fusion.25
  (57 shorter events, 6.4 us)
Async XLA Ops:
  6.5 16.5 %copy-start = (bf16[512,1024]{1,0:T(8,128)(2,1)S(1)}, bf16[512,1024]{1,0:T(8,128)(2,1)}, u32[]{:S(2)}) copy-start(bf16[512,1024]{1,0:T(8,128)(2,1)} %param.11) | copy-start | bytes 3145732
  15.1 70.6 %all-to-all-start = ((bf16[16,8,16512]{2,1,0:T(8,128)(2,1)}), bf16[16,8,16512]{2,1,0:T(8,128)(2,1)}, u32[]{:S(2)}, u32[]{:S(2)}) async-start(bf16[16,8,16512]{2,1,0:T(8,128)(2,1)} %broadcast_in_dim.102), calls=%async_computation | async-start | bytes 8454144 | tf_op jit(solution)/shard_map/all_to_all | solution.py:21
  22.8 123.4 %reduce-scatter.3.cloned.1.call-start = ((), (), s32[]{:S(2)}) async-start(), calls=%async_computation.5 | async-start | bytes 3538944 | tf_op jit(solution)/shard_map/reduce_scatter | solution.py:98
  95.5 6.0 %copy-start.3 = (f32[8,512,128]{1,2,0:T(8,128)S(1)}, f32[8,512,128]{1,2,0:T(8,128)}, u32[]{:S(2)}) copy-start(f32[8,512,128]{1,2,0:T(8,128)} %fusion.1) | copy-start | bytes 6291460
  104.1 8.0 %copy-start.4 = (s32[64,2]{0,1:T(2,128)S(1)}, s32[64,2]{0,1:T(2,128)}, u32[]{:S(2)}) copy-start(s32[64,2]{0,1:T(2,128)} %param.17) | copy-start | bytes 1540
  104.1 42.0 %copy-start.2 = (bf16[64,3072]{1,0:T(8,128)(2,1)S(1)}, bf16[64,3072]{1,0:T(8,128)(2,1)}, u32[]{:S(2)}) copy-start(bf16[64,3072]{1,0:T(8,128)(2,1)} %param.15) | copy-start | bytes 1179652
  111.8 164.5 %all-gather.2.cloned.1.call-start = ((), (), s32[]{:S(2)}) async-start(), calls=%async_computation.6 | async-start | bytes 16711680 | tf_op jit(solution)/shard_map/all_gather | solution.py:123
  171.0 249.7 %reduce-scatter.5.cloned.1.call-start = ((), (), s32[]{:S(2)}) async-start(), calls=%async_computation.7 | async-start | bytes 16711680 | tf_op jit(solution)/shard_map/reduce_scatter | solution.py:127
  315.7 114.2 %copy-start.5 = (f32[64,2]{0,1:T(2,128)S(1)}, f32[64,2]{0,1:T(2,128)}, u32[]{:S(2)}) copy-start(f32[64,2]{0,1:T(2,128)} %param.18) | copy-start | bytes 1540
  423.9 23.0 %copy-start.1 = (bf16[512,1024]{1,0:T(8,128)(2,1)S(1)}, bf16[512,1024]{1,0:T(8,128)(2,1)}, u32[]{:S(2)}) copy-start(bf16[512,1024]{1,0:T(8,128)(2,1)} %param.11) | copy-start | bytes 3145732
  423.9 20.2 %all-to-all-start.2 = ((bf16[8,10,2,3072]{3,2,1,0:T(2,128)(2,1)}), bf16[8,10,2,3072]{3,2,1,0:T(2,128)(2,1)S(1)}, u32[]{:S(2)}, u32[]{:S(2)}) async-start(bf16[8,10,2,3072]{3,2,1,0:T(2,128)(2,1)} %bitcast.16), calls=%async_computation.4 | async-start | bytes 1966080 | tf_op jit(solution)/shard_map/all_to_all | solution.py:136
Sparse Core Ops, SparseCore 0:
  112.0 34.1 reduce-scatter.2
  171.2 105.0 all-gather.1
  315.8 104.8 reduce-scatter.4

commit v4 on v2

--- a/solution.py
+++ b/solution.py
@@ -119,8 +119,15 @@
         n_exp * capacity, local_experts, width
     )
     piece = lax.all_gather(arrived, "ctx", axis=0, tiled=True)
-    gate = jnp.einsum("red,edf->ref", piece, w_gate, preferred_element_type=jnp.float32)
-    upper = jnp.einsum("red,edf->ref", piece, w_up, preferred_element_type=jnp.float32)
+    hidden_units = w_gate.shape[2]
+    both = jnp.einsum(
+        "red,edf->ref",
+        piece,
+        jnp.concatenate([w_gate, w_up], axis=2),
+        preferred_element_type=jnp.float32,
+    )
+    gate = both[:, :, :hidden_units]
+    upper = both[:, :, hidden_units:]
     acts = (jax.nn.silu(gate) * upper).astype(jnp.bfloat16)
     summed = lax.psum_scatter(
         jnp.einsum("ref,efd->red", acts, w_down, preferred_element_type=jnp.float32).astype(

time: 421 us -> 416 us (0.988)
  waiting for transfers between devices: 306 us -> 292 us
  local copies, waits for them, and re-layouts: 8.8 us -> 22.4 us
  matrix products: 54.8 us -> 50 us
    all_gather x1, waiting for transfers between devices: 105 us -> 91.5 us  [on_device(): piece = lax.all_gather(arrived, 'ctx', axis=0, tiled=True)]
    unnamed x20 -> x22, local copies, waits for them, and re-layouts: 0.59 us -> 14.2 us
    dot_general x1, matrix products: 25 us -> 15.4 us  [on_device(): jnp.einsum('ref,efd->red', acts, w_down, preferred_element_type=jnp.float32)]
    dot_general x1, matrix products: 14.3 us -> 19.2 us  [on_device(): jnp.einsum('red,edf->ref', piece, jnp.concatenate([w_gate, w_up], axis=2)...]
  transfers between devices with their start and end apart: 5 -> 5, of which waited for: 5 -> 5; matrix products, arithmetic and copies ran while one was open for 2% -> 5% of each run, Pallas kernels for 0% -> 0%
where the time goes in v4:
time: 416 us; the launch traced here: 415 us
  waiting for transfers between devices  292 us (70%)
  matrix products  50 us (12%)
  local copies, waits for them, and re-layouts  22.4 us (5%)
  blocking collectives  20.6 us (5%)
  between operations  13.4 us (3%)
  other arithmetic  11 us (3%)
  starting transfers between devices  6.08 us (1%)
    reduce_scatter x1, waiting for transfers between devices, on_device(): lax.psum_scatter(jnp.einsum('ref,efd->red', acts, w_down, preferred_eleme...  105 us
    all_gather x1, waiting for transfers between devices, on_device(): piece = lax.all_gather(arrived, 'ctx', axis=0, tiled=True)  91.5 us
    all_gather x1, waiting for transfers between devices, carried_state(): everything = lax.all_gather(payload, axis)  49.2 us
    reduce_scatter x1, waiting for transfers between devices, on_device(): lax.psum_scatter(jnp.dot(normed, out_proj, preferred_element_type=jnp.flo...  32 us
    all_to_all x1, blocking collectives, on_device(): lax.all_to_all(packed, 'exp', split_axis=0, concat_axis=1, tiled=True)  20.6 us
    dot_general x1, matrix products, on_device(): jnp.einsum('red,edf->ref', piece, jnp.concatenate([w_gate, w_up], axis=2)...  19.2 us
    dot_general x1, matrix products, on_device(): jnp.einsum('ref,efd->red', acts, w_down, preferred_element_type=jnp.float32)  15.4 us
    all_to_all x1, waiting for transfers between devices, on_device(): lax.all_to_all(outgoing, 'exp', split_axis=0, concat_axis=0, tiled=True)  14.3 us
  transfers between devices with their start and end apart: 5, of which 5 were waited for; matrix products, arithmetic and copies ran while one was open for 5% of the time, Pallas kernels for 0%

profile of v4, /device:TPU:1, one launch (start us, length us, event | category | flops | bytes accessed | tf_op | source)
XLA Modules:
  0.0 415.4 jit_solution(8647455658461594905)
XLA Ops:
  6.5 2.3 reduce-window.6
  9.4 1.5 copy.122
  10.9 2.1 fusion.16
  14.2 5.2 %fusion.8 = f32[8,512,128]{1,2,0:T(8,128)S(1)} fusion(f32[8,512]{1,0:T(8,128)S(1)} %add_bitcast_fusion.1, pred[512,512]{1,0:T(8,128)(4,1)S(1)} %iota_compare_fusion, bf16[512,8,128]{0,2,1:T(8,128)(2,1)} %bitcast.101, bf16[512,1024]{1,0:T(8,128)(2,1)} %param.13, bf16[512,1024]{1,0:T(8,128)(2,1)S(1)} %copy-done), kind=kOutput, calls=%fused_computation.10 | convolution fusion | flops 1084227584 | bytes 5521408 | tf_op jit(solution)/shard_map/hts,shd->thd/dot_general | solution.py:79
  19.4 49.2 %all-gather.6.cloned.1.call-done = bf16[128,16512]{1,0:T(8,128)(2,1)} async-done(((bf16[8,16512]{1,0:T(8,128)(2,1)}), bf16[128,16512]{1,0:T(8,128)(2,1)}) %all-gather.6.cloned.1.call-update) | async-done | bytes 4227088 | tf_op jit(solution)/shard_map/all_gather | solution.py:21
  68.6 0.9 fusion.49
  70.0 3.3 multiply_reduce_fusion
  73.3 1.3 multiply_reduce_fusion.1
  75.0 4.9 %convolution_convert_fusion.1 = bf16[512,3072]{1,0:T(8,128)(2,1)} fusion(bf16[512,1024]{0,1:T(8,128)(2,1)S(1)} %bitcast.99, bf16[1024,3072]{1,0:T(8,128)(2,1)S(1)} %bitcast.105), kind=kOutput, calls=%fused_computation.9 | convolution fusion | flops 3222798336 | bytes 10485760 | tf_op jit(solution)/shard_map/dot_general | solution.py:97
  81.1 32.0 %reduce-scatter.3.cloned.1.call-done = bf16[64,3072]{1,0:T(8,128)(2,1)} async-done(((bf16[512,3072]{1,0:T(8,128)(2,1)}), bf16[64,3072]{1,0:T(8,128)(2,1)}) %reduce-scatter.3.cloned.1.call-update) | async-done | bytes 393232 | tf_op jit(solution)/shard_map/reduce_scatter | solution.py:96
  113.0 1.2 multiply_reduce_fusion.2
  114.3 1.5 convolution_convert_fusion.2
  116.1 20.6 %all_to_all.14 = bf16[8,10,2,3072]{3,2,1,0:T(2,128)(2,1)S(1)} all-to-all(bf16[8,10,2,3072]{3,2,1,0:T(2,128)(2,1)S(1)} %reshape.304), channel_id=1, replica_groups=mesh['ctx'=16,'exp'=8] {'exp'}, dimensions={0} | all-to-all | bytes 1966080 | tf_op jit(solution)/shard_map/all_to_all | solution.py:118
  136.7 1.2 copy.115
  138.2 6.7 %copy.113 = bf16[2,3072,384]{1,2,0:T(8,128)(2,1)} copy(bf16[2,3072,384]{2,1,0:T(8,128)(2,1)} %param.19) | data formatting | bytes 9437184 | tf_op args[8]
  144.8 6.9 %copy.114 = bf16[2,3072,384]{1,2,0:T(8,128)(2,1)} copy(bf16[2,3072,384]{2,1,0:T(8,128)(2,1)} %param.20) | data formatting | bytes 9437184 | tf_op args[9]
  151.7 91.5 %all-gather.4.cloned.1.call-done = bf16[1280,2,3072]{2,0,1:T(8,128)(2,1)} async-done(((bf16[80,2,3072]{2,0,1:T(8,128)(2,1)}), bf16[1280,2,3072]{2,0,1:T(8,128)(2,1)}) %all-gather.4.cloned.1.call-update) | async-done | bytes 15728656 | tf_op jit(solution)/shard_map/all_gather | solution.py:121
  243.2 19.2 %fusion.5 = f32[1280,2,768]{0,2,1:T(8,128)} fusion(bf16[1280,2,3072]{2,0,1:T(8,128)(2,1)} %all-gather.4.cloned.1.call-done, bf16[2,3072,384]{1,2,0:T(8,128)(2,1)} %copy.114, bf16[2,3072,384]{1,2,0:T(8,128)(2,1)} %copy.113), kind=kOutput, calls=%fused_computation.8 | convolution fusion | flops 12098469888 | bytes 33030144 | tf_op jit(solution)/shard_map/red,edf->ref/dot_general | solution.py:123
  262.3 15.4 %fusion = bf16[1280,2,3072]{2,0,1:T(8,128)(2,1)} fusion(bf16[2,384,3072]{2,1,0:T(8,128)(2,1)} %param.21, f32[1280,2,768]{0,2,1:T(8,128)} %fusion.5), kind=kOutput, calls=%fused_computation.1 | convolution fusion | flops 6053560320 | bytes 28311552 | tf_op jit(solution)/shard_map/ref,efd->red/dot_general | solution.py:133
  277.8 105.0 %reduce-scatter.5.cloned.1.call-done = bf16[80,2,3072]{2,0,1:T(8,128)(2,1)} async-done(((bf16[1280,2,3072]{2,0,1:T(8,128)(2,1)}), bf16[80,2,3072]{2,0,1:T(8,128)(2,1)}) %reduce-scatter.5.cloned.1.call-update) | async-done | bytes 983056 | tf_op jit(solution)/shard_map/reduce_scatter | solution.py:132
  382.8 3.3 copy.117
  386.1 5.8 %all-to-all-start.1 = ((bf16[8,10,2,3072]{3,2,1,0:T(2,128)(2,1)}), bf16[8,10,2,3072]{3,2,1,0:T(2,128)(2,1)S(1)}, u32[]{:S(2)}, u32[]{:S(2)}) async-start(bf16[8,10,2,3072]{3,2,1,0:T(2,128)(2,1)} %bitcast.15), calls=%async_computation.3 | async-start | bytes 1966080 | tf_op jit(solution)/shard_map/all_to_all | solution.py:141
  391.8 14.3 %all-to-all-done.1 = bf16[8,10,2,3072]{3,2,1,0:T(2,128)(2,1)S(1)} async-done(((bf16[8,10,2,3072]{3,2,1,0:T(2,128)(2,1)}), bf16[8,10,2,3072]{3,2,1,0:T(2,128)(2,1)S(1)}, u32[]{:S(2)}, u32[]{:S(2)}) %all-to-all-start.1) | async-done | bytes 983072 | tf_op jit(solution)/shard_map/all_to_all | solution.py:141
  406.9 2.0 fusion.31
  (62 shorter events, 5.0 us)
Async XLA Ops:
  6.5 7.7 %copy-start = (bf16[512,1024]{1,0:T(8,128)(2,1)S(1)}, bf16[512,1024]{1,0:T(8,128)(2,1)}, u32[]{:S(2)}) copy-start(bf16[512,1024]{1,0:T(8,128)(2,1)} %param.11) | copy-start | bytes 3145732
  6.5 62.1 %all-gather.6.cloned.1.call-start = ((), (), s32[]{:S(2)}) async-start(), calls=%async_computation.7 | async-start | bytes 4491264 | tf_op jit(solution)/shard_map/all_gather | solution.py:21
  10.9 3.3 copy-start.3
  14.0 99.0 %reduce-scatter.3.cloned.1.call-start = ((), (), s32[]{:S(2)}) async-start(), calls=%async_computation.4 | async-start | bytes 3538944 | tf_op jit(solution)/shard_map/reduce_scatter | solution.py:96
  70.0 5.0 %slice-start = ((s8[6291456]{0:T(1024)(128)(4,1)}), s8[4194304]{0:T(1024)(128)(4,1)S(1)}, s32[]{:S(2)}) async-start(s8[6291456]{0:T(1024)(128)(4,1)} %bitcast.104), calls=%async_computation.8 | async-start | bytes 8388608
  73.3 1.7 slice-start.1
  75.0 5.0 %copy-start.4 = (s32[64,2]{0,1:T(2,128)S(1)}, s32[64,2]{0,1:T(2,128)}, u32[]{:S(2)}) copy-start(s32[64,2]{0,1:T(2,128)} %param.17) | copy-start | bytes 1540
  75.0 38.0 %copy-start.2 = (bf16[64,3072]{1,0:T(8,128)(2,1)S(1)}, bf16[64,3072]{1,0:T(8,128)(2,1)}, u32[]{:S(2)}) copy-start(bf16[64,3072]{1,0:T(8,128)(2,1)} %param.15) | copy-start | bytes 1179652
  80.0 163.2 %all-gather.4.cloned.1.call-start = ((), (), s32[]{:S(2)}) async-start(), calls=%async_computation.5 | async-start | bytes 16711680 | tf_op jit(solution)/shard_map/all_gather | solution.py:121
  137.9 244.9 %reduce-scatter.5.cloned.1.call-start = ((), (), s32[]{:S(2)}) async-start(), calls=%async_computation.6 | async-start | bytes 16711680 | tf_op jit(solution)/shard_map/reduce_scatter | solution.py:132
  277.8 114.1 %copy-start.5 = (f32[64,2]{0,1:T(2,128)S(1)}, f32[64,2]{0,1:T(2,128)}, u32[]{:S(2)}) copy-start(f32[64,2]{0,1:T(2,128)} %param.18) | copy-start | bytes 1540
  382.8 26.1 %copy-start.1 = (bf16[512,1024]{1,0:T(8,128)(2,1)S(1)}, bf16[512,1024]{1,0:T(8,128)(2,1)}, u32[]{:S(2)}) copy-start(bf16[512,1024]{1,0:T(8,128)(2,1)} %param.11) | copy-start | bytes 3145732
  386.1 20.0 %all-to-all-start.1 = ((bf16[8,10,2,3072]{3,2,1,0:T(2,128)(2,1)}), bf16[8,10,2,3072]{3,2,1,0:T(2,128)(2,1)S(1)}, u32[]{:S(2)}, u32[]{:S(2)}) async-start(bf16[8,10,2,3072]{3,2,1,0:T(2,128)(2,1)} %bitcast.15), calls=%async_computation.3 | async-start | bytes 1966080 | tf_op jit(solution)/shard_map/all_to_all | solution.py:141
Sparse Core Ops, SparseCore 0:
  14.1 54.4 all-gather.5
  80.1 32.8 reduce-scatter.2
  138.0 105.0 all-gather.3
  277.9 104.8 reduce-scatter.4

commit v5 on v4

--- a/solution.py
+++ b/solution.py
@@ -27,7 +27,7 @@
     between = ((block[:, None] < block[None, :]) & (block[None, :] < here)).astype(jnp.float32)
     exponent = jnp.sum(between[:, :, None] * rates[None, :, :], axis=1)
     weight = jnp.where((block < here)[:, None], jnp.exp(exponent), 0.0)
-    carried = jnp.sum(weight[:, :, None] * states, axis=0)
+    carried = jnp.einsum("kh,khx->hx", weight, states, precision=lax.Precision.HIGHEST)
     return carried.reshape(heads, hd, hd)
 
 
@@ -68,9 +68,10 @@
     q_heads = queries.reshape(tok, heads_here, head_dim)
     k_heads = keys.reshape(tok, heads_here, head_dim)
     v_heads = values.reshape(tok, heads_here, head_dim)
-    cum = jnp.cumsum(log_decay, axis=0)
+    place = jnp.arange(tok, dtype=jnp.int32)
+    lower = (place[:, None] >= place[None, :]).astype(jnp.float32)
+    cum = jnp.dot(lower, log_decay, precision=lax.Precision.HIGHEST)
     scores = jnp.einsum("thd,shd->hts", q_heads, k_heads, preferred_element_type=jnp.float32)
-    place = jnp.arange(tok, dtype=jnp.int32)
     causal = (place[:, None] >= place[None, :])[None]
     diff = cum.T[:, :, None] - cum.T[:, None, :]
     weights = jnp.where(causal, scores * jnp.exp(jnp.where(causal, diff, 0.0)), 0.0).astype(

time: 416 us -> 425 us (1.022)
  matrix products: 50 us -> 59.4 us
  other arithmetic: 11 us -> 5.24 us
  local copies, waits for them, and re-layouts: 22.4 us -> 27.1 us
    dot_general x0 -> x2, matrix products: none -> 9.4 us  [the longest x1 8.22 us: carried_state(): jnp.einsum('kh,khx->hx', weight, states, precision=lax.Precision.HIGHEST)]
    slice x1, local copies, waits for them, and re-layouts: 0.16 us -> 4.54 us  [carried_state(): states = everything[:, :, :hd * hd].astype(jnp.float32)]
where the time goes in v5:
time: 425 us; the launch traced here: 424 us
  waiting for transfers between devices  292 us (69%)
  matrix products  59.4 us (14%)
  local copies, waits for them, and re-layouts  27.1 us (6%)
  blocking collectives  20.6 us (5%)
  between operations  13.6 us (3%)
  starting transfers between devices  5.92 us (1%)
  other arithmetic  5.24 us (1%)
    reduce_scatter x1, waiting for transfers between devices, on_device(): lax.psum_scatter(jnp.einsum('ref,efd->red', acts, w_down, preferred_eleme...  105 us
    all_gather x1, waiting for transfers between devices, on_device(): piece = lax.all_gather(arrived, 'ctx', axis=0, tiled=True)  91.8 us
    all_gather x1, waiting for transfers between devices, carried_state(): everything = lax.all_gather(payload, axis)  49.2 us
    reduce_scatter x1, waiting for transfers between devices, on_device(): lax.psum_scatter(jnp.dot(normed, out_proj, preferred_element_type=jnp.flo...  32 us
    all_to_all x1, blocking collectives, on_device(): lax.all_to_all(packed, 'exp', split_axis=0, concat_axis=1, tiled=True)  20.6 us
    dot_general x1, matrix products, on_device(): jnp.einsum('red,edf->ref', piece, jnp.concatenate([w_gate, w_up], axis=2)...  19.2 us
    dot_general x1, matrix products, on_device(): jnp.einsum('ref,efd->red', acts, w_down, preferred_element_type=jnp.float32)  15.4 us
    all_to_all x1, waiting for transfers between devices, on_device(): lax.all_to_all(outgoing, 'exp', split_axis=0, concat_axis=0, tiled=True)  14.3 us
  transfers between devices with their start and end apart: 5, of which 5 were waited for; matrix products, arithmetic and copies ran while one was open for 5% of the time, Pallas kernels for 0%

profile of v5, /device:TPU:1, one launch (start us, length us, event | category | flops | bytes accessed | tf_op | source)
XLA Modules:
  0.0 424.2 jit_solution(15052449897159912733)
XLA Ops:
  6.5 1.2 fusion.38
  8.1 1.5 copy.98
  9.6 2.1 fusion.18
  12.9 5.2 %fusion.10 = f32[8,512,128]{1,2,0:T(8,128)S(1)} fusion(f32[8,512]{1,0:T(8,128)S(1)} %bitcast.102, pred[512,512]{1,0:T(8,128)(4,1)S(1)} %iota_compare_fusion, bf16[512,8,128]{0,2,1:T(8,128)(2,1)} %bitcast.100, bf16[512,1024]{1,0:T(8,128)(2,1)} %param.13, bf16[512,1024]{1,0:T(8,128)(2,1)S(1)} %copy-done), kind=kOutput, calls=%fused_computation.11 | convolution fusion | flops 1084227584 | bytes 5521408 | tf_op jit(solution)/shard_map/hts,shd->thd/dot_general | solution.py:80
  18.1 49.2 %all-gather.6.cloned.1.call-done = bf16[128,16512]{1,0:T(8,128)(2,1)} async-done(((bf16[8,16512]{1,0:T(8,128)(2,1)}), bf16[128,16512]{1,0:T(8,128)(2,1)}) %all-gather.6.cloned.1.call-update) | async-done | bytes 4227088 | tf_op jit(solution)/shard_map/all_gather | solution.py:21
  68.2 4.5 %slice.43 = bf16[16,8,16384]{2,1,0:T(8,128)(2,1)} slice(bf16[16,8,16512]{2,1,0:T(8,128)(2,1)} %bitcast.95), slice={[0:16], [0:8], [0:16384]} | slice | bytes 8388608 | tf_op jit(solution)/shard_map/slice | solution.py:22
  73.3 8.2 %fusion.8 = f32[8,1,16384]{2,1,0:T(1,128)S(1)} fusion(f32[16,8,1]{0,2,1:T(1,128)S(1)} %copy.91, bf16[16,8,16384]{2,1,0:T(8,128)(2,1)} %slice.43), kind=kOutput, calls=%fused_computation.9 | convolution fusion | flops 25165824 | bytes 4719104 | tf_op jit(solution)/shard_map/kh,khx->hx/dot_general | solution.py:30
  81.9 1.3 multiply_reduce_fusion
  83.7 4.9 %convolution_convert_fusion.1 = bf16[512,3072]{1,0:T(8,128)(2,1)} fusion(bf16[512,1024]{0,1:T(8,128)(2,1)S(1)} %bitcast.98, bf16[1024,3072]{1,0:T(8,128)(2,1)S(1)} %bitcast.104), kind=kOutput, calls=%fused_computation.8 | convolution fusion | flops 3222798336 | bytes 10485760 | tf_op jit(solution)/shard_map/dot_general | solution.py:98
  89.8 32.0 %reduce-scatter.3.cloned.1.call-done = bf16[64,3072]{1,0:T(8,128)(2,1)} async-done(((bf16[512,3072]{1,0:T(8,128)(2,1)}), bf16[64,3072]{1,0:T(8,128)(2,1)}) %reduce-scatter.3.cloned.1.call-update) | async-done | bytes 393232 | tf_op jit(solution)/shard_map/reduce_scatter | solution.py:97
  121.7 1.2 multiply_reduce_fusion.1
  122.9 1.5 convolution_convert_fusion.2
  124.8 20.6 %all_to_all.14 = bf16[8,10,2,3072]{3,2,1,0:T(2,128)(2,1)S(1)} all-to-all(bf16[8,10,2,3072]{3,2,1,0:T(2,128)(2,1)S(1)} %reshape.255), channel_id=1, replica_groups=mesh['ctx'=16,'exp'=8] {'exp'}, dimensions={0} | all-to-all | bytes 1966080 | tf_op jit(solution)/shard_map/all_to_all | solution.py:119
  145.4 1.2 copy.88
  146.7 6.7 %copy.86 = bf16[2,3072,384]{1,2,0:T(8,128)(2,1)} copy(bf16[2,3072,384]{2,1,0:T(8,128)(2,1)} %param.19) | data formatting | bytes 9437184 | tf_op args[8]
  153.3 6.8 %copy.87 = bf16[2,3072,384]{1,2,0:T(8,128)(2,1)} copy(bf16[2,3072,384]{2,1,0:T(8,128)(2,1)} %param.20) | data formatting | bytes 9437184 | tf_op args[9]
  160.1 91.8 %all-gather.4.cloned.1.call-done = bf16[1280,2,3072]{2,0,1:T(8,128)(2,1)} async-done(((bf16[80,2,3072]{2,0,1:T(8,128)(2,1)}), bf16[1280,2,3072]{2,0,1:T(8,128)(2,1)}) %all-gather.4.cloned.1.call-update) | async-done | bytes 15728656 | tf_op jit(solution)/shard_map/all_gather | solution.py:122
  251.9 19.2 %fusion.5 = f32[1280,2,768]{0,2,1:T(8,128)} fusion(bf16[1280,2,3072]{2,0,1:T(8,128)(2,1)} %all-gather.4.cloned.1.call-done, bf16[2,3072,384]{1,2,0:T(8,128)(2,1)} %copy.87, bf16[2,3072,384]{1,2,0:T(8,128)(2,1)} %copy.86), kind=kOutput, calls=%fused_computation.7 | convolution fusion | flops 12098469888 | bytes 33030144 | tf_op jit(solution)/shard_map/red,edf->ref/dot_general | solution.py:124
  271.0 15.4 %fusion = bf16[1280,2,3072]{2,0,1:T(8,128)(2,1)} fusion(bf16[2,384,3072]{2,1,0:T(8,128)(2,1)} %param.21, f32[1280,2,768]{0,2,1:T(8,128)} %fusion.5), kind=kOutput, calls=%fused_computation.1 | convolution fusion | flops 6053560320 | bytes 28311552 | tf_op jit(solution)/shard_map/ref,efd->red/dot_general | solution.py:134
  286.5 105.0 %reduce-scatter.5.cloned.1.call-done = bf16[80,2,3072]{2,0,1:T(8,128)(2,1)} async-done(((bf16[1280,2,3072]{2,0,1:T(8,128)(2,1)}), bf16[80,2,3072]{2,0,1:T(8,128)(2,1)}) %reduce-scatter.5.cloned.1.call-update) | async-done | bytes 983056 | tf_op jit(solution)/shard_map/reduce_scatter | solution.py:133
  391.5 3.3 copy.90
  394.8 5.8 %all-to-all-start.1 = ((bf16[8,10,2,3072]{3,2,1,0:T(2,128)(2,1)}), bf16[8,10,2,3072]{3,2,1,0:T(2,128)(2,1)S(1)}, u32[]{:S(2)}, u32[]{:S(2)}) async-start(bf16[8,10,2,3072]{3,2,1,0:T(2,128)(2,1)} %bitcast.13), calls=%async_computation.3 | async-start | bytes 1966080 | tf_op jit(solution)/shard_map/all_to_all | solution.py:142
  400.6 14.3 %all-to-all-done.1 = bf16[8,10,2,3072]{3,2,1,0:T(2,128)(2,1)S(1)} async-done(((bf16[8,10,2,3072]{3,2,1,0:T(2,128)(2,1)}), bf16[8,10,2,3072]{3,2,1,0:T(2,128)(2,1)S(1)}, u32[]{:S(2)}, u32[]{:S(2)}) %all-to-all-start.1) | async-done | bytes 983072 | tf_op jit(solution)/shard_map/all_to_all | solution.py:142
  415.6 2.0 fusion.33
  (60 shorter events, 5.9 us)
Async XLA Ops:
  6.5 6.3 %copy-start = (bf16[512,1024]{1,0:T(8,128)(2,1)S(1)}, bf16[512,1024]{1,0:T(8,128)(2,1)}, u32[]{:S(2)}) copy-start(bf16[512,1024]{1,0:T(8,128)(2,1)} %param.11) | copy-start | bytes 3145732
  6.5 60.8 %all-gather.6.cloned.1.call-start = ((), (), s32[]{:S(2)}) async-start(), calls=%async_computation.7 | async-start | bytes 4491264 | tf_op jit(solution)/shard_map/all_gather | solution.py:21
  9.6 3.3 copy-start.3
  12.7 109.0 %reduce-scatter.3.cloned.1.call-start = ((), (), s32[]{:S(2)}) async-start(), calls=%async_computation.4 | async-start | bytes 3538944 | tf_op jit(solution)/shard_map/reduce_scatter | solution.py:97
  73.3 10.2 %slice-start = ((s8[6291456]{0:T(1024)(128)(4,1)}), s8[4194304]{0:T(1024)(128)(4,1)S(1)}, s32[]{:S(2)}) async-start(s8[6291456]{0:T(1024)(128)(4,1)} %bitcast.103), calls=%async_computation.8 | async-start | bytes 8388608
  81.8 1.9 slice-start.1
  83.7 5.0 %copy-start.4 = (s32[64,2]{0,1:T(2,128)S(1)}, s32[64,2]{0,1:T(2,128)}, u32[]{:S(2)}) copy-start(s32[64,2]{0,1:T(2,128)} %param.17) | copy-start | bytes 1540
  83.7 38.0 %copy-start.2 = (bf16[64,3072]{1,0:T(8,128)(2,1)S(1)}, bf16[64,3072]{1,0:T(8,128)(2,1)}, u32[]{:S(2)}) copy-start(bf16[64,3072]{1,0:T(8,128)(2,1)} %param.15) | copy-start | bytes 1179652
  88.7 163.2 %all-gather.4.cloned.1.call-start = ((), (), s32[]{:S(2)}) async-start(), calls=%async_computation.5 | async-start | bytes 16711680 | tf_op jit(solution)/shard_map/all_gather | solution.py:122
  146.6 244.9 %reduce-scatter.5.cloned.1.call-start = ((), (), s32[]{:S(2)}) async-start(), calls=%async_computation.6 | async-start | bytes 16711680 | tf_op jit(solution)/shard_map/reduce_scatter | solution.py:133
  286.5 114.1 %copy-start.5 = (f32[64,2]{0,1:T(2,128)S(1)}, f32[64,2]{0,1:T(2,128)}, u32[]{:S(2)}) copy-start(f32[64,2]{0,1:T(2,128)} %param.18) | copy-start | bytes 1540
  391.5 26.1 %copy-start.1 = (bf16[512,1024]{1,0:T(8,128)(2,1)S(1)}, bf16[512,1024]{1,0:T(8,128)(2,1)}, u32[]{:S(2)}) copy-start(bf16[512,1024]{1,0:T(8,128)(2,1)} %param.11) | copy-start | bytes 3145732
  394.8 20.1 %all-to-all-start.1 = ((bf16[8,10,2,3072]{3,2,1,0:T(2,128)(2,1)}), bf16[8,10,2,3072]{3,2,1,0:T(2,128)(2,1)S(1)}, u32[]{:S(2)}, u32[]{:S(2)}) async-start(bf16[8,10,2,3072]{3,2,1,0:T(2,128)(2,1)} %bitcast.13), calls=%async_computation.3 | async-start | bytes 1966080 | tf_op jit(solution)/shard_map/all_to_all | solution.py:142
Sparse Core Ops, SparseCore 0:
  12.8 54.4 all-gather.5
  88.8 32.8 reduce-scatter.2
  146.7 105.0 all-gather.3
  286.6 104.8 reduce-scatter.4

commit v6 on v5

--- a/solution.py
+++ b/solution.py
@@ -6,29 +6,40 @@
 EPS = 1e-06
 
 
-def carried_state(last, summary, axis):
-    length, here = (lax.axis_size(axis), lax.axis_index(axis))
-    heads, hd, _ = summary.shape
-    hi = last.astype(jnp.bfloat16)
-    lo = (last - hi.astype(jnp.float32)).astype(jnp.bfloat16)
+def pack(rate, state):
+    heads, hd, _ = state.shape
+    hi = rate.astype(jnp.bfloat16)
+    lo = (rate - hi.astype(jnp.float32)).astype(jnp.bfloat16)
     lane = jnp.arange(hd, dtype=jnp.int32)[None, :]
     rate_row = jnp.where(lane == 0, hi[:, None], jnp.where(lane == 1, lo[:, None], 0.0)).astype(
         jnp.bfloat16
     )
-    payload = jnp.concatenate(
-        [summary.astype(jnp.bfloat16).reshape(heads, hd * hd), rate_row], axis=1
-    )
-    everything = lax.all_gather(payload, axis)
-    states = everything[:, :, : hd * hd].astype(jnp.float32)
-    rates = everything[:, :, hd * hd].astype(jnp.float32) + everything[:, :, hd * hd + 1].astype(
-        jnp.float32
-    )
-    block = jnp.arange(length, dtype=jnp.int32)
-    between = ((block[:, None] < block[None, :]) & (block[None, :] < here)).astype(jnp.float32)
-    exponent = jnp.sum(between[:, :, None] * rates[None, :, :], axis=1)
-    weight = jnp.where((block < here)[:, None], jnp.exp(exponent), 0.0)
-    carried = jnp.einsum("kh,khx->hx", weight, states, precision=lax.Precision.HIGHEST)
-    return carried.reshape(heads, hd, hd)
+    return jnp.concatenate([state.astype(jnp.bfloat16).reshape(heads, hd * hd), rate_row], axis=1)
+
+
+def unpack(payload, hd):
+    heads = payload.shape[0]
+    state = payload[:, : hd * hd].astype(jnp.float32).reshape(heads, hd, hd)
+    rate = payload[:, hd * hd].astype(jnp.float32) + payload[:, hd * hd + 1].astype(jnp.float32)
+    return rate, state
+
+
+def carried_state(last, summary, axis):
+    length = lax.axis_size(axis)
+    hd = summary.shape[1]
+    incl_r, incl_s = last, summary
+    excl_r, excl_s = jnp.zeros_like(last), jnp.zeros_like(summary)
+    shift = 1
+    while shift < length:
+        pairs = [(i, i + shift) for i in range(length - shift)]
+        in_r, in_s = unpack(lax.ppermute(pack(incl_r, incl_s), axis, pairs), hd)
+        excl_s = jnp.exp(excl_r)[:, None, None] * in_s + excl_s
+        excl_r = in_r + excl_r
+        if 2 * shift < length:
+            incl_s = jnp.exp(incl_r)[:, None, None] * in_s + incl_s
+            incl_r = in_r + incl_r
+        shift *= 2
+    return excl_s
 
 
 def slot_table(chosen_specialist_index, capacity, local_experts, experts):

time: 425 us -> 402 us (0.946)
  waiting for transfers between devices: 292 us -> 256 us
  starting transfers between devices: 5.92 us -> 28.2 us
  local copies, waits for them, and re-layouts: 27.1 us -> 22.4 us
  matrix products: 59.4 us -> 54.8 us
    all_gather x1 -> x0, waiting for transfers between devices: 49.2 us -> none  [carried_state(): everything = lax.all_gather(payload, axis)]
    ppermute x0 -> x4, starting transfers between devices: none -> 22.2 us  [carried_state(): in_r, in_s = unpack(lax.ppermute(pack(incl_r, incl_s), axis, pairs), hd)]
    ppermute x0 -> x4, waiting for transfers between devices: none -> 11.7 us  [carried_state(): in_r, in_s = unpack(lax.ppermute(pack(incl_r, incl_s), axis, pairs), hd)]
    dot_general x1 -> x0, matrix products: 8.22 us -> none  [carried_state(): jnp.einsum('kh,khx->hx', weight, states, precision=lax.Precision.HIGHEST)]
    slice x2 -> x3, local copies, waits for them, and re-layouts: 5.45 us -> 0.22 us  [unpack(): payload[:, hd * hd].astype(jnp.float32)]
    unnamed x22 -> x29, local copies, waits for them, and re-layouts: 14 us -> 14.9 us
  transfers between devices with their start and end apart: 5 -> 8, of which waited for: 5 -> 7; matrix products, arithmetic and copies ran while one was open for 5% -> 5% of each run, Pallas kernels for 0% -> 0%
where the time goes in v6:
time: 402 us; the launch traced here: 401 us
  waiting for transfers between devices  256 us (64%)
  matrix products  54.8 us (14%)
  starting transfers between devices  28.2 us (7%)
  local copies, waits for them, and re-layouts  22.4 us (6%)
  blocking collectives  20.6 us (5%)
  between operations  13.5 us (3%)
  other arithmetic  6.29 us (2%)
    reduce_scatter x1, waiting for transfers between devices, on_device(): lax.psum_scatter(jnp.einsum('ref,efd->red', acts, w_down, preferred_eleme...  105 us
    all_gather x1, waiting for transfers between devices, on_device(): piece = lax.all_gather(arrived, 'ctx', axis=0, tiled=True)  91.7 us
    reduce_scatter x1, waiting for transfers between devices, on_device(): lax.psum_scatter(jnp.dot(normed, out_proj, preferred_element_type=jnp.flo...  32.9 us
    ppermute x4, starting transfers between devices, carried_state(): in_r, in_s = unpack(lax.ppermute(pack(incl_r, incl_s), axis, pairs), hd)  22.2 us
    all_to_all x1, blocking collectives, on_device(): lax.all_to_all(packed, 'exp', split_axis=0, concat_axis=1, tiled=True)  20.6 us
    dot_general x1, matrix products, on_device(): jnp.einsum('red,edf->ref', piece, jnp.concatenate([w_gate, w_up], axis=2)...  19.2 us
    dot_general x1, matrix products, on_device(): jnp.einsum('ref,efd->red', acts, w_down, preferred_element_type=jnp.float32)  15.4 us
    unnamed x29, local copies, waits for them, and re-layouts  14.9 us
  transfers between devices with their start and end apart: 8, of which 7 were waited for; matrix products, arithmetic and copies ran while one was open for 5% of the time, Pallas kernels for 0%

profile of v6, /device:TPU:1, one launch (start us, length us, event | category | flops | bytes accessed | tf_op | source)
XLA Modules:
  0.0 401.4 jit_solution(10296518142198233179)
XLA Ops:
  8.1 1.5 copy.147
  9.6 2.1 fusion.16
  12.0 4.0 collective-permute-start
  16.0 5.0 %collective-permute-done = bf16[8,16512]{1,0:T(8,128)(2,1)S(1)} collective-permute-done((bf16[8,16512]{1,0:T(8,128)(2,1)S(1)}, bf16[8,16512]{1,0:T(8,128)(2,1)S(1)}, u32[]{:S(2)}, u32[]{:S(2)}) %collective-permute-start) | collective-permute-done | bytes 264224 | tf_op jit(solution)/shard_map/ppermute | solution.py:35
  21.8 5.6 %collective-permute-start.1 = (bf16[8,16512]{1,0:T(8,128)(2,1)S(1)}, bf16[8,16512]{1,0:T(8,128)(2,1)S(1)}, u32[]{:S(2)}, u32[]{:S(2)}) collective-permute-start(bf16[8,16512]{1,0:T(8,128)(2,1)S(1)} %pad_maximum_fusion.1), channel_id=1, source_target_pairs={{0,16},{8,24},{16,32},{24,40},{32,48},{40,56},{48,64},{56,72},{64,... | collective-permute-start | bytes 792584 | tf_op jit(solution)/shard_map/ppermute | solution.py:35
  27.4 4.1 %collective-permute-done.1 = bf16[8,16512]{1,0:T(8,128)(2,1)S(1)} collective-permute-done((bf16[8,16512]{1,0:T(8,128)(2,1)S(1)}, bf16[8,16512]{1,0:T(8,128)(2,1)S(1)}, u32[]{:S(2)}, u32[]{:S(2)}) %collective-permute-start.1) | collective-permute-done | bytes 264224 | tf_op jit(solution)/shard_map/ppermute | solution.py:35
  32.5 7.2 %collective-permute-start.2 = (bf16[8,16512]{1,0:T(8,128)(2,1)S(1)}, bf16[8,16512]{1,0:T(8,128)(2,1)S(1)}, u32[]{:S(2)}, u32[]{:S(2)}) collective-permute-start(bf16[8,16512]{1,0:T(8,128)(2,1)S(1)} %pad_maximum_fusion.2), channel_id=1, source_target_pairs={{0,32},{8,40},{16,48},{24,56},{32,64},{40,72},{48,80},{56,88},{64,... | collective-permute-start | bytes 792584 | tf_op jit(solution)/shard_map/ppermute | solution.py:35
  40.5 2.5 collective-permute-done.2
  43.9 5.4 %collective-permute-start.3 = (bf16[8,16512]{1,0:T(8,128)(2,1)S(1)}, bf16[8,16512]{1,0:T(8,128)(2,1)S(1)}, u32[]{:S(2)}, u32[]{:S(2)}) collective-permute-start(bf16[8,16512]{1,0:T(8,128)(2,1)S(1)} %pad_maximum_fusion.3), channel_id=1, source_target_pairs={{0,64},{8,72},{16,80},{24,88},{32,96},{40,104},{48,112},{56,120},{... | collective-permute-start | bytes 792584 | tf_op jit(solution)/shard_map/ppermute | solution.py:35
  49.3 6.6 %fusion.8 = f32[8,512,128]{1,2,0:T(8,128)} fusion(f32[8,512]{1,0:T(8,128)S(1)} %bitcast.207, pred[512,512]{1,0:T(8,128)(4,1)} %iota_compare_fusion, bf16[512,8,128]{0,2,1:T(8,128)(2,1)} %bitcast.202, bf16[512,1024]{1,0:T(8,128)(2,1)} %param.13, bf16[512,1024]{1,0:T(8,128)(2,1)S(1)} %copy-done), kind=kOutput, calls=%fused_computation.9 | convolution fusion | flops 1084227584 | bytes 5521408 | tf_op jit(solution)/shard_map/hts,shd->thd/dot_general | solution.py:91
  56.0 3.5 multiply_reduce_fusion
  59.9 4.9 %convolution_convert_fusion.1 = bf16[512,3072]{1,0:T(8,128)(2,1)} fusion(bf16[512,1024]{0,1:T(8,128)(2,1)S(1)} %bitcast.200, bf16[1024,3072]{1,0:T(8,128)(2,1)S(1)} %bitcast.209), kind=kOutput, calls=%fused_computation.8 | convolution fusion | flops 3222798336 | bytes 10485760 | tf_op jit(solution)/shard_map/dot_general | solution.py:109
  66.1 32.9 %reduce-scatter.3.cloned.1.call-done = bf16[64,3072]{1,0:T(8,128)(2,1)} async-done(((bf16[512,3072]{1,0:T(8,128)(2,1)}), bf16[64,3072]{1,0:T(8,128)(2,1)}) %reduce-scatter.3.cloned.1.call-update) | async-done | bytes 393232 | tf_op jit(solution)/shard_map/reduce_scatter | solution.py:108
  102.1 20.6 %all_to_all.14 = bf16[8,10,2,3072]{3,2,1,0:T(2,128)(2,1)S(1)} all-to-all(bf16[8,10,2,3072]{3,2,1,0:T(2,128)(2,1)S(1)} %reshape.351), channel_id=1, replica_groups=mesh['ctx'=16,'exp'=8] {'exp'}, dimensions={0} | all-to-all | bytes 1966080 | tf_op jit(solution)/shard_map/all_to_all | solution.py:130
  123.9 6.6 %copy.134 = bf16[2,3072,384]{1,2,0:T(8,128)(2,1)} copy(bf16[2,3072,384]{2,1,0:T(8,128)(2,1)} %param.19) | data formatting | bytes 9437184 | tf_op args[8]
  130.6 6.8 %copy.135 = bf16[2,3072,384]{1,2,0:T(8,128)(2,1)} copy(bf16[2,3072,384]{2,1,0:T(8,128)(2,1)} %param.20) | data formatting | bytes 9437184 | tf_op args[9]
  137.4 91.7 %all-gather.2.cloned.1.call-done = bf16[1280,2,3072]{2,0,1:T(8,128)(2,1)} async-done(((bf16[80,2,3072]{2,0,1:T(8,128)(2,1)}), bf16[1280,2,3072]{2,0,1:T(8,128)(2,1)}) %all-gather.2.cloned.1.call-update) | async-done | bytes 15728656 | tf_op jit(solution)/shard_map/all_gather | solution.py:133
  229.1 19.2 %fusion.5 = f32[1280,2,768]{0,2,1:T(8,128)} fusion(bf16[1280,2,3072]{2,0,1:T(8,128)(2,1)} %all-gather.2.cloned.1.call-done, bf16[2,3072,384]{1,2,0:T(8,128)(2,1)} %copy.135, bf16[2,3072,384]{1,2,0:T(8,128)(2,1)} %copy.134), kind=kOutput, calls=%fused_computation.7 | convolution fusion | flops 12098469888 | bytes 33030144 | tf_op jit(solution)/shard_map/red,edf->ref/dot_general | solution.py:135
  248.3 15.4 %fusion = bf16[1280,2,3072]{2,0,1:T(8,128)(2,1)} fusion(bf16[2,384,3072]{2,1,0:T(8,128)(2,1)} %param.21, f32[1280,2,768]{0,2,1:T(8,128)} %fusion.5), kind=kOutput, calls=%fused_computation.1 | convolution fusion | flops 6053560320 | bytes 28311552 | tf_op jit(solution)/shard_map/ref,efd->red/dot_general | solution.py:145
  263.7 105.0 %reduce-scatter.5.cloned.1.call-done = bf16[80,2,3072]{2,0,1:T(8,128)(2,1)} async-done(((bf16[1280,2,3072]{2,0,1:T(8,128)(2,1)}), bf16[80,2,3072]{2,0,1:T(8,128)(2,1)}) %reduce-scatter.5.cloned.1.call-update) | async-done | bytes 983056 | tf_op jit(solution)/shard_map/reduce_scatter | solution.py:144
  368.7 3.3 copy.138
  372.0 5.8 %all-to-all-start.1 = ((bf16[8,10,2,3072]{3,2,1,0:T(2,128)(2,1)}), bf16[8,10,2,3072]{3,2,1,0:T(2,128)(2,1)S(1)}, u32[]{:S(2)}, u32[]{:S(2)}) async-start(bf16[8,10,2,3072]{3,2,1,0:T(2,128)(2,1)} %bitcast.18), calls=%async_computation.3 | async-start | bytes 1966080 | tf_op jit(solution)/shard_map/all_to_all | solution.py:153
  377.8 14.3 %all-to-all-done.1 = bf16[8,10,2,3072]{3,2,1,0:T(2,128)(2,1)S(1)} async-done(((bf16[8,10,2,3072]{3,2,1,0:T(2,128)(2,1)}), bf16[8,10,2,3072]{3,2,1,0:T(2,128)(2,1)S(1)}, u32[]{:S(2)}, u32[]{:S(2)}) %all-to-all-start.1) | async-done | bytes 983072 | tf_op jit(solution)/shard_map/all_to_all | solution.py:153
  392.8 2.0 fusion.31
  (86 shorter events, 11.8 us)
Async XLA Ops:
  6.5 42.8 %copy-start = (bf16[512,1024]{1,0:T(8,128)(2,1)S(1)}, bf16[512,1024]{1,0:T(8,128)(2,1)}, u32[]{:S(2)}) copy-start(bf16[512,1024]{1,0:T(8,128)(2,1)} %param.11) | copy-start | bytes 3145732
  6.5 92.5 %reduce-scatter.3.cloned.1.call-start = ((), (), s32[]{:S(2)}) async-start(), calls=%async_computation.4 | async-start | bytes 3538944 | tf_op jit(solution)/shard_map/reduce_scatter | solution.py:108
  9.6 22.2 %copy-start.3 = (bf16[512,1024]{0,1:T(8,128)(2,1)}, bf16[512,1024]{0,1:T(8,128)(2,1)S(1)}, u32[]{:S(2)}) copy-start(bf16[512,1024]{0,1:T(8,128)(2,1)S(1)} %copy.147) | copy-start | bytes 3145732
  12.0 9.0 %collective-permute-start = (bf16[8,16512]{1,0:T(8,128)(2,1)S(1)}, bf16[8,16512]{1,0:T(8,128)(2,1)S(1)}, u32[]{:S(2)}, u32[]{:S(2)}) collective-permute-start(bf16[8,16512]{1,0:T(8,128)(2,1)S(1)} %pad_maximum_fusion), channel_id=1, source_target_pairs={{0,8},{8,16},{16,24},{24,32},{32,40},{40,48},{48,56},{56,64},{64,7... | collective-permute-start | bytes 792584 | tf_op jit(solution)/shard_map/ppermute | solution.py:35
  21.8 9.8 %collective-permute-start.1 = (bf16[8,16512]{1,0:T(8,128)(2,1)S(1)}, bf16[8,16512]{1,0:T(8,128)(2,1)S(1)}, u32[]{:S(2)}, u32[]{:S(2)}) collective-permute-start(bf16[8,16512]{1,0:T(8,128)(2,1)S(1)} %pad_maximum_fusion.1), channel_id=1, source_target_pairs={{0,16},{8,24},{16,32},{24,40},{32,48},{40,56},{48,64},{56,72},{64,... | collective-permute-start | bytes 792584 | tf_op jit(solution)/shard_map/ppermute | solution.py:35
  32.5 10.5 %collective-permute-start.2 = (bf16[8,16512]{1,0:T(8,128)(2,1)S(1)}, bf16[8,16512]{1,0:T(8,128)(2,1)S(1)}, u32[]{:S(2)}, u32[]{:S(2)}) collective-permute-start(bf16[8,16512]{1,0:T(8,128)(2,1)S(1)} %pad_maximum_fusion.2), channel_id=1, source_target_pairs={{0,32},{8,40},{16,48},{24,56},{32,64},{40,72},{48,80},{56,88},{64,... | collective-permute-start | bytes 792584 | tf_op jit(solution)/shard_map/ppermute | solution.py:35
  43.9 12.1 %collective-permute-start.3 = (bf16[8,16512]{1,0:T(8,128)(2,1)S(1)}, bf16[8,16512]{1,0:T(8,128)(2,1)S(1)}, u32[]{:S(2)}, u32[]{:S(2)}) collective-permute-start(bf16[8,16512]{1,0:T(8,128)(2,1)S(1)} %pad_maximum_fusion.3), channel_id=1, source_target_pairs={{0,64},{8,72},{16,80},{24,88},{32,96},{40,104},{48,112},{56,120},{... | collective-permute-start | bytes 792584 | tf_op jit(solution)/shard_map/ppermute | solution.py:35
  55.9 3.9 slice-start
  56.0 3.8 slice-start.1
  59.8 5.2 %copy-start.4 = (s32[64,2]{0,1:T(2,128)S(1)}, s32[64,2]{0,1:T(2,128)}, u32[]{:S(2)}) copy-start(s32[64,2]{0,1:T(2,128)} %param.17) | copy-start | bytes 1540
  59.9 39.2 %copy-start.2 = (bf16[64,3072]{1,0:T(8,128)(2,1)S(1)}, bf16[64,3072]{1,0:T(8,128)(2,1)}, u32[]{:S(2)}) copy-start(bf16[64,3072]{1,0:T(8,128)(2,1)} %param.15) | copy-start | bytes 1179652
  64.8 164.3 %all-gather.2.cloned.1.call-start = ((), (), s32[]{:S(2)}) async-start(), calls=%async_computation.5 | async-start | bytes 16711680 | tf_op jit(solution)/shard_map/all_gather | solution.py:133
  123.9 244.9 %reduce-scatter.5.cloned.1.call-start = ((), (), s32[]{:S(2)}) async-start(), calls=%async_computation.6 | async-start | bytes 16711680 | tf_op jit(solution)/shard_map/reduce_scatter | solution.py:144
  263.7 114.1 %copy-start.5 = (f32[64,2]{0,1:T(2,128)S(1)}, f32[64,2]{0,1:T(2,128)}, u32[]{:S(2)}) copy-start(f32[64,2]{0,1:T(2,128)} %param.18) | copy-start | bytes 1540
  368.7 26.1 %copy-start.1 = (bf16[512,1024]{1,0:T(8,128)(2,1)S(1)}, bf16[512,1024]{1,0:T(8,128)(2,1)}, u32[]{:S(2)}) copy-start(bf16[512,1024]{1,0:T(8,128)(2,1)} %param.11) | copy-start | bytes 3145732
  372.0 20.0 %all-to-all-start.1 = ((bf16[8,10,2,3072]{3,2,1,0:T(2,128)(2,1)}), bf16[8,10,2,3072]{3,2,1,0:T(2,128)(2,1)S(1)}, u32[]{:S(2)}, u32[]{:S(2)}) async-start(bf16[8,10,2,3072]{3,2,1,0:T(2,128)(2,1)} %bitcast.18), calls=%async_computation.3 | async-start | bytes 1966080 | tf_op jit(solution)/shard_map/all_to_all | solution.py:153
Sparse Core Ops, SparseCore 0:
  64.9 34.0 reduce-scatter.2
  124.0 105.0 all-gather.1
  263.9 104.8 reduce-scatter.4

commit v7 on v6

--- a/solution.py
+++ b/solution.py
@@ -24,22 +24,31 @@
     return rate, state
 
 
+def combine(earlier, later):
+    return (earlier[0] + later[0], jnp.exp(later[0])[:, None, None] * earlier[1] + later[1])
+
+
 def carried_state(last, summary, axis):
     length = lax.axis_size(axis)
     hd = summary.shape[1]
-    incl_r, incl_s = last, summary
-    excl_r, excl_s = jnp.zeros_like(last), jnp.zeros_like(summary)
+    incl = (last, summary)
+    excl = (jnp.zeros_like(last), jnp.zeros_like(summary))
     shift = 1
     while shift < length:
-        pairs = [(i, i + shift) for i in range(length - shift)]
-        in_r, in_s = unpack(lax.ppermute(pack(incl_r, incl_s), axis, pairs), hd)
-        excl_s = jnp.exp(excl_r)[:, None, None] * in_s + excl_s
-        excl_r = in_r + excl_r
-        if 2 * shift < length:
-            incl_s = jnp.exp(incl_r)[:, None, None] * in_s + incl_s
-            incl_r = in_r + incl_r
-        shift *= 2
-    return excl_s
+        sent = pack(*incl)
+        arrived = []
+        for k in range(1, 4):
+            if k * shift < length:
+                pairs = [(i, i + k * shift) for i in range(length - k * shift)]
+                arrived.append(unpack(lax.ppermute(sent, axis, pairs), hd))
+        before = arrived[-1]
+        for part in reversed(arrived[:-1]):
+            before = combine(before, part)
+        excl = combine(before, excl)
+        if 4 * shift < length:
+            incl = combine(before, incl)
+        shift *= 4
+    return excl[1]
 
 
 def slot_table(chosen_specialist_index, capacity, local_experts, experts):

time: 402 us -> 408 us (1.015)
    ppermute x4 -> x6, waiting for transfers between devices: 11.7 us -> 15.6 us  [carried_state(): arrived.append(unpack(lax.ppermute(sent, axis, pairs), hd))]
    ppermute x4 -> x6, starting transfers between devices: 22.2 us -> 24.9 us  [carried_state(): arrived.append(unpack(lax.ppermute(sent, axis, pairs), hd))]
    unnamed x29 -> x27, local copies, waits for them, and re-layouts: 14.9 us -> 14.6 us
  transfers between devices with their start and end apart: 8 -> 10, of which waited for: 7 -> 8; matrix products, arithmetic and copies ran while one was open for 5% -> 5% of each run, Pallas kernels for 0% -> 0%
where the time goes in v7:
time: 408 us; the launch traced here: 407 us
  waiting for transfers between devices  259 us (63%)
  matrix products  52.8 us (13%)
  starting transfers between devices  30.9 us (8%)
  local copies, waits for them, and re-layouts  22 us (5%)
  blocking collectives  20.6 us (5%)
  between operations  13.5 us (3%)
  other arithmetic  8.52 us (2%)
    reduce_scatter x1, waiting for transfers between devices, on_device(): lax.psum_scatter(jnp.einsum('ref,efd->red', acts, w_down, preferred_eleme...  105 us
    all_gather x1, waiting for transfers between devices, on_device(): piece = lax.all_gather(arrived, 'ctx', axis=0, tiled=True)  91.5 us
    reduce_scatter x1, waiting for transfers between devices, on_device(): lax.psum_scatter(jnp.dot(normed, out_proj, preferred_element_type=jnp.flo...  32.1 us
    ppermute x6, starting transfers between devices, carried_state(): arrived.append(unpack(lax.ppermute(sent, axis, pairs), hd))  24.9 us
    all_to_all x1, blocking collectives, on_device(): lax.all_to_all(packed, 'exp', split_axis=0, concat_axis=1, tiled=True)  20.6 us
    dot_general x1, matrix products, on_device(): jnp.einsum('red,edf->ref', piece, jnp.concatenate([w_gate, w_up], axis=2)...  19.2 us
    ppermute x6, waiting for transfers between devices, carried_state(): arrived.append(unpack(lax.ppermute(sent, axis, pairs), hd))  15.6 us
    dot_general x1, matrix products, on_device(): jnp.einsum('ref,efd->red', acts, w_down, preferred_element_type=jnp.float32)  15.4 us
  transfers between devices with their start and end apart: 10, of which 8 were waited for; matrix products, arithmetic and copies ran while one was open for 5% of the time, Pallas kernels for 0%

profile of v7, /device:TPU:1, one launch (start us, length us, event | category | flops | bytes accessed | tf_op | source)
XLA Modules:
  0.0 406.9 jit_solution(15935309267503597026)
XLA Ops:
  9.6 2.1 fusion.16
  12.7 5.2 %collective-permute-start = (bf16[8,16512]{1,0:T(8,128)(2,1)}, bf16[8,16512]{1,0:T(8,128)(2,1)S(1)}, u32[]{:S(2)}, u32[]{:S(2)}) collective-permute-start(bf16[8,16512]{1,0:T(8,128)(2,1)} %pad_maximum_fusion), channel_id=1, source_target_pairs={{0,24},{8,32},{16,40},{24,48},{32,56},{40,64},{48,72},{56,80},{64,... | collective-permute-start | bytes 792584 | tf_op jit(solution)/shard_map/ppermute | solution.py:43
  17.9 3.5 collective-permute-start.1
  21.4 2.5 collective-permute-start.2
  26.7 5.4 %collective-permute-done.2 = bf16[8,16512]{1,0:T(8,128)(2,1)S(1)} collective-permute-done((bf16[8,16512]{1,0:T(8,128)(2,1)}, bf16[8,16512]{1,0:T(8,128)(2,1)S(1)}, u32[]{:S(2)}, u32[]{:S(2)}) %collective-permute-start.2) | collective-permute-done | bytes 264224 | tf_op jit(solution)/shard_map/ppermute | solution.py:43
  34.8 7.9 %collective-permute-start.3 = (bf16[8,16512]{1,0:T(8,128)(2,1)}, bf16[8,16512]{1,0:T(8,128)(2,1)S(1)}, u32[]{:S(2)}, u32[]{:S(2)}) collective-permute-start(bf16[8,16512]{1,0:T(8,128)(2,1)} %pad_maximum_fusion.1), channel_id=1, source_target_pairs={{0,32},{8,40},{16,48},{24,56},{32,64},{40,72},{48,80},{56,88},{64,... | collective-permute-start | bytes 792584 | tf_op jit(solution)/shard_map/ppermute | solution.py:43
  42.7 5.3 %fusion.8 = f32[8,512,128]{1,2,0:T(8,128)S(1)} fusion(f32[8,512]{1,0:T(8,128)S(1)} %bitcast.158, pred[512,512]{1,0:T(8,128)(4,1)} %iota_compare_fusion, bf16[512,8,128]{0,2,1:T(8,128)(2,1)} %bitcast.155, bf16[512,1024]{1,0:T(8,128)(2,1)} %param.13, bf16[512,1024]{1,0:T(8,128)(2,1)S(1)} %copy-done), kind=kOutput, calls=%fused_computation.9 | convolution fusion | flops 1084227584 | bytes 5521408 | tf_op jit(solution)/shard_map/hts,shd->thd/dot_general | solution.py:100
  48.0 4.5 %collective-permute-start.4 = (bf16[8,16512]{1,0:T(8,128)(2,1)}, bf16[8,16512]{1,0:T(8,128)(2,1)S(1)}, u32[]{:S(2)}, u32[]{:S(2)}) collective-permute-start(bf16[8,16512]{1,0:T(8,128)(2,1)} %pad_maximum_fusion.1), channel_id=1, source_target_pairs={{0,64},{8,72},{16,80},{24,88},{32,96},{40,104},{48,112},{56,120},{... | collective-permute-start | bytes 792584 | tf_op jit(solution)/shard_map/ppermute | solution.py:43
  54.1 3.6 collective-permute-done.4
  57.9 5.1 %collective-permute-done.5 = bf16[8,16512]{1,0:T(8,128)(2,1)S(1)} collective-permute-done((bf16[8,16512]{1,0:T(8,128)(2,1)}, bf16[8,16512]{1,0:T(8,128)(2,1)S(1)}, u32[]{:S(2)}, u32[]{:S(2)}) %collective-permute-start.5) | collective-permute-done | bytes 264224 | tf_op jit(solution)/shard_map/ppermute | solution.py:43
  63.1 2.8 multiply_reduce_fusion
  66.3 5.0 %convolution_convert_fusion.1 = bf16[512,3072]{1,0:T(8,128)(2,1)} fusion(bf16[512,1024]{0,1:T(8,128)(2,1)S(1)} %bitcast.153, bf16[1024,3072]{1,0:T(8,128)(2,1)S(1)} %bitcast.160), kind=kOutput, calls=%fused_computation.8 | convolution fusion | flops 3222798336 | bytes 10485760 | tf_op jit(solution)/shard_map/dot_general | solution.py:118
  72.4 32.1 %reduce-scatter.3.cloned.1.call-done = bf16[64,3072]{1,0:T(8,128)(2,1)} async-done(((bf16[512,3072]{1,0:T(8,128)(2,1)}), bf16[64,3072]{1,0:T(8,128)(2,1)}) %reduce-scatter.3.cloned.1.call-update) | async-done | bytes 393232 | tf_op jit(solution)/shard_map/reduce_scatter | solution.py:117
  107.7 20.6 %all_to_all.14 = bf16[8,10,2,3072]{3,2,1,0:T(2,128)(2,1)S(1)} all-to-all(bf16[8,10,2,3072]{3,2,1,0:T(2,128)(2,1)S(1)} %reshape.356), channel_id=1, replica_groups=mesh['ctx'=16,'exp'=8] {'exp'}, dimensions={0} | all-to-all | bytes 1966080 | tf_op jit(solution)/shard_map/all_to_all | solution.py:139
  129.7 6.6 %copy.163 = bf16[2,3072,384]{1,2,0:T(8,128)(2,1)} copy(bf16[2,3072,384]{2,1,0:T(8,128)(2,1)} %param.19) | data formatting | bytes 9437184 | tf_op args[8]
  136.3 6.9 %copy.164 = bf16[2,3072,384]{1,2,0:T(8,128)(2,1)} copy(bf16[2,3072,384]{2,1,0:T(8,128)(2,1)} %param.20) | data formatting | bytes 9437184 | tf_op args[9]
  143.2 91.5 %all-gather.2.cloned.1.call-done = bf16[1280,2,3072]{2,0,1:T(8,128)(2,1)} async-done(((bf16[80,2,3072]{2,0,1:T(8,128)(2,1)}), bf16[1280,2,3072]{2,0,1:T(8,128)(2,1)}) %all-gather.2.cloned.1.call-update) | async-done | bytes 15728656 | tf_op jit(solution)/shard_map/all_gather | solution.py:142
  234.6 19.2 %fusion.5 = f32[1280,2,768]{0,2,1:T(8,128)} fusion(bf16[1280,2,3072]{2,0,1:T(8,128)(2,1)} %all-gather.2.cloned.1.call-done, bf16[2,3072,384]{1,2,0:T(8,128)(2,1)} %copy.164, bf16[2,3072,384]{1,2,0:T(8,128)(2,1)} %copy.163), kind=kOutput, calls=%fused_computation.7 | convolution fusion | flops 12098469888 | bytes 33030144 | tf_op jit(solution)/shard_map/red,edf->ref/dot_general | solution.py:144
  253.8 15.4 %fusion = bf16[1280,2,3072]{2,0,1:T(8,128)(2,1)} fusion(bf16[2,384,3072]{2,1,0:T(8,128)(2,1)} %param.21, f32[1280,2,768]{0,2,1:T(8,128)} %fusion.5), kind=kOutput, calls=%fused_computation.1 | convolution fusion | flops 6053560320 | bytes 28311552 | tf_op jit(solution)/shard_map/ref,efd->red/dot_general | solution.py:154
  269.3 105.0 %reduce-scatter.5.cloned.1.call-done = bf16[80,2,3072]{2,0,1:T(8,128)(2,1)} async-done(((bf16[1280,2,3072]{2,0,1:T(8,128)(2,1)}), bf16[80,2,3072]{2,0,1:T(8,128)(2,1)}) %reduce-scatter.5.cloned.1.call-update) | async-done | bytes 983056 | tf_op jit(solution)/shard_map/reduce_scatter | solution.py:153
  374.2 3.2 copy.167
  377.5 5.8 %all-to-all-start.1 = ((bf16[8,10,2,3072]{3,2,1,0:T(2,128)(2,1)}), bf16[8,10,2,3072]{3,2,1,0:T(2,128)(2,1)S(1)}, u32[]{:S(2)}, u32[]{:S(2)}) async-start(bf16[8,10,2,3072]{3,2,1,0:T(2,128)(2,1)} %bitcast.14), calls=%async_computation.3 | async-start | bytes 1966080 | tf_op jit(solution)/shard_map/all_to_all | solution.py:162
  383.3 14.3 %all-to-all-done.1 = bf16[8,10,2,3072]{3,2,1,0:T(2,128)(2,1)S(1)} async-done(((bf16[8,10,2,3072]{3,2,1,0:T(2,128)(2,1)}), bf16[8,10,2,3072]{3,2,1,0:T(2,128)(2,1)S(1)}, u32[]{:S(2)}, u32[]{:S(2)}) %all-to-all-start.1) | async-done | bytes 983072 | tf_op jit(solution)/shard_map/all_to_all | solution.py:162
  398.3 2.0 fusion.31
  (81 shorter events, 18.0 us)
Async XLA Ops:
  6.5 36.1 %copy-start = (bf16[512,1024]{1,0:T(8,128)(2,1)S(1)}, bf16[512,1024]{1,0:T(8,128)(2,1)}, u32[]{:S(2)}) copy-start(bf16[512,1024]{1,0:T(8,128)(2,1)} %param.11) | copy-start | bytes 3145732
  6.5 98.0 %reduce-scatter.3.cloned.1.call-start = ((), (), s32[]{:S(2)}) async-start(), calls=%async_computation.4 | async-start | bytes 3538944 | tf_op jit(solution)/shard_map/reduce_scatter | solution.py:117
  9.6 24.2 %copy-start.3 = (bf16[512,1024]{0,1:T(8,128)(2,1)}, bf16[512,1024]{0,1:T(8,128)(2,1)S(1)}, u32[]{:S(2)}) copy-start(bf16[512,1024]{0,1:T(8,128)(2,1)S(1)} %copy.176) | copy-start | bytes 3145732
  12.7 12.0 %collective-permute-start = (bf16[8,16512]{1,0:T(8,128)(2,1)}, bf16[8,16512]{1,0:T(8,128)(2,1)S(1)}, u32[]{:S(2)}, u32[]{:S(2)}) collective-permute-start(bf16[8,16512]{1,0:T(8,128)(2,1)} %pad_maximum_fusion), channel_id=1, source_target_pairs={{0,24},{8,32},{16,40},{24,48},{32,56},{40,64},{48,72},{56,80},{64,... | collective-permute-start | bytes 792584 | tf_op jit(solution)/shard_map/ppermute | solution.py:43
  17.9 8.5 %collective-permute-start.1 = (bf16[8,16512]{1,0:T(8,128)(2,1)}, bf16[8,16512]{1,0:T(8,128)(2,1)S(1)}, u32[]{:S(2)}, u32[]{:S(2)}) collective-permute-start(bf16[8,16512]{1,0:T(8,128)(2,1)} %pad_maximum_fusion), channel_id=1, source_target_pairs={{0,16},{8,24},{16,32},{24,40},{32,48},{40,56},{48,64},{56,72},{64,... | collective-permute-start | bytes 792584 | tf_op jit(solution)/shard_map/ppermute | solution.py:43
  21.4 10.7 %collective-permute-start.2 = (bf16[8,16512]{1,0:T(8,128)(2,1)}, bf16[8,16512]{1,0:T(8,128)(2,1)S(1)}, u32[]{:S(2)}, u32[]{:S(2)}) collective-permute-start(bf16[8,16512]{1,0:T(8,128)(2,1)} %pad_maximum_fusion), channel_id=1, source_target_pairs={{0,8},{8,16},{16,24},{24,32},{32,40},{40,48},{48,56},{56,64},{64,7... | collective-permute-start | bytes 792584 | tf_op jit(solution)/shard_map/ppermute | solution.py:43
  34.8 19.0 %collective-permute-start.3 = (bf16[8,16512]{1,0:T(8,128)(2,1)}, bf16[8,16512]{1,0:T(8,128)(2,1)S(1)}, u32[]{:S(2)}, u32[]{:S(2)}) collective-permute-start(bf16[8,16512]{1,0:T(8,128)(2,1)} %pad_maximum_fusion.1), channel_id=1, source_target_pairs={{0,32},{8,40},{16,48},{24,56},{32,64},{40,72},{48,80},{56,88},{64,... | collective-permute-start | bytes 792584 | tf_op jit(solution)/shard_map/ppermute | solution.py:43
  48.0 9.7 %collective-permute-start.4 = (bf16[8,16512]{1,0:T(8,128)(2,1)}, bf16[8,16512]{1,0:T(8,128)(2,1)S(1)}, u32[]{:S(2)}, u32[]{:S(2)}) collective-permute-start(bf16[8,16512]{1,0:T(8,128)(2,1)} %pad_maximum_fusion.1), channel_id=1, source_target_pairs={{0,64},{8,72},{16,80},{24,88},{32,96},{40,104},{48,112},{56,120},{... | collective-permute-start | bytes 792584 | tf_op jit(solution)/shard_map/ppermute | solution.py:43
  52.5 10.5 %collective-permute-start.5 = (bf16[8,16512]{1,0:T(8,128)(2,1)}, bf16[8,16512]{1,0:T(8,128)(2,1)S(1)}, u32[]{:S(2)}, u32[]{:S(2)}) collective-permute-start(bf16[8,16512]{1,0:T(8,128)(2,1)} %pad_maximum_fusion.1), channel_id=1, source_target_pairs={{0,96},{8,104},{16,112},{24,120},{1,97},{9,105},{17,113},{25,121},... | collective-permute-start | bytes 792584 | tf_op jit(solution)/shard_map/ppermute | solution.py:43
  63.0 3.2 slice-start
  63.1 3.2 slice-start.1
  66.3 5.1 %copy-start.4 = (s32[64,2]{0,1:T(2,128)S(1)}, s32[64,2]{0,1:T(2,128)}, u32[]{:S(2)}) copy-start(s32[64,2]{0,1:T(2,128)} %param.17) | copy-start | bytes 1540
  66.3 38.2 %copy-start.2 = (bf16[64,3072]{1,0:T(8,128)(2,1)S(1)}, bf16[64,3072]{1,0:T(8,128)(2,1)}, u32[]{:S(2)}) copy-start(bf16[64,3072]{1,0:T(8,128)(2,1)} %param.15) | copy-start | bytes 1179652
  71.3 163.4 %all-gather.2.cloned.1.call-start = ((), (), s32[]{:S(2)}) async-start(), calls=%async_computation.5 | async-start | bytes 16711680 | tf_op jit(solution)/shard_map/all_gather | solution.py:142
  129.4 244.8 %reduce-scatter.5.cloned.1.call-start = ((), (), s32[]{:S(2)}) async-start(), calls=%async_computation.6 | async-start | bytes 16711680 | tf_op jit(solution)/shard_map/reduce_scatter | solution.py:153
  269.2 114.1 %copy-start.5 = (f32[64,2]{0,1:T(2,128)S(1)}, f32[64,2]{0,1:T(2,128)}, u32[]{:S(2)}) copy-start(f32[64,2]{0,1:T(2,128)} %param.18) | copy-start | bytes 1540
  374.2 26.1 %copy-start.1 = (bf16[512,1024]{1,0:T(8,128)(2,1)S(1)}, bf16[512,1024]{1,0:T(8,128)(2,1)}, u32[]{:S(2)}) copy-start(bf16[512,1024]{1,0:T(8,128)(2,1)} %param.11) | copy-start | bytes 3145732
  377.5 20.1 %all-to-all-start.1 = ((bf16[8,10,2,3072]{3,2,1,0:T(2,128)(2,1)}), bf16[8,10,2,3072]{3,2,1,0:T(2,128)(2,1)S(1)}, u32[]{:S(2)}, u32[]{:S(2)}) async-start(bf16[8,10,2,3072]{3,2,1,0:T(2,128)(2,1)} %bitcast.14), calls=%async_computation.3 | async-start | bytes 1966080 | tf_op jit(solution)/shard_map/all_to_all | solution.py:162
Sparse Core Ops, SparseCore 0:
  71.4 33.0 reduce-scatter.2
  129.5 105.0 all-gather.1
  269.4 104.8 reduce-scatter.4

commit v8 on v6

--- a/solution.py
+++ b/solution.py
@@ -24,7 +24,7 @@
     return rate, state
 
 
-def carried_state(last, summary, axis):
+def carried_state(last, summary, axis, tied):
     length = lax.axis_size(axis)
     hd = summary.shape[1]
     incl_r, incl_s = last, summary
@@ -32,14 +32,17 @@
     shift = 1
     while shift < length:
         pairs = [(i, i + shift) for i in range(length - shift)]
-        in_r, in_s = unpack(lax.ppermute(pack(incl_r, incl_s), axis, pairs), hd)
+        sent = pack(incl_r, incl_s)
+        if shift == 2:
+            tied, sent = lax.optimization_barrier((tied, sent))
+        in_r, in_s = unpack(lax.ppermute(sent, axis, pairs), hd)
         excl_s = jnp.exp(excl_r)[:, None, None] * in_s + excl_s
         excl_r = in_r + excl_r
         if 2 * shift < length:
             incl_s = jnp.exp(incl_r)[:, None, None] * in_s + incl_s
             incl_r = in_r + incl_r
         shift *= 2
-    return excl_s
+    return excl_s, tied
 
 
 def slot_table(chosen_specialist_index, capacity, local_experts, experts):
@@ -94,7 +97,7 @@
         jnp.bfloat16
     )
     summary = jnp.einsum("thd,the->hde", scaled_keys, v_heads, preferred_element_type=jnp.float32)
-    carried = carried_state(last, summary, "ctx")
+    carried, intra = carried_state(last, summary, "ctx", intra)
     inter = jnp.exp(cum)[:, :, None] * jnp.einsum(
         "thd,hde->the", q_heads.astype(jnp.float32), carried, precision=lax.Precision.HIGHEST
     )

time: 402 us -> 405 us (level)
    unnamed x29 -> x25, local copies, waits for them, and re-layouts: 14.9 us -> 14.9 us
where the time goes in v8:
time: 405 us; the launch traced here: 404 us
  waiting for transfers between devices  259 us (64%)
  matrix products  55.3 us (14%)
  starting transfers between devices  26.2 us (6%)
  local copies, waits for them, and re-layouts  22.9 us (6%)
  blocking collectives  20.6 us (5%)
  between operations  13.4 us (3%)
  other arithmetic  6.7 us (2%)
    reduce_scatter x1, waiting for transfers between devices, on_device(): lax.psum_scatter(jnp.einsum('ref,efd->red', acts, w_down, preferred_eleme...  105 us
    all_gather x1, waiting for transfers between devices, on_device(): piece = lax.all_gather(arrived, 'ctx', axis=0, tiled=True)  91.7 us
    reduce_scatter x1, waiting for transfers between devices, on_device(): lax.psum_scatter(jnp.dot(normed, out_proj, preferred_element_type=jnp.flo...  36.7 us
    all_to_all x1, blocking collectives, on_device(): lax.all_to_all(packed, 'exp', split_axis=0, concat_axis=1, tiled=True)  20.6 us
    ppermute x4, starting transfers between devices, carried_state(): in_r, in_s = unpack(lax.ppermute(sent, axis, pairs), hd)  20.3 us
    dot_general x1, matrix products, on_device(): jnp.einsum('red,edf->ref', piece, jnp.concatenate([w_gate, w_up], axis=2)...  19.2 us
    dot_general x1, matrix products, on_device(): jnp.einsum('ref,efd->red', acts, w_down, preferred_element_type=jnp.float32)  15.4 us
    unnamed x25, local copies, waits for them, and re-layouts  14.9 us
  transfers between devices with their start and end apart: 8, of which 7 were waited for; matrix products, arithmetic and copies ran while one was open for 5% of the time, Pallas kernels for 0%

profile of v8, /device:TPU:1, one launch (start us, length us, event | category | flops | bytes accessed | tf_op | source)
XLA Modules:
  0.0 403.9 jit_solution(2120160553493721338)
XLA Ops:
  8.1 1.5 copy.157
  9.6 1.7 fusion.17
  11.6 3.9 collective-permute-start
  16.4 5.9 %fusion.16 = f32[512,8,128]{2,0,1:T(8,128)} fusion(f32[8,512]{1,0:T(8,128)S(1)} %bitcast.207, pred[512,512]{1,0:T(8,128)(4,1)} %iota_compare_fusion, bf16[512,8,128]{0,2,1:T(8,128)(2,1)S(1)} %bitcast.201, bf16[512,1024]{1,0:T(8,128)(2,1)} %param.13, bf16[512,1024]{1,0:T(8,128)(2,1)S(1)} %copy-done), kind=kOutput, calls=%fused_computation.21 | convolution fusion | flops 1084227584 | bytes 5521408 | tf_op jit(solution)/shard_map/hts,shd->thd/dot_general | solution.py:94
  23.1 4.4 %collective-permute-start.1 = (bf16[8,16512]{1,0:T(8,128)(2,1)S(1)}, bf16[8,16512]{1,0:T(8,128)(2,1)S(1)}, u32[]{:S(2)}, u32[]{:S(2)}) collective-permute-start(bf16[8,16512]{1,0:T(8,128)(2,1)S(1)} %pad_maximum_fusion.1), channel_id=1, source_target_pairs={{0,16},{8,24},{16,32},{24,40},{32,48},{40,56},{48,64},{56,72},{64,... | collective-permute-start | bytes 792584 | tf_op jit(solution)/shard_map/ppermute | solution.py:38
  27.4 4.5 %collective-permute-done.1 = bf16[8,16512]{1,0:T(8,128)(2,1)S(1)} collective-permute-done((bf16[8,16512]{1,0:T(8,128)(2,1)S(1)}, bf16[8,16512]{1,0:T(8,128)(2,1)S(1)}, u32[]{:S(2)}, u32[]{:S(2)}) %collective-permute-start.1) | collective-permute-done | bytes 264224 | tf_op jit(solution)/shard_map/ppermute | solution.py:38
  32.9 6.4 %collective-permute-start.2 = (bf16[8,16512]{1,0:T(8,128)(2,1)S(1)}, bf16[8,16512]{1,0:T(8,128)(2,1)S(1)}, u32[]{:S(2)}, u32[]{:S(2)}) collective-permute-start(bf16[8,16512]{1,0:T(8,128)(2,1)S(1)} %pad_maximum_fusion.2), channel_id=1, source_target_pairs={{0,32},{8,40},{16,48},{24,56},{32,64},{40,72},{48,80},{56,88},{64,... | collective-permute-start | bytes 792584 | tf_op jit(solution)/shard_map/ppermute | solution.py:38
  39.3 3.3 collective-permute-done.2
  43.5 5.6 %collective-permute-start.3 = (bf16[8,16512]{1,0:T(8,128)(2,1)S(1)}, bf16[8,16512]{1,0:T(8,128)(2,1)S(1)}, u32[]{:S(2)}, u32[]{:S(2)}) collective-permute-start(bf16[8,16512]{1,0:T(8,128)(2,1)S(1)} %pad_maximum_fusion.3), channel_id=1, source_target_pairs={{0,64},{8,72},{16,80},{24,88},{32,96},{40,104},{48,112},{56,120},{... | collective-permute-start | bytes 792584 | tf_op jit(solution)/shard_map/ppermute | solution.py:38
  49.0 3.3 collective-permute-done.3
  52.4 2.4 multiply_reduce_fusion
  56.1 7.7 %convolution_convert_fusion.1 = bf16[512,3072]{1,0:T(8,128)(2,1)} fusion(bf16[512,1024]{0,1:T(8,128)(2,1)S(1)} %bitcast.202, bf16[1024,3072]{1,0:T(8,128)(2,1)} %param.16), kind=kOutput, calls=%fused_computation.8 | convolution fusion | flops 3222798336 | bytes 10485760 | tf_op jit(solution)/shard_map/dot_general | solution.py:112
  64.9 36.7 %reduce-scatter.3.cloned.1.call-done = bf16[64,3072]{1,0:T(8,128)(2,1)} async-done(((bf16[512,3072]{1,0:T(8,128)(2,1)}), bf16[64,3072]{1,0:T(8,128)(2,1)}) %reduce-scatter.3.cloned.1.call-update) | async-done | bytes 393232 | tf_op jit(solution)/shard_map/reduce_scatter | solution.py:111
  104.7 20.6 %all_to_all.14 = bf16[8,10,2,3072]{3,2,1,0:T(2,128)(2,1)S(1)} all-to-all(bf16[8,10,2,3072]{3,2,1,0:T(2,128)(2,1)S(1)} %reshape.351), channel_id=1, replica_groups=mesh['ctx'=16,'exp'=8] {'exp'}, dimensions={0} | all-to-all | bytes 1966080 | tf_op jit(solution)/shard_map/all_to_all | solution.py:133
  126.4 6.7 %copy.143 = bf16[2,3072,384]{1,2,0:T(8,128)(2,1)} copy(bf16[2,3072,384]{2,1,0:T(8,128)(2,1)} %param.19) | data formatting | bytes 9437184 | tf_op args[8]
  133.1 6.8 %copy.144 = bf16[2,3072,384]{1,2,0:T(8,128)(2,1)} copy(bf16[2,3072,384]{2,1,0:T(8,128)(2,1)} %param.20) | data formatting | bytes 9437184 | tf_op args[9]
  140.0 91.7 %all-gather.2.cloned.1.call-done = bf16[1280,2,3072]{2,0,1:T(8,128)(2,1)} async-done(((bf16[80,2,3072]{2,0,1:T(8,128)(2,1)}), bf16[1280,2,3072]{2,0,1:T(8,128)(2,1)}) %all-gather.2.cloned.1.call-update) | async-done | bytes 15728656 | tf_op jit(solution)/shard_map/all_gather | solution.py:136
  231.7 19.2 %fusion.5 = f32[1280,2,768]{0,2,1:T(8,128)} fusion(bf16[1280,2,3072]{2,0,1:T(8,128)(2,1)} %all-gather.2.cloned.1.call-done, bf16[2,3072,384]{1,2,0:T(8,128)(2,1)} %copy.144, bf16[2,3072,384]{1,2,0:T(8,128)(2,1)} %copy.143), kind=kOutput, calls=%fused_computation.7 | convolution fusion | flops 12098469888 | bytes 33030144 | tf_op jit(solution)/shard_map/red,edf->ref/dot_general | solution.py:138
  250.8 15.4 %fusion = bf16[1280,2,3072]{2,0,1:T(8,128)(2,1)} fusion(bf16[2,384,3072]{2,1,0:T(8,128)(2,1)} %param.21, f32[1280,2,768]{0,2,1:T(8,128)} %fusion.5), kind=kOutput, calls=%fused_computation.1 | convolution fusion | flops 6053560320 | bytes 28311552 | tf_op jit(solution)/shard_map/ref,efd->red/dot_general | solution.py:148
  266.3 105.0 %reduce-scatter.5.cloned.1.call-done = bf16[80,2,3072]{2,0,1:T(8,128)(2,1)} async-done(((bf16[1280,2,3072]{2,0,1:T(8,128)(2,1)}), bf16[80,2,3072]{2,0,1:T(8,128)(2,1)}) %reduce-scatter.5.cloned.1.call-update) | async-done | bytes 983056 | tf_op jit(solution)/shard_map/reduce_scatter | solution.py:147
  371.3 3.3 copy.147
  374.5 5.8 %all-to-all-start.1 = ((bf16[8,10,2,3072]{3,2,1,0:T(2,128)(2,1)}), bf16[8,10,2,3072]{3,2,1,0:T(2,128)(2,1)S(1)}, u32[]{:S(2)}, u32[]{:S(2)}) async-start(bf16[8,10,2,3072]{3,2,1,0:T(2,128)(2,1)} %bitcast.18), calls=%async_computation.3 | async-start | bytes 1966080 | tf_op jit(solution)/shard_map/all_to_all | solution.py:156
  380.3 14.3 %all-to-all-done.1 = bf16[8,10,2,3072]{3,2,1,0:T(2,128)(2,1)S(1)} async-done(((bf16[8,10,2,3072]{3,2,1,0:T(2,128)(2,1)}), bf16[8,10,2,3072]{3,2,1,0:T(2,128)(2,1)S(1)}, u32[]{:S(2)}, u32[]{:S(2)}) %all-to-all-start.1) | async-done | bytes 983072 | tf_op jit(solution)/shard_map/all_to_all | solution.py:156
  395.4 2.0 fusion.32
  (82 shorter events, 12.6 us)
Async XLA Ops:
  6.5 9.8 %copy-start = (bf16[512,1024]{1,0:T(8,128)(2,1)S(1)}, bf16[512,1024]{1,0:T(8,128)(2,1)}, u32[]{:S(2)}) copy-start(bf16[512,1024]{1,0:T(8,128)(2,1)} %param.11) | copy-start | bytes 3145732
  6.5 95.0 %reduce-scatter.3.cloned.1.call-start = ((), (), s32[]{:S(2)}) async-start(), calls=%async_computation.4 | async-start | bytes 3538944 | tf_op jit(solution)/shard_map/reduce_scatter | solution.py:111
  11.6 10.6 %collective-permute-start = (bf16[8,16512]{1,0:T(8,128)(2,1)S(1)}, bf16[8,16512]{1,0:T(8,128)(2,1)S(1)}, u32[]{:S(2)}, u32[]{:S(2)}) collective-permute-start(bf16[8,16512]{1,0:T(8,128)(2,1)S(1)} %pad_maximum_fusion), channel_id=1, source_target_pairs={{0,8},{8,16},{16,24},{24,32},{32,40},{40,48},{48,56},{56,64},{64,7... | collective-permute-start | bytes 792584 | tf_op jit(solution)/shard_map/ppermute | solution.py:38
  23.1 8.9 %collective-permute-start.1 = (bf16[8,16512]{1,0:T(8,128)(2,1)S(1)}, bf16[8,16512]{1,0:T(8,128)(2,1)S(1)}, u32[]{:S(2)}, u32[]{:S(2)}) collective-permute-start(bf16[8,16512]{1,0:T(8,128)(2,1)S(1)} %pad_maximum_fusion.1), channel_id=1, source_target_pairs={{0,16},{8,24},{16,32},{24,40},{32,48},{40,56},{48,64},{56,72},{64,... | collective-permute-start | bytes 792584 | tf_op jit(solution)/shard_map/ppermute | solution.py:38
  32.9 9.7 %collective-permute-start.2 = (bf16[8,16512]{1,0:T(8,128)(2,1)S(1)}, bf16[8,16512]{1,0:T(8,128)(2,1)S(1)}, u32[]{:S(2)}, u32[]{:S(2)}) collective-permute-start(bf16[8,16512]{1,0:T(8,128)(2,1)S(1)} %pad_maximum_fusion.2), channel_id=1, source_target_pairs={{0,32},{8,40},{16,48},{24,56},{32,64},{40,72},{48,80},{56,88},{64,... | collective-permute-start | bytes 792584 | tf_op jit(solution)/shard_map/ppermute | solution.py:38
  42.9 9.5 %copy-start.3 = (f32[512,8,128]{2,0,1:T(8,128)S(1)}, f32[512,8,128]{2,0,1:T(8,128)}, u32[]{:S(2)}) copy-start(f32[512,8,128]{2,0,1:T(8,128)} %fusion.16) | copy-start | bytes 6291460
  43.5 8.9 %collective-permute-start.3 = (bf16[8,16512]{1,0:T(8,128)(2,1)S(1)}, bf16[8,16512]{1,0:T(8,128)(2,1)S(1)}, u32[]{:S(2)}, u32[]{:S(2)}) collective-permute-start(bf16[8,16512]{1,0:T(8,128)(2,1)S(1)} %pad_maximum_fusion.3), channel_id=1, source_target_pairs={{0,64},{8,72},{16,80},{24,88},{32,96},{40,104},{48,112},{56,120},{... | collective-permute-start | bytes 792584 | tf_op jit(solution)/shard_map/ppermute | solution.py:38
  56.0 7.8 %copy-start.4 = (s32[64,2]{0,1:T(2,128)S(1)}, s32[64,2]{0,1:T(2,128)}, u32[]{:S(2)}) copy-start(s32[64,2]{0,1:T(2,128)} %param.17) | copy-start | bytes 1540
  56.0 45.5 %copy-start.2 = (bf16[64,3072]{1,0:T(8,128)(2,1)S(1)}, bf16[64,3072]{1,0:T(8,128)(2,1)}, u32[]{:S(2)}) copy-start(bf16[64,3072]{1,0:T(8,128)(2,1)} %param.15) | copy-start | bytes 1179652
  63.8 167.9 %all-gather.2.cloned.1.call-start = ((), (), s32[]{:S(2)}) async-start(), calls=%async_computation.5 | async-start | bytes 16711680 | tf_op jit(solution)/shard_map/all_gather | solution.py:136
  126.4 244.9 %reduce-scatter.5.cloned.1.call-start = ((), (), s32[]{:S(2)}) async-start(), calls=%async_computation.6 | async-start | bytes 16711680 | tf_op jit(solution)/shard_map/reduce_scatter | solution.py:147
  266.2 114.1 %copy-start.5 = (f32[64,2]{0,1:T(2,128)S(1)}, f32[64,2]{0,1:T(2,128)}, u32[]{:S(2)}) copy-start(f32[64,2]{0,1:T(2,128)} %param.18) | copy-start | bytes 1540
  371.3 26.1 %copy-start.1 = (bf16[512,1024]{1,0:T(8,128)(2,1)S(1)}, bf16[512,1024]{1,0:T(8,128)(2,1)}, u32[]{:S(2)}) copy-start(bf16[512,1024]{1,0:T(8,128)(2,1)} %param.11) | copy-start | bytes 3145732
  374.5 20.1 %all-to-all-start.1 = ((bf16[8,10,2,3072]{3,2,1,0:T(2,128)(2,1)}), bf16[8,10,2,3072]{3,2,1,0:T(2,128)(2,1)S(1)}, u32[]{:S(2)}, u32[]{:S(2)}) async-start(bf16[8,10,2,3072]{3,2,1,0:T(2,128)(2,1)} %bitcast.18), calls=%async_computation.3 | async-start | bytes 1966080 | tf_op jit(solution)/shard_map/all_to_all | solution.py:156
Sparse Core Ops, SparseCore 0:
  63.9 37.6 reduce-scatter.2
  126.5 105.1 all-gather.1
  266.4 104.8 reduce-scatter.4

commit v9 on v8

--- a/solution.py
+++ b/solution.py
@@ -91,13 +91,13 @@
     weights = jnp.where(causal, scores * jnp.exp(jnp.where(causal, diff, 0.0)), 0.0).astype(
         jnp.bfloat16
     )
-    intra = jnp.einsum("hts,shd->thd", weights, v_heads, preferred_element_type=jnp.float32)
     last = cum[-1]
     scaled_keys = (k_heads.astype(jnp.float32) * jnp.exp(last[None, :] - cum)[:, :, None]).astype(
         jnp.bfloat16
     )
     summary = jnp.einsum("thd,the->hde", scaled_keys, v_heads, preferred_element_type=jnp.float32)
-    carried, intra = carried_state(last, summary, "ctx", intra)
+    carried, weights = carried_state(last, summary, "ctx", weights)
+    intra = jnp.einsum("hts,shd->thd", weights, v_heads, preferred_element_type=jnp.float32)
     inter = jnp.exp(cum)[:, :, None] * jnp.einsum(
         "thd,hde->the", q_heads.astype(jnp.float32), carried, precision=lax.Precision.HIGHEST
     )

time: 405 us -> 405 us (level)
    unnamed x25 -> x33, local copies, waits for them, and re-layouts: 14.9 us -> 15.6 us
  transfers between devices with their start and end apart: 8 -> 8, of which waited for: 7 -> 7; matrix products, arithmetic and copies ran while one was open for 5% -> 6% of each run, Pallas kernels for 0% -> 0%
where the time goes in v9:
time: 405 us; the launch traced here: 404 us
  waiting for transfers between devices  255 us (63%)
  matrix products  53.7 us (13%)
  starting transfers between devices  28.3 us (7%)
  local copies, waits for them, and re-layouts  25.4 us (6%)
  blocking collectives  20.6 us (5%)
  between operations  13.5 us (3%)
  other arithmetic  7.49 us (2%)
    reduce_scatter x1, waiting for transfers between devices, on_device(): lax.psum_scatter(jnp.einsum('ref,efd->red', acts, w_down, preferred_eleme...  105 us
    all_gather x1, waiting for transfers between devices, on_device(): piece = lax.all_gather(arrived, 'ctx', axis=0, tiled=True)  91.5 us
    reduce_scatter x1, waiting for transfers between devices, on_device(): lax.psum_scatter(jnp.dot(normed, out_proj, preferred_element_type=jnp.flo...  36.1 us
    ppermute x4, starting transfers between devices, carried_state(): in_r, in_s = unpack(lax.ppermute(sent, axis, pairs), hd)  22.2 us
    all_to_all x1, blocking collectives, on_device(): lax.all_to_all(packed, 'exp', split_axis=0, concat_axis=1, tiled=True)  20.6 us
    dot_general x1, matrix products, on_device(): jnp.einsum('red,edf->ref', piece, jnp.concatenate([w_gate, w_up], axis=2)...  19.2 us
    unnamed x33, local copies, waits for them, and re-layouts  15.6 us
    dot_general x1, matrix products, on_device(): jnp.einsum('ref,efd->red', acts, w_down, preferred_element_type=jnp.float32)  15.4 us
  transfers between devices with their start and end apart: 8, of which 7 were waited for; matrix products, arithmetic and copies ran while one was open for 6% of the time, Pallas kernels for 0%

profile of v9, /device:TPU:1, one launch (start us, length us, event | category | flops | bytes accessed | tf_op | source)
XLA Modules:
  0.0 404.2 jit_solution(10496666796344131264)
XLA Ops:
  8.1 2.3 copy.151
  11.9 1.7 fusion.12
  14.0 3.9 collective-permute-start
  18.0 4.0 select_convert_fusion
  23.7 5.7 %collective-permute-start.1 = (bf16[8,16512]{1,0:T(8,128)(2,1)S(1)}, bf16[8,16512]{1,0:T(8,128)(2,1)S(1)}, u32[]{:S(2)}, u32[]{:S(2)}) collective-permute-start(bf16[8,16512]{1,0:T(8,128)(2,1)S(1)} %pad_maximum_fusion.1), channel_id=1, source_target_pairs={{0,16},{8,24},{16,32},{24,40},{32,48},{40,56},{48,64},{56,72},{64,... | collective-permute-start | bytes 792584 | tf_op jit(solution)/shard_map/ppermute | solution.py:38
  29.4 4.1 %collective-permute-done.1 = bf16[8,16512]{1,0:T(8,128)(2,1)S(1)} collective-permute-done((bf16[8,16512]{1,0:T(8,128)(2,1)S(1)}, bf16[8,16512]{1,0:T(8,128)(2,1)S(1)}, u32[]{:S(2)}, u32[]{:S(2)}) %collective-permute-start.1) | collective-permute-done | bytes 264224 | tf_op jit(solution)/shard_map/ppermute | solution.py:38
  35.4 7.2 %collective-permute-start.2 = (bf16[8,16512]{1,0:T(8,128)(2,1)S(1)}, bf16[8,16512]{1,0:T(8,128)(2,1)S(1)}, u32[]{:S(2)}, u32[]{:S(2)}) collective-permute-start(bf16[8,16512]{1,0:T(8,128)(2,1)S(1)} %pad_maximum_fusion.2), channel_id=1, source_target_pairs={{0,32},{8,40},{16,48},{24,56},{32,64},{40,72},{48,80},{56,88},{64,... | collective-permute-start | bytes 792584 | tf_op jit(solution)/shard_map/ppermute | solution.py:38
  42.6 3.3 collective-permute-done.2
  47.7 5.4 %collective-permute-start.3 = (bf16[8,16512]{1,0:T(8,128)(2,1)S(1)}, bf16[8,16512]{1,0:T(8,128)(2,1)S(1)}, u32[]{:S(2)}, u32[]{:S(2)}) collective-permute-start(bf16[8,16512]{1,0:T(8,128)(2,1)S(1)} %pad_maximum_fusion.3), channel_id=1, source_target_pairs={{0,64},{8,72},{16,80},{24,88},{32,96},{40,104},{48,112},{56,120},{... | collective-permute-start | bytes 792584 | tf_op jit(solution)/shard_map/ppermute | solution.py:38
  53.2 3.7 fusion.66
  56.9 1.8 multiply_reduce_fusion
  59.7 4.9 %convolution_convert_fusion.1 = bf16[512,3072]{1,0:T(8,128)(2,1)} fusion(bf16[512,1024]{0,1:T(8,128)(2,1)S(1)} %bitcast.194, bf16[1024,3072]{1,0:T(8,128)(2,1)S(1)} %bitcast.201), kind=kOutput, calls=%fused_computation.8 | convolution fusion | flops 3222798336 | bytes 10485760 | tf_op jit(solution)/shard_map/dot_general | solution.py:112
  65.7 36.1 %reduce-scatter.3.cloned.1.call-done = bf16[64,3072]{1,0:T(8,128)(2,1)} async-done(((bf16[512,3072]{1,0:T(8,128)(2,1)}), bf16[64,3072]{1,0:T(8,128)(2,1)}) %reduce-scatter.3.cloned.1.call-update) | async-done | bytes 393232 | tf_op jit(solution)/shard_map/reduce_scatter | solution.py:111
  105.0 20.6 %all_to_all.14 = bf16[8,10,2,3072]{3,2,1,0:T(2,128)(2,1)S(1)} all-to-all(bf16[8,10,2,3072]{3,2,1,0:T(2,128)(2,1)S(1)} %reshape.351), channel_id=1, replica_groups=mesh['ctx'=16,'exp'=8] {'exp'}, dimensions={0} | all-to-all | bytes 1966080 | tf_op jit(solution)/shard_map/all_to_all | solution.py:133
  126.9 6.7 %copy.138 = bf16[2,3072,384]{1,2,0:T(8,128)(2,1)} copy(bf16[2,3072,384]{2,1,0:T(8,128)(2,1)} %param.19) | data formatting | bytes 9437184 | tf_op args[8]
  133.6 6.9 %copy.139 = bf16[2,3072,384]{1,2,0:T(8,128)(2,1)} copy(bf16[2,3072,384]{2,1,0:T(8,128)(2,1)} %param.20) | data formatting | bytes 9437184 | tf_op args[9]
  140.5 91.5 %all-gather.2.cloned.1.call-done = bf16[1280,2,3072]{2,0,1:T(8,128)(2,1)} async-done(((bf16[80,2,3072]{2,0,1:T(8,128)(2,1)}), bf16[1280,2,3072]{2,0,1:T(8,128)(2,1)}) %all-gather.2.cloned.1.call-update) | async-done | bytes 15728656 | tf_op jit(solution)/shard_map/all_gather | solution.py:136
  231.9 19.2 %fusion.5 = f32[1280,2,768]{0,2,1:T(8,128)} fusion(bf16[1280,2,3072]{2,0,1:T(8,128)(2,1)} %all-gather.2.cloned.1.call-done, bf16[2,3072,384]{1,2,0:T(8,128)(2,1)} %copy.139, bf16[2,3072,384]{1,2,0:T(8,128)(2,1)} %copy.138), kind=kOutput, calls=%fused_computation.7 | convolution fusion | flops 12098469888 | bytes 33030144 | tf_op jit(solution)/shard_map/red,edf->ref/dot_general | solution.py:138
  251.1 15.4 %fusion = bf16[1280,2,3072]{2,0,1:T(8,128)(2,1)} fusion(bf16[2,384,3072]{2,1,0:T(8,128)(2,1)} %param.21, f32[1280,2,768]{0,2,1:T(8,128)} %fusion.5), kind=kOutput, calls=%fused_computation.1 | convolution fusion | flops 6053560320 | bytes 28311552 | tf_op jit(solution)/shard_map/ref,efd->red/dot_general | solution.py:148
  266.5 105.0 %reduce-scatter.5.cloned.1.call-done = bf16[80,2,3072]{2,0,1:T(8,128)(2,1)} async-done(((bf16[1280,2,3072]{2,0,1:T(8,128)(2,1)}), bf16[80,2,3072]{2,0,1:T(8,128)(2,1)}) %reduce-scatter.5.cloned.1.call-update) | async-done | bytes 983056 | tf_op jit(solution)/shard_map/reduce_scatter | solution.py:147
  371.5 3.3 copy.142
  374.8 5.8 %all-to-all-start.1 = ((bf16[8,10,2,3072]{3,2,1,0:T(2,128)(2,1)}), bf16[8,10,2,3072]{3,2,1,0:T(2,128)(2,1)S(1)}, u32[]{:S(2)}, u32[]{:S(2)}) async-start(bf16[8,10,2,3072]{3,2,1,0:T(2,128)(2,1)} %bitcast.18), calls=%async_computation.3 | async-start | bytes 1966080 | tf_op jit(solution)/shard_map/all_to_all | solution.py:156
  380.6 14.3 %all-to-all-done.1 = bf16[8,10,2,3072]{3,2,1,0:T(2,128)(2,1)S(1)} async-done(((bf16[8,10,2,3072]{3,2,1,0:T(2,128)(2,1)}), bf16[8,10,2,3072]{3,2,1,0:T(2,128)(2,1)S(1)}, u32[]{:S(2)}, u32[]{:S(2)}) %all-to-all-start.1) | async-done | bytes 983072 | tf_op jit(solution)/shard_map/all_to_all | solution.py:156
  395.7 2.0 fusion.21
  (92 shorter events, 16.1 us)
Async XLA Ops:
  6.5 11.5 %copy-start = (bf16[512,1024]{1,0:T(8,128)(2,1)S(1)}, bf16[512,1024]{1,0:T(8,128)(2,1)}, u32[]{:S(2)}) copy-start(bf16[512,1024]{1,0:T(8,128)(2,1)} %param.11) | copy-start | bytes 3145732
  6.5 95.3 %reduce-scatter.3.cloned.1.call-start = ((), (), s32[]{:S(2)}) async-start(), calls=%async_computation.4 | async-start | bytes 3538944 | tf_op jit(solution)/shard_map/reduce_scatter | solution.py:111
  11.9 6.1 %copy-start.4 = (bf16[512,1024]{0,1:T(8,128)(2,1)S(1)}, bf16[512,1024]{0,1:T(8,128)(2,1)}, u32[]{:S(2)}) copy-start(bf16[512,1024]{0,1:T(8,128)(2,1)} %copy.151) | copy-start | bytes 3145732
  14.0 9.0 %collective-permute-start = (bf16[8,16512]{1,0:T(8,128)(2,1)S(1)}, bf16[8,16512]{1,0:T(8,128)(2,1)S(1)}, u32[]{:S(2)}, u32[]{:S(2)}) collective-permute-start(bf16[8,16512]{1,0:T(8,128)(2,1)S(1)} %pad_maximum_fusion), channel_id=1, source_target_pairs={{0,8},{8,16},{16,24},{24,32},{32,40},{40,48},{48,56},{56,64},{64,7... | collective-permute-start | bytes 792584 | tf_op jit(solution)/shard_map/ppermute | solution.py:38
  23.7 9.8 %collective-permute-start.1 = (bf16[8,16512]{1,0:T(8,128)(2,1)S(1)}, bf16[8,16512]{1,0:T(8,128)(2,1)S(1)}, u32[]{:S(2)}, u32[]{:S(2)}) collective-permute-start(bf16[8,16512]{1,0:T(8,128)(2,1)S(1)} %pad_maximum_fusion.1), channel_id=1, source_target_pairs={{0,16},{8,24},{16,32},{24,40},{32,48},{40,56},{48,64},{56,72},{64,... | collective-permute-start | bytes 792584 | tf_op jit(solution)/shard_map/ppermute | solution.py:38
  33.9 1.2 copy-start.2
  35.4 10.5 %collective-permute-start.2 = (bf16[8,16512]{1,0:T(8,128)(2,1)S(1)}, bf16[8,16512]{1,0:T(8,128)(2,1)S(1)}, u32[]{:S(2)}, u32[]{:S(2)}) collective-permute-start(bf16[8,16512]{1,0:T(8,128)(2,1)S(1)} %pad_maximum_fusion.2), channel_id=1, source_target_pairs={{0,32},{8,40},{16,48},{24,56},{32,64},{40,72},{48,80},{56,88},{64,... | collective-permute-start | bytes 792584 | tf_op jit(solution)/shard_map/ppermute | solution.py:38
  47.4 9.5 %copy-start.3 = (f32[1,8,128,128]{3,1,2,0:T(8,128)S(1)}, f32[1,8,128,128]{3,1,2,0:T(8,128)}, u32[]{:S(2)}) copy-start(f32[1,8,128,128]{3,1,2,0:T(8,128)} %copy-done.2) | copy-start | bytes 1572868
  47.7 9.1 %collective-permute-start.3 = (bf16[8,16512]{1,0:T(8,128)(2,1)S(1)}, bf16[8,16512]{1,0:T(8,128)(2,1)S(1)}, u32[]{:S(2)}, u32[]{:S(2)}) collective-permute-start(bf16[8,16512]{1,0:T(8,128)(2,1)S(1)} %pad_maximum_fusion.3), channel_id=1, source_target_pairs={{0,64},{8,72},{16,80},{24,88},{32,96},{40,104},{48,112},{56,120},{... | collective-permute-start | bytes 792584 | tf_op jit(solution)/shard_map/ppermute | solution.py:38
  56.8 2.2 slice-start
  56.9 2.8 slice-start.1
  59.7 5.0 %copy-start.6 = (s32[64,2]{0,1:T(2,128)S(1)}, s32[64,2]{0,1:T(2,128)}, u32[]{:S(2)}) copy-start(s32[64,2]{0,1:T(2,128)} %param.17) | copy-start | bytes 1540
  59.7 42.2 %copy-start.5 = (bf16[64,3072]{1,0:T(8,128)(2,1)S(1)}, bf16[64,3072]{1,0:T(8,128)(2,1)}, u32[]{:S(2)}) copy-start(bf16[64,3072]{1,0:T(8,128)(2,1)} %param.15) | copy-start | bytes 1179652
  64.6 167.3 %all-gather.2.cloned.1.call-start = ((), (), s32[]{:S(2)}) async-start(), calls=%async_computation.5 | async-start | bytes 16711680 | tf_op jit(solution)/shard_map/all_gather | solution.py:136
  126.7 244.8 %reduce-scatter.5.cloned.1.call-start = ((), (), s32[]{:S(2)}) async-start(), calls=%async_computation.6 | async-start | bytes 16711680 | tf_op jit(solution)/shard_map/reduce_scatter | solution.py:147
  266.5 114.1 %copy-start.7 = (f32[64,2]{0,1:T(2,128)S(1)}, f32[64,2]{0,1:T(2,128)}, u32[]{:S(2)}) copy-start(f32[64,2]{0,1:T(2,128)} %param.18) | copy-start | bytes 1540
  371.5 26.1 %copy-start.1 = (bf16[512,1024]{1,0:T(8,128)(2,1)S(1)}, bf16[512,1024]{1,0:T(8,128)(2,1)}, u32[]{:S(2)}) copy-start(bf16[512,1024]{1,0:T(8,128)(2,1)} %param.11) | copy-start | bytes 3145732
  374.8 20.1 %all-to-all-start.1 = ((bf16[8,10,2,3072]{3,2,1,0:T(2,128)(2,1)}), bf16[8,10,2,3072]{3,2,1,0:T(2,128)(2,1)S(1)}, u32[]{:S(2)}, u32[]{:S(2)}) async-start(bf16[8,10,2,3072]{3,2,1,0:T(2,128)(2,1)} %bitcast.18), calls=%async_computation.3 | async-start | bytes 1966080 | tf_op jit(solution)/shard_map/all_to_all | solution.py:156
Sparse Core Ops, SparseCore 0:
  64.8 37.0 reduce-scatter.2
  126.8 105.0 all-gather.1
  266.6 104.8 reduce-scatter.4

commit v10 on v6

--- a/solution.py
+++ b/solution.py
@@ -10,17 +10,15 @@
     heads, hd, _ = state.shape
     hi = rate.astype(jnp.bfloat16)
     lo = (rate - hi.astype(jnp.float32)).astype(jnp.bfloat16)
-    lane = jnp.arange(hd, dtype=jnp.int32)[None, :]
-    rate_row = jnp.where(lane == 0, hi[:, None], jnp.where(lane == 1, lo[:, None], 0.0)).astype(
-        jnp.bfloat16
-    )
-    return jnp.concatenate([state.astype(jnp.bfloat16).reshape(heads, hd * hd), rate_row], axis=1)
+    row = jnp.arange(16, dtype=jnp.int32)[None, :, None]
+    rate_rows = jnp.where(row == 0, hi[:, None, None], jnp.where(row == 1, lo[:, None, None], 0.0))
+    rate_rows = jnp.broadcast_to(rate_rows, (heads, 16, hd)).astype(jnp.bfloat16)
+    return jnp.concatenate([state.astype(jnp.bfloat16), rate_rows], axis=1)
 
 
 def unpack(payload, hd):
-    heads = payload.shape[0]
-    state = payload[:, : hd * hd].astype(jnp.float32).reshape(heads, hd, hd)
-    rate = payload[:, hd * hd].astype(jnp.float32) + payload[:, hd * hd + 1].astype(jnp.float32)
+    state = payload[:, :hd, :].astype(jnp.float32)
+    rate = payload[:, hd, 0].astype(jnp.float32) + payload[:, hd + 1, 0].astype(jnp.float32)
     return rate, state
 
 

time: 402 us -> 407 us (1.012)
    unnamed x29 -> x15, local copies, waits for them, and re-layouts: 14.9 us -> 14.1 us
where the time goes in v10:
time: 407 us; the launch traced here: 406 us
  waiting for transfers between devices  258 us (63%)
  matrix products  56.5 us (14%)
  starting transfers between devices  29.3 us (7%)
  local copies, waits for them, and re-layouts  21.7 us (5%)
  blocking collectives  20.6 us (5%)
  between operations  13.4 us (3%)
  other arithmetic  6.73 us (2%)
    reduce_scatter x1, waiting for transfers between devices, on_device(): lax.psum_scatter(jnp.einsum('ref,efd->red', acts, w_down, preferred_eleme...  105 us
    all_gather x1, waiting for transfers between devices, on_device(): piece = lax.all_gather(arrived, 'ctx', axis=0, tiled=True)  91.5 us
    reduce_scatter x1, waiting for transfers between devices, on_device(): lax.psum_scatter(jnp.dot(normed, out_proj, preferred_element_type=jnp.flo...  32.9 us
    ppermute x4, starting transfers between devices, carried_state(): in_r, in_s = unpack(lax.ppermute(pack(incl_r, incl_s), axis, pairs), hd)  23.3 us
    all_to_all x1, blocking collectives, on_device(): lax.all_to_all(packed, 'exp', split_axis=0, concat_axis=1, tiled=True)  20.6 us
    dot_general x1, matrix products, on_device(): jnp.einsum('red,edf->ref', piece, jnp.concatenate([w_gate, w_up], axis=2)...  19.2 us
    dot_general x1, matrix products, on_device(): jnp.einsum('ref,efd->red', acts, w_down, preferred_element_type=jnp.float32)  15.4 us
    ppermute x4, waiting for transfers between devices, carried_state(): in_r, in_s = unpack(lax.ppermute(pack(incl_r, incl_s), axis, pairs), hd)  14.3 us
  transfers between devices with their start and end apart: 8, of which 7 were waited for; matrix products, arithmetic and copies ran while one was open for 5% of the time, Pallas kernels for 0%

profile of v10, /device:TPU:1, one launch (start us, length us, event | category | flops | bytes accessed | tf_op | source)
XLA Modules:
  0.0 406.1 jit_solution(733703884428525647)
XLA Ops:
  8.5 1.5 copy.92
  10.0 1.7 fusion.70
  11.9 3.9 collective-permute-start
  15.9 5.7 %collective-permute-done = bf16[8,144,128]{2,1,0:T(8,128)(2,1)S(1)} collective-permute-done((bf16[8,144,128]{2,1,0:T(8,128)(2,1)S(1)}, bf16[8,144,128]{2,1,0:T(8,128)(2,1)S(1)}, u32[]{:S(2)}, u32[]{:S(2)}) %collective-permute-start) | collective-permute-done | bytes 294944 | tf_op jit(solution)/shard_map/ppermute | solution.py:33
  22.2 5.6 %collective-permute-start.1 = (bf16[8,144,128]{2,1,0:T(8,128)(2,1)S(1)}, bf16[8,144,128]{2,1,0:T(8,128)(2,1)S(1)}, u32[]{:S(2)}, u32[]{:S(2)}) collective-permute-start(bf16[8,144,128]{2,1,0:T(8,128)(2,1)S(1)} %pad_maximum_fusion.1), channel_id=1, source_target_pairs={{0,16},{8,24},{16,32},{24,40},{32,48},{40,56},{48,64},{56,72},{64,... | collective-permute-start | bytes 884744 | tf_op jit(solution)/shard_map/ppermute | solution.py:33
  27.8 4.8 %collective-permute-done.1 = bf16[8,144,128]{2,1,0:T(8,128)(2,1)S(1)} collective-permute-done((bf16[8,144,128]{2,1,0:T(8,128)(2,1)S(1)}, bf16[8,144,128]{2,1,0:T(8,128)(2,1)S(1)}, u32[]{:S(2)}, u32[]{:S(2)}) %collective-permute-start.1) | collective-permute-done | bytes 294944 | tf_op jit(solution)/shard_map/ppermute | solution.py:33
  33.3 7.2 %collective-permute-start.2 = (bf16[8,144,128]{2,1,0:T(8,128)(2,1)S(1)}, bf16[8,144,128]{2,1,0:T(8,128)(2,1)S(1)}, u32[]{:S(2)}, u32[]{:S(2)}) collective-permute-start(bf16[8,144,128]{2,1,0:T(8,128)(2,1)S(1)} %pad_maximum_fusion.2), channel_id=1, source_target_pairs={{0,32},{8,40},{16,48},{24,56},{32,64},{40,72},{48,80},{56,88},{64,... | collective-permute-start | bytes 884744 | tf_op jit(solution)/shard_map/ppermute | solution.py:33
  40.6 3.9 collective-permute-done.2
  45.8 6.5 %collective-permute-start.3 = (bf16[8,144,128]{2,1,0:T(8,128)(2,1)S(1)}, bf16[8,144,128]{2,1,0:T(8,128)(2,1)}, u32[]{:S(2)}, u32[]{:S(2)}) collective-permute-start(bf16[8,144,128]{2,1,0:T(8,128)(2,1)S(1)} %pad_maximum_fusion.3), channel_id=1, source_target_pairs={{0,64},{8,72},{16,80},{24,88},{32,96},{40,104},{48,112},{56,120},{... | collective-permute-start | bytes 884744 | tf_op jit(solution)/shard_map/ppermute | solution.py:33
  52.3 6.2 %fusion.8 = f32[8,512,128]{1,2,0:T(8,128)} fusion(f32[8,512]{1,0:T(8,128)} %bitcast.81, pred[512,512]{1,0:T(8,128)(4,1)S(1)} %iota_compare_fusion, bf16[512,8,128]{0,2,1:T(8,128)(2,1)S(1)} %bitcast.80, bf16[512,1024]{1,0:T(8,128)(2,1)} %param.13, bf16[512,1024]{1,0:T(8,128)(2,1)S(1)} %copy-done), kind=kOutput, calls=%fused_computation.9 | convolution fusion | flops 1084227584 | bytes 5521408 | tf_op jit(solution)/shard_map/hts,shd->thd/dot_general | solution.py:89
  58.5 3.2 multiply_reduce_fusion
  62.1 7.7 %convolution_convert_fusion.1 = bf16[512,3072]{1,0:T(8,128)(2,1)} fusion(bf16[512,1024]{0,1:T(8,128)(2,1)S(1)} %bitcast.78, bf16[1024,3072]{1,0:T(8,128)(2,1)} %param.16), kind=kOutput, calls=%fused_computation.8 | convolution fusion | flops 3222798336 | bytes 10485760 | tf_op jit(solution)/shard_map/dot_general | solution.py:107
  70.9 32.9 %reduce-scatter.3.cloned.1.call-done = bf16[64,3072]{1,0:T(8,128)(2,1)} async-done(((bf16[512,3072]{1,0:T(8,128)(2,1)}), bf16[64,3072]{1,0:T(8,128)(2,1)}) %reduce-scatter.3.cloned.1.call-update) | async-done | bytes 393232 | tf_op jit(solution)/shard_map/reduce_scatter | solution.py:106
  106.9 20.6 %all_to_all.14 = bf16[8,10,2,3072]{3,2,1,0:T(2,128)(2,1)S(1)} all-to-all(bf16[8,10,2,3072]{3,2,1,0:T(2,128)(2,1)S(1)} %reshape.473), channel_id=1, replica_groups=mesh['ctx'=16,'exp'=8] {'exp'}, dimensions={0} | all-to-all | bytes 1966080 | tf_op jit(solution)/shard_map/all_to_all | solution.py:128
  128.9 6.7 %copy.85 = bf16[2,3072,384]{1,2,0:T(8,128)(2,1)} copy(bf16[2,3072,384]{2,1,0:T(8,128)(2,1)} %param.19) | data formatting | bytes 9437184 | tf_op args[8]
  135.6 6.9 %copy.86 = bf16[2,3072,384]{1,2,0:T(8,128)(2,1)} copy(bf16[2,3072,384]{2,1,0:T(8,128)(2,1)} %param.20) | data formatting | bytes 9437184 | tf_op args[9]
  142.5 91.5 %all-gather.2.cloned.1.call-done = bf16[1280,2,3072]{2,0,1:T(8,128)(2,1)} async-done(((bf16[80,2,3072]{2,0,1:T(8,128)(2,1)}), bf16[1280,2,3072]{2,0,1:T(8,128)(2,1)}) %all-gather.2.cloned.1.call-update) | async-done | bytes 15728656 | tf_op jit(solution)/shard_map/all_gather | solution.py:131
  233.9 19.2 %fusion.5 = f32[1280,2,768]{0,2,1:T(8,128)} fusion(bf16[1280,2,3072]{2,0,1:T(8,128)(2,1)} %all-gather.2.cloned.1.call-done, bf16[2,3072,384]{1,2,0:T(8,128)(2,1)} %copy.86, bf16[2,3072,384]{1,2,0:T(8,128)(2,1)} %copy.85), kind=kOutput, calls=%fused_computation.7 | convolution fusion | flops 12098469888 | bytes 33030144 | tf_op jit(solution)/shard_map/red,edf->ref/dot_general | solution.py:133
  253.1 15.4 %fusion = bf16[1280,2,3072]{2,0,1:T(8,128)(2,1)} fusion(bf16[2,384,3072]{2,1,0:T(8,128)(2,1)} %param.21, f32[1280,2,768]{0,2,1:T(8,128)} %fusion.5), kind=kOutput, calls=%fused_computation.1 | convolution fusion | flops 6053560320 | bytes 28311552 | tf_op jit(solution)/shard_map/ref,efd->red/dot_general | solution.py:143
  268.5 105.0 %reduce-scatter.5.cloned.1.call-done = bf16[80,2,3072]{2,0,1:T(8,128)(2,1)} async-done(((bf16[1280,2,3072]{2,0,1:T(8,128)(2,1)}), bf16[80,2,3072]{2,0,1:T(8,128)(2,1)}) %reduce-scatter.5.cloned.1.call-update) | async-done | bytes 983056 | tf_op jit(solution)/shard_map/reduce_scatter | solution.py:142
  373.5 3.3 copy.89
  376.8 5.8 %all-to-all-start.1 = ((bf16[8,10,2,3072]{3,2,1,0:T(2,128)(2,1)}), bf16[8,10,2,3072]{3,2,1,0:T(2,128)(2,1)S(1)}, u32[]{:S(2)}, u32[]{:S(2)}) async-start(bf16[8,10,2,3072]{3,2,1,0:T(2,128)(2,1)} %bitcast.10), calls=%async_computation.3 | async-start | bytes 1966080 | tf_op jit(solution)/shard_map/all_to_all | solution.py:151
  382.6 14.3 %all-to-all-done.1 = bf16[8,10,2,3072]{3,2,1,0:T(2,128)(2,1)S(1)} async-done(((bf16[8,10,2,3072]{3,2,1,0:T(2,128)(2,1)}), bf16[8,10,2,3072]{3,2,1,0:T(2,128)(2,1)S(1)}, u32[]{:S(2)}, u32[]{:S(2)}) %all-to-all-start.1) | async-done | bytes 983072 | tf_op jit(solution)/shard_map/all_to_all | solution.py:151
  397.6 2.0 fusion.31
  (66 shorter events, 11.5 us)
Async XLA Ops:
  6.5 45.7 %copy-start = (bf16[512,1024]{1,0:T(8,128)(2,1)S(1)}, bf16[512,1024]{1,0:T(8,128)(2,1)}, u32[]{:S(2)}) copy-start(bf16[512,1024]{1,0:T(8,128)(2,1)} %param.11) | copy-start | bytes 3145732
  6.5 97.2 %reduce-scatter.3.cloned.1.call-start = ((), (), s32[]{:S(2)}) async-start(), calls=%async_computation.4 | async-start | bytes 3538944 | tf_op jit(solution)/shard_map/reduce_scatter | solution.py:106
  7.7 0.7 copy-start.3
  11.9 9.6 %collective-permute-start = (bf16[8,144,128]{2,1,0:T(8,128)(2,1)S(1)}, bf16[8,144,128]{2,1,0:T(8,128)(2,1)S(1)}, u32[]{:S(2)}, u32[]{:S(2)}) collective-permute-start(bf16[8,144,128]{2,1,0:T(8,128)(2,1)S(1)} %pad_maximum_fusion), channel_id=1, source_target_pairs={{0,8},{8,16},{16,24},{24,32},{32,40},{40,48},{48,56},{56,64},{64,7... | collective-permute-start | bytes 884744 | tf_op jit(solution)/shard_map/ppermute | solution.py:33
  22.2 10.5 %collective-permute-start.1 = (bf16[8,144,128]{2,1,0:T(8,128)(2,1)S(1)}, bf16[8,144,128]{2,1,0:T(8,128)(2,1)S(1)}, u32[]{:S(2)}, u32[]{:S(2)}) collective-permute-start(bf16[8,144,128]{2,1,0:T(8,128)(2,1)S(1)} %pad_maximum_fusion.1), channel_id=1, source_target_pairs={{0,16},{8,24},{16,32},{24,40},{32,48},{40,56},{48,64},{56,72},{64,... | collective-permute-start | bytes 884744 | tf_op jit(solution)/shard_map/ppermute | solution.py:33
  33.3 11.1 %collective-permute-start.2 = (bf16[8,144,128]{2,1,0:T(8,128)(2,1)S(1)}, bf16[8,144,128]{2,1,0:T(8,128)(2,1)S(1)}, u32[]{:S(2)}, u32[]{:S(2)}) collective-permute-start(bf16[8,144,128]{2,1,0:T(8,128)(2,1)S(1)} %pad_maximum_fusion.2), channel_id=1, source_target_pairs={{0,32},{8,40},{16,48},{24,56},{32,64},{40,72},{48,80},{56,88},{64,... | collective-permute-start | bytes 884744 | tf_op jit(solution)/shard_map/ppermute | solution.py:33
  45.8 12.7 %collective-permute-start.3 = (bf16[8,144,128]{2,1,0:T(8,128)(2,1)S(1)}, bf16[8,144,128]{2,1,0:T(8,128)(2,1)}, u32[]{:S(2)}, u32[]{:S(2)}) collective-permute-start(bf16[8,144,128]{2,1,0:T(8,128)(2,1)S(1)} %pad_maximum_fusion.3), channel_id=1, source_target_pairs={{0,64},{8,72},{16,80},{24,88},{32,96},{40,104},{48,112},{56,120},{... | collective-permute-start | bytes 884744 | tf_op jit(solution)/shard_map/ppermute | solution.py:33
  62.0 7.8 %copy-start.4 = (s32[64,2]{0,1:T(2,128)S(1)}, s32[64,2]{0,1:T(2,128)}, u32[]{:S(2)}) copy-start(s32[64,2]{0,1:T(2,128)} %param.17) | copy-start | bytes 1540
  62.1 41.7 %copy-start.2 = (bf16[64,3072]{1,0:T(8,128)(2,1)S(1)}, bf16[64,3072]{1,0:T(8,128)(2,1)}, u32[]{:S(2)}) copy-start(bf16[64,3072]{1,0:T(8,128)(2,1)} %param.15) | copy-start | bytes 1179652
  69.8 164.2 %all-gather.2.cloned.1.call-start = ((), (), s32[]{:S(2)}) async-start(), calls=%async_computation.5 | async-start | bytes 16711680 | tf_op jit(solution)/shard_map/all_gather | solution.py:131
  128.7 244.9 %reduce-scatter.5.cloned.1.call-start = ((), (), s32[]{:S(2)}) async-start(), calls=%async_computation.6 | async-start | bytes 16711680 | tf_op jit(solution)/shard_map/reduce_scatter | solution.py:142
  268.5 114.1 %copy-start.5 = (f32[64,2]{0,1:T(2,128)S(1)}, f32[64,2]{0,1:T(2,128)}, u32[]{:S(2)}) copy-start(f32[64,2]{0,1:T(2,128)} %param.18) | copy-start | bytes 1540
  373.5 26.1 %copy-start.1 = (bf16[512,1024]{1,0:T(8,128)(2,1)S(1)}, bf16[512,1024]{1,0:T(8,128)(2,1)}, u32[]{:S(2)}) copy-start(bf16[512,1024]{1,0:T(8,128)(2,1)} %param.11) | copy-start | bytes 3145732
  376.8 20.1 %all-to-all-start.1 = ((bf16[8,10,2,3072]{3,2,1,0:T(2,128)(2,1)}), bf16[8,10,2,3072]{3,2,1,0:T(2,128)(2,1)S(1)}, u32[]{:S(2)}, u32[]{:S(2)}) async-start(bf16[8,10,2,3072]{3,2,1,0:T(2,128)(2,1)} %bitcast.10), calls=%async_computation.3 | async-start | bytes 1966080 | tf_op jit(solution)/shard_map/all_to_all | solution.py:151
Sparse Core Ops, SparseCore 0:
  69.9 33.8 reduce-scatter.2
  128.8 105.0 all-gather.1
  268.7 104.8 reduce-scatter.4
